TPU v7x, 256 devices: a whole 4x4x8 slice. The times are simulated.
256 devices in a mesh: seg: 32 (over x, z_hi, core), band: 8 (over y, z_lo).
Axes of the slice: x: 4, y: 4, z: 8 (z_hi: 4, z_lo: 2; z = z_hi * 2 + z_lo), core: 2. Of those that a mesh axis runs over, the one named last changes fastest.
Arguments:
- spectra: bfloat16 [2, 32768, 1024], P(None, 'seg', 'band'), may hold values from -100 to 100, as said below
- pair_first: int32 [131072], P('seg'), may hold values from 0 to 32767, as said below
- pair_second: int32 [131072], P('seg'), may hold values from 0 to 32767, as said below
- pair_bin: int32 [131072], P('seg'), may hold values from 0 to 255, as said below
Outputs:
- correlation_stack: float32 [256, 1024], P('seg', 'band')
Inputs may be any that keep to these rules, and one draw needn't show every extreme that they name: The spectra are finite; their magnitude varies from channel to channel and from bin to bin. `pair_first`: rows s * 4096 to (s + 1) * 4096 - 1 name channels of segment s, that is s * 1024 to (s + 1) * 1024 - 1. pair_second differs from pair_first of the same row by 1 to 256 in either direction; some row of every segment differs by exactly 256. `pair_bin`: offset bins s * 8 to (s + 1) * 8 - 1 belong to segment s; of one segment's rows at most 256 have bins of any one segment, and in every draw the bins of some segment receive exactly 256 rows from every segment.
All inputs are finite; a program needn't handle non-finite values.
Results may differ from a plain program's by a relative error of at most 0.0054.
Values may be sent and summed in bfloat16 or wider, within the bound.
No kernel may reach another device: no remote copies, remote signals or barrier semaphores. Data moves between devices by JAX's collectives and lax.ppermute only.
A program may use at most 64 MiB of HBM per device.

v0:
```python
import math

import jax
import jax.numpy as jnp
from jax import lax
from jax.sharding import PartitionSpec as P

OB_DEV = 8
REACH = 256
FREQ = 1024
LAGS = 1024
HALF_WIN = 64
CAP = 256


epsilon = 1e-06


def extended(block, sides, width):
    for axis, dim in sides:
        count = lax.axis_size(axis)
        forward = [(i, i + 1) for i in range(count - 1)]
        backward = [(target, source) for source, target in forward]
        low = lax.ppermute(
            lax.slice_in_dim(block, block.shape[dim] - width, None, axis=dim), axis, forward
        )
        high = lax.ppermute(lax.slice_in_dim(block, 0, width, axis=dim), axis, backward)
        block = jnp.concatenate([low, block, high], axis=dim)
    return block


def window_matrix(local_bins, half_width):
    padded_index = jnp.arange(local_bins + 2 * half_width)[:, None]
    bin_index = jnp.arange(local_bins)[None, :]
    inside = (padded_index >= bin_index) & (padded_index <= bin_index + 2 * half_width)
    return inside.astype(jnp.float32)


def lag_table(first_bin, local_bins, total_bins, lag_count):
    frequency = first_bin + jnp.arange(local_bins, dtype=jnp.int32)
    lag_index = jnp.arange(lag_count, dtype=jnp.int32) - lag_count // 2
    residue = frequency[:, None] * lag_index[None, :] % (2 * total_bins)
    angles = residue.astype(jnp.float32) * (math.pi / total_bins)
    cosine = jnp.cos(angles) / total_bins
    negsine = -jnp.sin(angles) / total_bins
    return jnp.concatenate([cosine, negsine], axis=0).astype(jnp.bfloat16)


def per_device(spectra, pair_first, pair_second, pair_bin):
    seg_position = lax.axis_index("seg")
    band_position = lax.axis_index("band")
    segments = lax.axis_size("seg")
    channels = spectra.shape[1]
    local_bins = spectra.shape[2]
    real_part = spectra[0].astype(jnp.float32)
    imag_part = spectra[1].astype(jnp.float32)
    power_sum = real_part * real_part + imag_part * imag_part
    padded_power = extended(power_sum, (("band", 1),), HALF_WIN)
    window_sum = jnp.dot(
        padded_power, window_matrix(local_bins, HALF_WIN), precision=lax.Precision.HIGHEST
    )
    scaling = lax.rsqrt(window_sum / (2 * HALF_WIN + 1) + epsilon)
    whitened = jnp.concatenate([real_part * scaling, imag_part * scaling], axis=1).astype(
        jnp.bfloat16
    )
    first_rows = whitened[pair_first - seg_position * channels]
    near_rows = extended(whitened, (("seg", 0),), REACH)
    second_rows = near_rows[pair_second - seg_position * channels + REACH]
    first_real = first_rows[:, :local_bins].astype(jnp.float32)
    first_imag = first_rows[:, local_bins:].astype(jnp.float32)
    second_real = second_rows[:, :local_bins].astype(jnp.float32)
    second_imag = second_rows[:, local_bins:].astype(jnp.float32)
    cross_real = first_real * second_real + first_imag * second_imag
    cross_imag = first_imag * second_real - first_real * second_imag
    cross_both = jnp.concatenate([cross_real, cross_imag], axis=1).astype(jnp.bfloat16)
    table = lag_table(band_position * local_bins, local_bins, FREQ, LAGS)
    owner_seg = pair_bin // OB_DEV
    owner_hits = (owner_seg[:, None] == jnp.arange(segments, dtype=jnp.int32)[None, :]).astype(
        jnp.int32
    )
    earlier_hits = jnp.cumsum(owner_hits, axis=0) - owner_hits
    slot_rank = jnp.sum(earlier_hits * owner_hits, axis=1)
    slot_index = owner_seg * CAP + slot_rank
    send_rows = (
        jnp.zeros((segments * CAP, 2 * local_bins), jnp.bfloat16).at[slot_index].set(cross_both)
    )
    send_tags = jnp.zeros((segments * CAP,), jnp.int32).at[slot_index].set(pair_bin % OB_DEV + 1)
    recv_rows, recv_tags = (
        lax.all_to_all(
            send_rows.reshape(segments, CAP, 2 * local_bins),
            "seg",
            split_axis=0,
            concat_axis=0,
            tiled=True,
        ),
        lax.all_to_all(
            send_tags.reshape(segments, CAP), "seg", split_axis=0, concat_axis=0, tiled=True
        ),
    )
    group_size = math.gcd(segments, max(1, 512 // CAP))
    block_rows = recv_rows.reshape(segments // group_size, group_size * CAP, 2 * local_bins)
    block_tags = recv_tags.reshape(segments // group_size, group_size * CAP)
    bin_labels = jnp.arange(1, OB_DEV + 1, dtype=jnp.int32)

    def stack_block(running, block_data):
        slot_rows, slot_tags = block_data
        slot_lags = jnp.dot(slot_rows, table, preferred_element_type=jnp.float32)
        member_table = (slot_tags[:, None] == bin_labels[None, :]).astype(jnp.float32)
        added = lax.dot_general(
            member_table, slot_lags, (((0,), (0,)), ((), ())), precision=lax.Precision.HIGHEST
        )
        return (running + added, None)

    partial_lags, _ = lax.scan(
        stack_block, jnp.zeros((OB_DEV, LAGS), jnp.float32), (block_rows, block_tags)
    )
    return lax.psum_scatter(partial_lags, "band", scatter_dimension=1, tiled=True)


def solution(mesh):
    placed = (P(None, "seg", "band"), P("seg"), P("seg"), P("seg"))
    return jax.shard_map(
        per_device, mesh=mesh, in_specs=placed, out_specs=P("seg", "band"), check_vma=False
    )
```

profile of v0, /device:TPU:1, one launch (start us, length us, event | category | flops | bytes accessed | tf_op | source)
XLA Modules:
  0.0 305.7 jit_solution(16693032658908340649)
XLA Ops:
  6.5 1.1 fusion.49
  7.6 0.1 copy.17
  7.8 0.1 copy.18
  7.9 0.1 fusion.25
  8.1 4.4 %collective-permute-start = (f32[1024,64]{0,1:T(8,128)S(1)}, f32[1024,64]{0,1:T(8,128)S(1)}, u32[]{:S(2)}, u32[]{:S(2)}) collective-permute-start(f32[1024,64]{0,1:T(8,128)S(1)} %get-tuple-element.74), channel_id=1, source_target_pairs={{0,1},{1,2},{2,3},{3,4},{4,5},{5,6},{6,7},{8,9},{9,10},{10,11},{11... | collective-permute-start | bytes 786440 | tf_op jit(solution)/shard_map/ppermute | solution.py:24
  12.4 1.3 collective-permute-start.1
  13.8 0.1 fusion.34
  13.8 9.2 %reduce-window.6 = s32[32,32,128]{2,1,0:T(8,128)S(1)} reduce-window(s32[32,32,128]{2,1,0:T(8,128)S(1)} %fusion.34, s32[]{:T(128)} %constant.77.clone.1), window={size=1x1x128 pad=0_0x0_0x127_0}, to_apply=%region_0.1 | reduce-window | flops 16646144 | bytes 1048580 | tf_op jit(solution)/shard_map/reduce-window
  23.1 0.8 slice_reduce_fusion
  23.9 0.2 reduce-window.9
  24.1 0.2 broadcast_add_fusion
  24.3 0.4 fusion.33
  24.7 16.1 %scatter_custom_fusion = s32[8192]{0:T(1024)} fusion(s32[4096]{0:T(1024)S(1)} %compare_select_fusion.2, s32[4096]{0:T(1024)S(1)} %get-tuple-element.78, s32[]{:T(128)} %constant.77.clone.1), kind=kCustom, calls=%fused_computation.87 | custom fusion | bytes 32772 | tf_op jit(solution)/shard_map/scatter | solution.py:87
  40.8 11.1 %all-to-all-start = ((s32[32,1,256]{2,1,0:T(1,128)}), s32[32,1,256]{2,1,0:T(1,128)S(1)}, u32[]{:S(2)}, u32[]{:S(2)}) async-start(s32[32,1,256]{2,1,0:T(1,128)} %bitcast.2), calls=%async_computation | async-start | bytes 65536 | tf_op jit(solution)/shard_map/all_to_all | solution.py:96
  52.0 1.6 fusion.27
  53.5 0.7 fusion.35
  54.2 4.4 %collective-permute-start.2 = (bf16[256,256]{0,1:T(8,128)(2,1)}, bf16[256,256]{0,1:T(8,128)(2,1)S(1)}, u32[]{:S(2)}, u32[]{:S(2)}) collective-permute-start(bf16[256,256]{0,1:T(8,128)(2,1)} %get-tuple-element.70), channel_id=1, source_target_pairs={{0,8},{8,16},{16,24},{24,32},{32,40},{40,48},{48,56},{56,64},{64,7... | collective-permute-start | bytes 393224 | tf_op jit(solution)/shard_map/ppermute | solution.py:24
  58.7 1.9 collective-permute-start.3
  60.7 0.2 copy.15
  60.9 14.6 %gather_fusion = bf16[4096,256]{1,0:T(8,128)(2,1)S(1)} fusion(bf16[1024,256]{1,0:T(8,128)(2,1)S(1)} %copy.15, s32[4096]{0:T(1024)S(1)} %get-tuple-element.82), kind=kCustom, calls=%fused_computation | custom fusion | bytes 4210688 | tf_op jit(solution)/shard_map/gather | solution.py:66
  75.6 0.9 pad_maximum_fusion
  76.5 1.4 copy.16
  77.9 17.0 %gather_fusion.1 = bf16[4096,256]{1,0:T(8,128)(2,1)} fusion(bf16[1536,256]{1,0:T(8,128)(2,1)S(1)} %copy.16, s32[4096]{0:T(1024)S(1)} %get-tuple-element.83), kind=kCustom, calls=%fused_computation.1 | custom fusion | bytes 4210688 | tf_op jit(solution)/shard_map/gather | solution.py:68
  94.9 3.4 %fusion.10 = (bf16[4096,128]{1,0:T(8,128)(2,1)S(1)}, bf16[4096,128]{1,0:T(8,128)(2,1)}) fusion(bf16[4096,256]{1,0:T(8,128)(2,1)} %gather_fusion.1, bf16[4096,256]{1,0:T(8,128)(2,1)S(1)} %gather_fusion), kind=kLoop, calls=%fused_computation.20 | loop fusion | flops 6291456 | bytes 6291456 | tf_op jit(solution)/shard_map/convert.4
  98.3 20.8 %scatter_custom_fusion.1 = bf16[8192,256]{1,0:T(8,128)(2,1)} fusion(s32[4096]{0:T(1024)S(1)} %compare_select_fusion.2, bf16[4096,128]{1,0:T(8,128)(2,1)} %get-tuple-element.69, bf16[]{:T(256)} %constant.102, bf16[4096,128]{1,0:T(8,128)(2,1)S(1)} %get-tuple-element.68, bf16[]{:T(256)} %constant.79.clone.1), kind=kCustom, calls=%fused_computation.23 | custom fusion | flops 4194304 | bytes 6291460 | tf_op jit(solution)/shard_map/scatter | solution.py:85
  119.1 11.2 %all-to-all-start.1 = ((bf16[32,256,256]{2,1,0:T(8,128)(2,1)}), bf16[32,256,256]{2,1,0:T(8,128)(2,1)}, u32[]{:S(2)}, u32[]{:S(2)}) async-start(bf16[32,256,256]{2,1,0:T(8,128)(2,1)} %bitcast.44), calls=%async_computation.1 | async-start | bytes 8388608 | tf_op jit(solution)/shard_map/all_to_all | solution.py:89
  130.3 2.5 multiply_convert_fusion.1
  132.9 0.1 reduce.1
  133.0 82.8 %all-to-all-done.1 = bf16[32,256,256]{2,1,0:T(8,128)(2,1)} async-done(((bf16[32,256,256]{2,1,0:T(8,128)(2,1)}), bf16[32,256,256]{2,1,0:T(8,128)(2,1)}, u32[]{:S(2)}, u32[]{:S(2)}) %all-to-all-start.1) | async-done | bytes 4194336 | tf_op jit(solution)/shard_map/all_to_all | solution.py:89
  215.8 36.6 %while.11 = (s32[]{:T(128)}, f32[8,1024]{1,0:T(8,128)S(1)}, s32[16,512]{1,0:T(8,128)S(1)}, bf16[16,512,256]{2,1,0:T(8,128)(2,1)}, bf16[256,1024]{1,0:T(8,128)(2,1)S(1)}, /*index=5*/s32[]{:T(128)}, s32[]{:T(128)}) while((s32[]{:T(128)}, f32[8,1024]{1,0:T(8,128)S(1)}, s32[16,512]{1,0:T(8,128)S(1)}, bf16[16,512,256]{2,1,0:T(8,128)(2,1)}, ...), condition=%wide.region_6.7_spmd.clone, body=%wide.region_5.6_spmd.clone.sunk | while | flops 318787584 | bytes 5053083 | solution.py:114
  215.8 1.4 fusion.61
  217.2 0.9 convolution_add_fusion.2
  218.0 1.4 fusion.61
  219.5 0.9 convolution_add_fusion.2
  220.3 1.4 fusion.61
  221.8 0.9 convolution_add_fusion.2
  222.6 1.4 fusion.61
  224.1 0.9 convolution_add_fusion.2
  224.9 1.4 fusion.61
  226.4 0.9 convolution_add_fusion.2
  227.2 1.4 fusion.61
  228.6 0.9 convolution_add_fusion.2
  229.5 1.4 fusion.61
  230.9 0.9 convolution_add_fusion.2
  231.8 1.4 fusion.61
  233.2 0.9 convolution_add_fusion.2
  234.1 1.4 fusion.61
  235.5 0.9 convolution_add_fusion.2
  236.4 1.4 fusion.61
  237.8 0.9 convolution_add_fusion.2
  238.7 1.4 fusion.61
  240.1 0.9 convolution_add_fusion.2
  240.9 1.4 fusion.61
  242.4 0.9 convolution_add_fusion.2
  243.2 1.4 fusion.61
  244.7 0.9 convolution_add_fusion.2
  245.5 1.4 fusion.61
  247.0 0.9 convolution_add_fusion.2
  247.8 1.4 fusion.61
  249.3 0.9 convolution_add_fusion.2
  250.1 1.4 fusion.61
  251.5 0.9 convolution_add_fusion.2
  252.4 0.6 copy-done
  253.0 45.8 %reduce-scatter.2.cloned.1.call-done = f32[8,128]{1,0:T(8,128)} async-done(((f32[8,1024]{1,0:T(8,128)}), f32[8,128]{1,0:T(8,128)}) %reduce-scatter.2.cloned.1.call-update) | async-done | bytes 4112 | tf_op jit(solution)/shard_map/reduce_scatter | solution.py:117
  (57 shorter events, 0.5 us)
Async XLA Ops:
  6.5 7.2 %copy-start.1 = (s32[4096]{0:T(1024)S(1)}, s32[4096]{0:T(1024)}, u32[]{:S(2)}) copy-start(s32[4096]{0:T(1024)} %param.9) | copy-start | bytes 49156
  8.1 43.9 %collective-permute-start = (f32[1024,64]{0,1:T(8,128)S(1)}, f32[1024,64]{0,1:T(8,128)S(1)}, u32[]{:S(2)}, u32[]{:S(2)}) collective-permute-start(f32[1024,64]{0,1:T(8,128)S(1)} %get-tuple-element.74), channel_id=1, source_target_pairs={{0,1},{1,2},{2,3},{3,4},{4,5},{5,6},{6,7},{8,9},{9,10},{10,11},{11... | collective-permute-start | bytes 786440 | tf_op jit(solution)/shard_map/ppermute | solution.py:24
  12.4 39.5 %collective-permute-start.1 = (f32[1024,64]{0,1:T(8,128)S(1)}, f32[1024,64]{0,1:T(8,128)}, u32[]{:S(2)}, u32[]{:S(2)}) collective-permute-start(f32[1024,64]{0,1:T(8,128)S(1)} %get-tuple-element.75), channel_id=1, source_target_pairs={{1,0},{2,1},{3,2},{4,3},{5,4},{6,5},{7,6},{9,8},{10,9},{11,10},{12... | collective-permute-start | bytes 786440 | tf_op jit(solution)/shard_map/ppermute | solution.py:27
  24.3 36.4 %copy-start.2 = (s32[4096]{0:T(1024)S(1)}, s32[4096]{0:T(1024)}, u32[]{:S(2)}) copy-start(s32[4096]{0:T(1024)} %param.7) | copy-start | bytes 49156
  24.3 36.3 %copy-start.3 = (s32[4096]{0:T(1024)S(1)}, s32[4096]{0:T(1024)}, u32[]{:S(2)}) copy-start(s32[4096]{0:T(1024)} %param.8) | copy-start | bytes 49156
  40.8 78.3 %all-to-all-start = ((s32[32,1,256]{2,1,0:T(1,128)}), s32[32,1,256]{2,1,0:T(1,128)S(1)}, u32[]{:S(2)}, u32[]{:S(2)}) async-start(s32[32,1,256]{2,1,0:T(1,128)} %bitcast.2), calls=%async_computation | async-start | bytes 65536 | tf_op jit(solution)/shard_map/all_to_all | solution.py:96
  54.2 21.3 %collective-permute-start.2 = (bf16[256,256]{0,1:T(8,128)(2,1)}, bf16[256,256]{0,1:T(8,128)(2,1)S(1)}, u32[]{:S(2)}, u32[]{:S(2)}) collective-permute-start(bf16[256,256]{0,1:T(8,128)(2,1)} %get-tuple-element.70), channel_id=1, source_target_pairs={{0,8},{8,16},{16,24},{24,32},{32,40},{40,48},{48,56},{56,64},{64,7... | collective-permute-start | bytes 393224 | tf_op jit(solution)/shard_map/ppermute | solution.py:24
  58.7 16.9 %collective-permute-start.3 = (bf16[256,256]{0,1:T(8,128)(2,1)}, bf16[256,256]{0,1:T(8,128)(2,1)S(1)}, u32[]{:S(2)}, u32[]{:S(2)}) collective-permute-start(bf16[256,256]{0,1:T(8,128)(2,1)} %get-tuple-element.71), channel_id=1, source_target_pairs={{8,0},{16,8},{24,16},{32,24},{40,32},{48,40},{56,48},{64,56},{72,6... | collective-permute-start | bytes 393224 | tf_op jit(solution)/shard_map/ppermute | solution.py:27
  119.1 96.7 %all-to-all-start.1 = ((bf16[32,256,256]{2,1,0:T(8,128)(2,1)}), bf16[32,256,256]{2,1,0:T(8,128)(2,1)}, u32[]{:S(2)}, u32[]{:S(2)}) async-start(bf16[32,256,256]{2,1,0:T(8,128)(2,1)} %bitcast.44), calls=%async_computation.1 | async-start | bytes 8388608 | tf_op jit(solution)/shard_map/all_to_all | solution.py:89
  130.3 168.6 %reduce-scatter.2.cloned.1.call-start = ((), (), s32[]{:S(2)}) async-start(), calls=%async_computation.3 | async-start | bytes 36864 | tf_op jit(solution)/shard_map/reduce_scatter | solution.py:117
  252.4 0.6 copy-start
Sparse Core Ops, SparseCore 0:
  253.2 45.6 reduce-scatter.1
where the time goes:
time: 311 us; the launch traced here: 306 us
  waiting for transfers between devices  129 us (41%)
  local copies, waits for them, and re-layouts  52.4 us (17%)
  other arithmetic  38.7 us (12%)
  matrix products  37.5 us (12%)
  starting transfers between devices  34.3 us (11%)
  between operations  13.7 us (4%)
    all_to_all x1, waiting for transfers between devices, per_device(): lax.all_to_all(send_rows.reshape(segments, CAP, 2 * local_bins), 'seg', s...  82.8 us
    reduce_scatter x1, waiting for transfers between devices, per_device(): lax.psum_scatter(partial_lags, 'band', scatter_dimension=1, tiled=True)  45.8 us
    dot_general x16, matrix products, stack_block(): slot_lags = jnp.dot(slot_rows, table, preferred_element_type=jnp.float32)  22.3 us
    scatter x1, other arithmetic, per_device(): jnp.zeros((segments * CAP, 2 * local_bins), jnp.bfloat16).at[slot_index]  20.8 us
    gather x1, local copies, waits for them, and re-layouts, per_device(): second_rows = near_rows[pair_second - seg_position * channels + REACH]  17 us
    scatter x1, local copies, waits for them, and re-layouts, per_device(): jnp.zeros((segments * CAP,), jnp.int32).at[slot_index]  16.1 us
    another operation x5, other arithmetic  15.4 us
    gather x1, local copies, waits for them, and re-layouts, per_device(): first_rows = whitened[pair_first - seg_position * channels]  14.6 us
  transfers between devices with their start and end apart: 7, of which 2 were waited for; matrix products, arithmetic and copies ran while one was open for 30% of the time, Pallas kernels for 0%

commit v1 on v0

v1 whole, which is shorter than its diff:
```python
import math

import jax
import jax.numpy as jnp
from jax import lax
from jax.sharding import PartitionSpec as P

OB_DEV = 8
REACH = 256
FREQ = 1024
LAGS = 1024
HALF_WIN = 64


epsilon = 1e-06


def extended(block, sides, width):
    for axis, dim in sides:
        count = lax.axis_size(axis)
        forward = [(i, i + 1) for i in range(count - 1)]
        backward = [(target, source) for source, target in forward]
        low = lax.ppermute(
            lax.slice_in_dim(block, block.shape[dim] - width, None, axis=dim), axis, forward
        )
        high = lax.ppermute(lax.slice_in_dim(block, 0, width, axis=dim), axis, backward)
        block = jnp.concatenate([low, block, high], axis=dim)
    return block


def window_matrix(local_bins, half_width):
    padded_index = jnp.arange(local_bins + 2 * half_width)[:, None]
    bin_index = jnp.arange(local_bins)[None, :]
    inside = (padded_index >= bin_index) & (padded_index <= bin_index + 2 * half_width)
    return inside.astype(jnp.bfloat16)


def exact_dot(values, selector):
    high = values.astype(jnp.bfloat16)
    rest = values - high.astype(jnp.float32)
    mid = rest.astype(jnp.bfloat16)
    low = (rest - mid.astype(jnp.float32)).astype(jnp.bfloat16)
    total = jnp.dot(high, selector, preferred_element_type=jnp.float32)
    total = total + jnp.dot(mid, selector, preferred_element_type=jnp.float32)
    return total + jnp.dot(low, selector, preferred_element_type=jnp.float32)


def lag_table(first_bin, local_bins, total_bins, lag_count):
    frequency = first_bin + jnp.arange(local_bins, dtype=jnp.int32)
    lag_index = jnp.arange(lag_count, dtype=jnp.int32) - lag_count // 2
    residue = frequency[:, None] * lag_index[None, :] % (2 * total_bins)
    angles = residue.astype(jnp.float32) * (math.pi / total_bins)
    cosine = jnp.cos(angles) / total_bins
    negsine = -jnp.sin(angles) / total_bins
    return jnp.concatenate([cosine, negsine], axis=0).astype(jnp.bfloat16)


def per_device(spectra, pair_first, pair_second, pair_bin):
    seg_position = lax.axis_index("seg")
    band_position = lax.axis_index("band")
    segments = lax.axis_size("seg")
    bands = lax.axis_size("band")
    channels = spectra.shape[1]
    local_bins = spectra.shape[2]
    real_part = spectra[0].astype(jnp.float32)
    imag_part = spectra[1].astype(jnp.float32)
    power_sum = real_part * real_part + imag_part * imag_part
    padded_power = extended(power_sum, (("band", 1),), HALF_WIN)
    window_sum = exact_dot(padded_power, window_matrix(local_bins, HALF_WIN))
    scaling = lax.rsqrt(window_sum / (2 * HALF_WIN + 1) + epsilon)
    whitened = jnp.concatenate([real_part * scaling, imag_part * scaling], axis=1).astype(
        jnp.bfloat16
    )
    first_rows = whitened[pair_first - seg_position * channels]
    near_rows = extended(whitened, (("seg", 0),), REACH)
    second_rows = near_rows[pair_second - seg_position * channels + REACH]
    first_real = first_rows[:, :local_bins].astype(jnp.float32)
    first_imag = first_rows[:, local_bins:].astype(jnp.float32)
    second_real = second_rows[:, :local_bins].astype(jnp.float32)
    second_imag = second_rows[:, local_bins:].astype(jnp.float32)
    cross_real = first_real * second_real + first_imag * second_imag
    cross_imag = first_imag * second_real - first_real * second_imag
    cross_both = jnp.concatenate([cross_real, cross_imag], axis=1).astype(jnp.bfloat16)
    all_bins = segments * OB_DEV
    members = (pair_bin[:, None] == jnp.arange(all_bins, dtype=jnp.int32)[None, :]).astype(
        jnp.bfloat16
    )
    local_stack = lax.dot_general(
        members, cross_both, (((0,), (0,)), ((), ())), preferred_element_type=jnp.float32
    )
    gathered = lax.all_to_all(local_stack, "seg", split_axis=0, concat_axis=0, tiled=True)
    stack = jnp.sum(gathered.reshape(segments, OB_DEV, 2 * local_bins), axis=0)
    table = lag_table(band_position * local_bins, local_bins, FREQ, LAGS)
    partial_lags = jnp.dot(
        stack, table.astype(jnp.float32), precision=lax.Precision.HIGHEST
    )
    pieces = lax.all_to_all(partial_lags, "band", split_axis=1, concat_axis=0, tiled=True)
    return jnp.sum(pieces.reshape(bands, OB_DEV, LAGS // bands), axis=0)


def solution(mesh):
    placed = (P(None, "seg", "band"), P("seg"), P("seg"), P("seg"))
    return jax.shard_map(
        per_device, mesh=mesh, in_specs=placed, out_specs=P("seg", "band"), check_vma=False
    )
```

time: 311 us -> 106 us (0.34); the launches traced: 306 us -> 106 us
  waiting for transfers between devices: 129 us -> 21.6 us
  matrix products: 37.5 us -> 4.01 us
  other arithmetic: 38.7 us -> 7.93 us
  local copies, waits for them, and re-layouts: 52.4 us -> 36.6 us
  between operations: 13.7 us -> 0.22 us
  blocking collectives: 0 us -> 9.52 us
  starting transfers between devices: 34.3 us -> 25.9 us
    all_to_all x2 -> x1, waiting for transfers between devices: 82.8 us -> 10.8 us  [per_device(): lax.all_to_all(local_stack, 'seg', split_axis=0, concat_axis=0, tiled=True)]
    reduce_scatter x1 -> x0, waiting for transfers between devices: 45.8 us -> none  [per_device(): lax.psum_scatter(partial_lags, 'band', scatter_dimension=1, tiled=True)]
    dot_general x33 -> x5, matrix products: 37.5 us -> 4.01 us  [the longest x1 2.57 us: per_device(): lax.dot_general(members, cross_both, (((0,), (0,)), ((), ())), preferred_...]
    scatter x1 -> x0, other arithmetic: 20.8 us -> none  [per_device(): jnp.zeros((segments * CAP, 2 * local_bins), jnp.bfloat16).at[slot_index]]
    scatter x1 -> x0, local copies, waits for them, and re-layouts: 16.1 us -> none  [per_device(): jnp.zeros((segments * CAP,), jnp.int32).at[slot_index]]
    another operation x5 -> x2, other arithmetic: 15.4 us -> 4.89 us
    all_to_all x2 -> x1, starting transfers between devices: 22.3 us -> 12 us  [per_device(): lax.all_to_all(local_stack, 'seg', split_axis=0, concat_axis=0, tiled=True)]
    all_to_all x0 -> x1, blocking collectives: none -> 9.52 us  [per_device(): lax.all_to_all(partial_lags, 'band', split_axis=1, concat_axis=0, tiled=T...]
  transfers between devices with their start and end apart: 7 -> 5, of which waited for: 2 -> 3; matrix products, arithmetic and copies ran while one was open for 30% -> 19% of each run, Pallas kernels for 0% -> 0%
where the time goes in v1:
time: 106 us
  local copies, waits for them, and re-layouts  36.6 us (35%)
  starting transfers between devices  25.9 us (24%)
  waiting for transfers between devices  21.6 us (20%)
  blocking collectives  9.52 us (9%)
  other arithmetic  7.93 us (7%)
  matrix products  4.01 us (4%)
    gather x1, local copies, waits for them, and re-layouts, per_device(): second_rows = near_rows[pair_second - seg_position * channels + REACH]  17 us
    gather x1, local copies, waits for them, and re-layouts, per_device(): first_rows = whitened[pair_first - seg_position * channels]  16.6 us
    all_to_all x1, starting transfers between devices, per_device(): lax.all_to_all(local_stack, 'seg', split_axis=0, concat_axis=0, tiled=True)  12 us
    all_to_all x1, waiting for transfers between devices, per_device(): lax.all_to_all(local_stack, 'seg', split_axis=0, concat_axis=0, tiled=True)  10.8 us
    ppermute x2, starting transfers between devices, extended(): lax.ppermute(lax.slice_in_dim(block, block.shape[dim] - width, None, axis...  10.7 us
    all_to_all x1, blocking collectives, per_device(): lax.all_to_all(partial_lags, 'band', split_axis=1, concat_axis=0, tiled=T...  9.52 us
    ppermute x2, waiting for transfers between devices, extended(): lax.ppermute(lax.slice_in_dim(block, 0, width, axis=dim), axis, backward)  7.2 us
    another operation x2, other arithmetic  4.89 us
  transfers between devices with their start and end apart: 5, of which 3 were waited for; matrix products, arithmetic and copies ran while one was open for 19% of the time, Pallas kernels for 0%

profile of v1, /device:TPU:1, one launch (start us, length us, event | category | flops | bytes accessed | tf_op | source)
XLA Modules:
  0.0 105.8 jit_solution(12813751956930395136)
XLA Ops:
  0.0 1.1 %fusion.47 = (bf16[1,1024,128]{2,1,0:T(8,128)(2,1)S(1)}, bf16[1,1024,128]{2,1,0:T(8,128)(2,1)S(1)}) fusion(bf16[2,1024,128]{2,1,0:T(8,128)(2,1)} %param.4), kind=kLoop, calls=%fused_computation.75 | loop fusion | bytes 1048576 | tf_op jit(solution)/shard_map/slice | solution.py:65
  1.1 0.1 copy.10
  1.2 0.1 copy.9
  1.4 0.1 fusion.17
  1.5 4.4 %collective-permute-start = (f32[1024,64]{0,1:T(8,128)S(1)}, f32[1024,64]{0,1:T(8,128)S(1)}, u32[]{:S(2)}, u32[]{:S(2)}) collective-permute-start(f32[1024,64]{0,1:T(8,128)S(1)} %get-tuple-element.11), channel_id=1, source_target_pairs={{0,1},{1,2},{2,3},{3,4},{4,5},{5,6},{6,7},{8,9},{9,10},{10,11},{11... | collective-permute-start | bytes 786440 | tf_op jit(solution)/shard_map/ppermute | solution.py:23
  5.9 1.3 %collective-permute-start.1 = (f32[1024,64]{0,1:T(8,128)S(1)}, f32[1024,64]{0,1:T(8,128)S(1)}, u32[]{:S(2)}, u32[]{:S(2)}) collective-permute-start(f32[1024,64]{0,1:T(8,128)S(1)} %get-tuple-element.12), channel_id=1, source_target_pairs={{1,0},{2,1},{3,2},{4,3},{5,4},{6,5},{7,6},{9,8},{10,9},{11,10},{12... | collective-permute-start | bytes 786440 | tf_op jit(solution)/shard_map/ppermute | solution.py:26
  7.2 3.6 %collective-permute-done = f32[1024,64]{0,1:T(8,128)S(1)} collective-permute-done((f32[1024,64]{0,1:T(8,128)S(1)}, f32[1024,64]{0,1:T(8,128)S(1)}, u32[]{:S(2)}, u32[]{:S(2)}) %collective-permute-start) | collective-permute-done | bytes 262176 | tf_op jit(solution)/shard_map/ppermute | solution.py:23
  10.9 7.2 %collective-permute-done.1 = f32[1024,64]{0,1:T(8,128)S(1)} collective-permute-done((f32[1024,64]{0,1:T(8,128)S(1)}, f32[1024,64]{0,1:T(8,128)S(1)}, u32[]{:S(2)}, u32[]{:S(2)}) %collective-permute-start.1) | collective-permute-done | bytes 262176 | tf_op jit(solution)/shard_map/ppermute | solution.py:26
  18.1 0.3 fusion.30
  18.3 0.3 fusion.23
  18.6 0.0 copy-start
  18.6 0.0 copy-start.1
  18.6 0.4 fusion.19
  19.0 0.7 fusion.26
  19.7 6.3 %collective-permute-start.2 = (bf16[256,256]{0,1:T(8,128)(2,1)}, bf16[256,256]{0,1:T(8,128)(2,1)S(1)}, u32[]{:S(2)}, u32[]{:S(2)}) collective-permute-start(bf16[256,256]{0,1:T(8,128)(2,1)} %get-tuple-element.7), channel_id=1, source_target_pairs={{0,8},{8,16},{16,24},{24,32},{32,40},{40,48},{48,56},{56,64},{64,7... | collective-permute-start | bytes 393224 | tf_op jit(solution)/shard_map/ppermute | solution.py:23
  26.0 1.9 %collective-permute-start.3 = (bf16[256,256]{0,1:T(8,128)(2,1)S(1)}, bf16[256,256]{0,1:T(8,128)(2,1)S(1)}, u32[]{:S(2)}, u32[]{:S(2)}) collective-permute-start(bf16[256,256]{0,1:T(8,128)(2,1)S(1)} %get-tuple-element.8), channel_id=1, source_target_pairs={{8,0},{16,8},{24,16},{32,24},{40,32},{48,40},{56,48},{64,56},{72,6... | collective-permute-start | bytes 393224 | tf_op jit(solution)/shard_map/ppermute | solution.py:26
  27.9 0.0 copy-done
  27.9 0.0 copy-done.1
  27.9 0.6 fusion.38
  28.6 0.2 copy.7
  28.8 16.6 %gather_fusion = bf16[4096,256]{1,0:T(8,128)(2,1)S(1)} fusion(bf16[1024,256]{1,0:T(8,128)(2,1)S(1)} %copy.7, s32[4096]{0:T(1024)} %get-tuple-element.17), kind=kCustom, calls=%fused_computation | custom fusion | bytes 4210688 | tf_op jit(solution)/shard_map/gather | solution.py:74
  45.4 0.0 collective-permute-done.2
  45.4 0.0 collective-permute-done.3
  45.4 0.9 pad_maximum_fusion.1
  46.3 1.4 %copy.8 = bf16[1536,256]{1,0:T(8,128)(2,1)S(1)} copy(bf16[1536,256]{0,1:T(8,128)(2,1)} %pad_maximum_fusion.1) | data formatting | bytes 1572864 | tf_op jit(solution)/shard_map/concatenate | solution.py:27
  47.7 17.0 %gather_fusion.1 = bf16[4096,256]{1,0:T(8,128)(2,1)} fusion(bf16[1536,256]{1,0:T(8,128)(2,1)S(1)} %copy.8, s32[4096]{0:T(1024)S(1)} %get-tuple-element.18), kind=kCustom, calls=%fused_computation.1 | custom fusion | bytes 4210688 | tf_op jit(solution)/shard_map/gather | solution.py:76
  64.8 0.0 copy-start.2
  64.8 2.4 %fusion.2 = (bf16[4096,128]{1,0:T(8,128)(2,1)S(1)}, bf16[4096,128]{1,0:T(8,128)(2,1)S(1)}) fusion(bf16[4096,256]{1,0:T(8,128)(2,1)} %gather_fusion.1, bf16[4096,256]{1,0:T(8,128)(2,1)S(1)} %gather_fusion), kind=kLoop, calls=%fused_computation.9 | loop fusion | flops 6291456 | bytes 6291456 | tf_op jit(solution)/shard_map/convert.4
  67.1 0.0 copy-done.2
  67.2 2.6 %fusion.13 = f32[32,8,256]{2,1,0:T(8,128)} fusion(bf16[4096,128]{1,0:T(8,128)(2,1)S(1)} %get-tuple-element.6, bf16[4096,128]{1,0:T(8,128)(2,1)S(1)} %get-tuple-element.5, s32[4096]{0:T(1024)S(1)} %copy-done.2), kind=kOutput, calls=%fused_computation.21 | convolution fusion | flops 542113792 | bytes 2375680 | tf_op jit(solution)/shard_map/dot_general | solution.py:88
  69.7 12.0 %all-to-all-start = ((f32[32,8,256]{2,1,0:T(8,128)}), f32[32,8,256]{2,1,0:T(8,128)S(1)}, u32[]{:S(2)}, u32[]{:S(2)}) async-start(f32[32,8,256]{2,1,0:T(8,128)} %fusion.13), calls=%async_computation | async-start | bytes 524288 | tf_op jit(solution)/shard_map/all_to_all | solution.py:91
  81.8 2.5 %multiply_convert_fusion.1 = (bf16[128,1024]{0,1:T(8,128)(2,1)S(1)}, bf16[128,1024]{0,1:T(8,128)(2,1)S(1)}) fusion(s32[1024]{0:T(1024)S(1)} %iota_add_fusion, s32[128]{0:T(128)S(1)} %iota_add_fusion.1), kind=kLoop, calls=%fused_computation.50 | loop fusion | flops 2490368 | bytes 528896 | tf_op jit(solution)/shard_map/convert.2
  84.3 0.1 pad_maximum_fusion.3
  84.4 10.8 %all-to-all-done = f32[32,8,256]{2,1,0:T(8,128)S(1)} async-done(((f32[32,8,256]{2,1,0:T(8,128)}), f32[32,8,256]{2,1,0:T(8,128)S(1)}, u32[]{:S(2)}, u32[]{:S(2)}) %all-to-all-start) | async-done | bytes 262176 | tf_op jit(solution)/shard_map/all_to_all | solution.py:91
  95.2 0.5 fusion.40
  95.7 9.5 %all_to_all.19 = f32[8,8,128]{2,0,1:T(8,128)S(1)} all-to-all(f32[8,8,128]{2,0,1:T(8,128)S(1)} %fusion.40), channel_id=1, replica_groups=mesh['seg'=32,'band'=8] {'band'}, dimensions={1} | all-to-all | bytes 65536 | tf_op jit(solution)/shard_map/all_to_all | solution.py:97
  105.2 0.6 reduce_sum.19
  (6 shorter events, 0.1 us)
Async XLA Ops:
  1.5 9.3 %collective-permute-start = (f32[1024,64]{0,1:T(8,128)S(1)}, f32[1024,64]{0,1:T(8,128)S(1)}, u32[]{:S(2)}, u32[]{:S(2)}) collective-permute-start(f32[1024,64]{0,1:T(8,128)S(1)} %get-tuple-element.11), channel_id=1, source_target_pairs={{0,1},{1,2},{2,3},{3,4},{4,5},{5,6},{6,7},{8,9},{9,10},{10,11},{11... | collective-permute-start | bytes 786440 | tf_op jit(solution)/shard_map/ppermute | solution.py:23
  5.9 12.1 %collective-permute-start.1 = (f32[1024,64]{0,1:T(8,128)S(1)}, f32[1024,64]{0,1:T(8,128)S(1)}, u32[]{:S(2)}, u32[]{:S(2)}) collective-permute-start(f32[1024,64]{0,1:T(8,128)S(1)} %get-tuple-element.12), channel_id=1, source_target_pairs={{1,0},{2,1},{3,2},{4,3},{5,4},{6,5},{7,6},{9,8},{10,9},{11,10},{12... | collective-permute-start | bytes 786440 | tf_op jit(solution)/shard_map/ppermute | solution.py:26
  18.6 9.3 %copy-start = (s32[4096]{0:T(1024)S(1)}, s32[4096]{0:T(1024)}, u32[]{:S(2)}) copy-start(s32[4096]{0:T(1024)} %param.5) | copy-start | bytes 49156
  18.6 9.3 %copy-start.1 = (s32[4096]{0:T(1024)S(1)}, s32[4096]{0:T(1024)}, u32[]{:S(2)}) copy-start(s32[4096]{0:T(1024)} %param.6) | copy-start | bytes 49156
  19.7 25.7 %collective-permute-start.2 = (bf16[256,256]{0,1:T(8,128)(2,1)}, bf16[256,256]{0,1:T(8,128)(2,1)S(1)}, u32[]{:S(2)}, u32[]{:S(2)}) collective-permute-start(bf16[256,256]{0,1:T(8,128)(2,1)} %get-tuple-element.7), channel_id=1, source_target_pairs={{0,8},{8,16},{16,24},{24,32},{32,40},{40,48},{48,56},{56,64},{64,7... | collective-permute-start | bytes 393224 | tf_op jit(solution)/shard_map/ppermute | solution.py:23
  26.0 19.4 %collective-permute-start.3 = (bf16[256,256]{0,1:T(8,128)(2,1)S(1)}, bf16[256,256]{0,1:T(8,128)(2,1)S(1)}, u32[]{:S(2)}, u32[]{:S(2)}) collective-permute-start(bf16[256,256]{0,1:T(8,128)(2,1)S(1)} %get-tuple-element.8), channel_id=1, source_target_pairs={{8,0},{16,8},{24,16},{32,24},{40,32},{48,40},{56,48},{64,56},{72,6... | collective-permute-start | bytes 393224 | tf_op jit(solution)/shard_map/ppermute | solution.py:26
  64.8 2.4 %copy-start.2 = (s32[4096]{0:T(1024)S(1)}, s32[4096]{0:T(1024)}, u32[]{:S(2)}) copy-start(s32[4096]{0:T(1024)} %param.7) | copy-start | bytes 49156
  69.7 25.4 %all-to-all-start = ((f32[32,8,256]{2,1,0:T(8,128)}), f32[32,8,256]{2,1,0:T(8,128)S(1)}, u32[]{:S(2)}, u32[]{:S(2)}) async-start(f32[32,8,256]{2,1,0:T(8,128)} %fusion.13), calls=%async_computation | async-start | bytes 524288 | tf_op jit(solution)/shard_map/all_to_all | solution.py:91

commit v2 on v1

--- a/solution.py
+++ b/solution.py
@@ -36,13 +36,20 @@
 
 
 def exact_dot(values, selector):
-    high = values.astype(jnp.bfloat16)
-    rest = values - high.astype(jnp.float32)
-    mid = rest.astype(jnp.bfloat16)
-    low = (rest - mid.astype(jnp.float32)).astype(jnp.bfloat16)
-    total = jnp.dot(high, selector, preferred_element_type=jnp.float32)
-    total = total + jnp.dot(mid, selector, preferred_element_type=jnp.float32)
-    return total + jnp.dot(low, selector, preferred_element_type=jnp.float32)
+    high = lax.reduce_precision(values, exponent_bits=8, mantissa_bits=7)
+    rest = values - high
+    mid = lax.reduce_precision(rest, exponent_bits=8, mantissa_bits=7)
+    low = rest - mid
+    total = jnp.dot(high.astype(jnp.bfloat16), selector, preferred_element_type=jnp.float32)
+    total = total + jnp.dot(mid.astype(jnp.bfloat16), selector, preferred_element_type=jnp.float32)
+    return total + jnp.dot(low.astype(jnp.bfloat16), selector, preferred_element_type=jnp.float32)
+
+
+def select_rows(table, index):
+    chosen = (index[:, None] == jnp.arange(table.shape[0], dtype=jnp.int32)[None, :]).astype(
+        table.dtype
+    )
+    return jnp.dot(chosen, table, preferred_element_type=jnp.float32)
 
 
 def lag_table(first_bin, local_bins, total_bins, lag_count):
@@ -71,13 +78,13 @@
     whitened = jnp.concatenate([real_part * scaling, imag_part * scaling], axis=1).astype(
         jnp.bfloat16
     )
-    first_rows = whitened[pair_first - seg_position * channels]
+    first_rows = select_rows(whitened, pair_first - seg_position * channels)
     near_rows = extended(whitened, (("seg", 0),), REACH)
-    second_rows = near_rows[pair_second - seg_position * channels + REACH]
-    first_real = first_rows[:, :local_bins].astype(jnp.float32)
-    first_imag = first_rows[:, local_bins:].astype(jnp.float32)
-    second_real = second_rows[:, :local_bins].astype(jnp.float32)
-    second_imag = second_rows[:, local_bins:].astype(jnp.float32)
+    second_rows = select_rows(near_rows, pair_second - seg_position * channels + REACH)
+    first_real = first_rows[:, :local_bins]
+    first_imag = first_rows[:, local_bins:]
+    second_real = second_rows[:, :local_bins]
+    second_imag = second_rows[:, local_bins:]
     cross_real = first_real * second_real + first_imag * second_imag
     cross_imag = first_imag * second_real - first_real * second_imag
     cross_both = jnp.concatenate([cross_real, cross_imag], axis=1).astype(jnp.bfloat16)

time: 106 us -> 74.8 us (0.71)
  local copies, waits for them, and re-layouts: 36.6 us -> 1.43 us
  matrix products: 4.01 us -> 12 us
  other arithmetic: 7.93 us -> 4.2 us
  waiting for transfers between devices: 21.6 us -> 22.8 us
    gather x2 -> x0, local copies, waits for them, and re-layouts: 33.6 us -> none  [the longest x1 17 us: per_device(): second_rows = near_rows[pair_second - seg_position * channels + REACH]]
    dot_general x3 -> x5, matrix products: 0.93 us -> 9.3 us  [the longest x2 8.28 us: select_rows(): return jnp.dot(chosen, table, preferred_element_type=jnp.float32)]
    ppermute x2, waiting for transfers between devices: 7.2 us -> 9.08 us  [extended(): lax.ppermute(lax.slice_in_dim(block, 0, width, axis=dim), axis, backward)]
    concatenate x3 -> x0, other arithmetic: 1.63 us -> none  [the longest x1 0.93 us: extended(): block = jnp.concatenate([low, block, high], axis=dim)]
    concatenate x2 -> x0, local copies, waits for them, and re-layouts: 1.61 us -> none  [the longest x1 1.4 us: extended(): block = jnp.concatenate([low, block, high], axis=dim)]
    another operation x2, other arithmetic: 4.89 us -> 3.37 us
  transfers between devices with their start and end apart: 5 -> 5, of which waited for: 3 -> 4; matrix products, arithmetic and copies ran while one was open for 19% -> 8% of each run, Pallas kernels for 0% -> 0%
where the time goes in v2:
time: 74.8 us; the launch traced here: 74.4 us
  starting transfers between devices  25 us (33%)
  waiting for transfers between devices  22.8 us (30%)
  matrix products  12 us (16%)
  blocking collectives  8.82 us (12%)
  other arithmetic  4.2 us (6%)
  local copies, waits for them, and re-layouts  1.43 us (2%)
    all_to_all x1, starting transfers between devices, per_device(): lax.all_to_all(local_stack, 'seg', split_axis=0, concat_axis=0, tiled=True)  11.1 us
    ppermute x2, starting transfers between devices, extended(): lax.ppermute(lax.slice_in_dim(block, block.shape[dim] - width, None, axis...  10.7 us
    all_to_all x1, waiting for transfers between devices, per_device(): lax.all_to_all(local_stack, 'seg', split_axis=0, concat_axis=0, tiled=True)  10.1 us
    ppermute x2, waiting for transfers between devices, extended(): lax.ppermute(lax.slice_in_dim(block, 0, width, axis=dim), axis, backward)  9.08 us
    all_to_all x1, blocking collectives, per_device(): lax.all_to_all(partial_lags, 'band', split_axis=1, concat_axis=0, tiled=T...  8.82 us
    dot_general x2, matrix products, select_rows(): return jnp.dot(chosen, table, preferred_element_type=jnp.float32)  8.28 us
    ppermute x2, waiting for transfers between devices, extended(): lax.ppermute(lax.slice_in_dim(block, block.shape[dim] - width, None, axis...  3.61 us
    another operation x2, other arithmetic  3.37 us
  transfers between devices with their start and end apart: 5, of which 4 were waited for; matrix products, arithmetic and copies ran while one was open for 8% of the time, Pallas kernels for 0%

profile of v2, /device:TPU:1, one launch (start us, length us, event | category | flops | bytes accessed | tf_op | source)
XLA Modules:
  0.0 74.4 jit_solution(3552078366453263378)
XLA Ops:
  0.0 0.0 copy-start.1
  0.0 0.0 copy-start
  0.0 1.1 %fusion.56 = (bf16[1,1024,128]{2,1,0:T(8,128)(2,1)S(1)}, bf16[1,1024,128]{2,1,0:T(8,128)(2,1)S(1)}) fusion(bf16[2,1024,128]{2,1,0:T(8,128)(2,1)} %param.4), kind=kLoop, calls=%fused_computation.79 | loop fusion | bytes 1048576 | tf_op jit(solution)/shard_map/slice | solution.py:72
  1.1 0.1 copy.7
  1.2 0.1 copy.8
  1.4 0.1 fusion.28
  1.5 4.4 %collective-permute-start = (f32[1024,64]{0,1:T(8,128)S(1)}, f32[1024,64]{0,1:T(8,128)S(1)}, u32[]{:S(2)}, u32[]{:S(2)}) collective-permute-start(f32[1024,64]{0,1:T(8,128)S(1)} %get-tuple-element.11), channel_id=1, source_target_pairs={{0,1},{1,2},{2,3},{3,4},{4,5},{5,6},{6,7},{8,9},{9,10},{10,11},{11... | collective-permute-start | bytes 786440 | tf_op jit(solution)/shard_map/ppermute | solution.py:23
  5.9 1.3 %collective-permute-start.1 = (f32[1024,64]{0,1:T(8,128)S(1)}, f32[1024,64]{0,1:T(8,128)S(1)}, u32[]{:S(2)}, u32[]{:S(2)}) collective-permute-start(f32[1024,64]{0,1:T(8,128)S(1)} %get-tuple-element.12), channel_id=1, source_target_pairs={{1,0},{2,1},{3,2},{4,3},{5,4},{6,5},{7,6},{9,8},{10,9},{11,10},{12... | collective-permute-start | bytes 786440 | tf_op jit(solution)/shard_map/ppermute | solution.py:26
  7.2 0.0 copy-done.1
  7.3 0.0 copy-done
  7.3 3.6 %collective-permute-done = f32[1024,64]{0,1:T(8,128)S(1)} collective-permute-done((f32[1024,64]{0,1:T(8,128)S(1)}, f32[1024,64]{0,1:T(8,128)S(1)}, u32[]{:S(2)}, u32[]{:S(2)}) %collective-permute-start) | collective-permute-done | bytes 262176 | tf_op jit(solution)/shard_map/ppermute | solution.py:23
  10.9 7.2 %collective-permute-done.1 = f32[1024,64]{0,1:T(8,128)S(1)} collective-permute-done((f32[1024,64]{0,1:T(8,128)S(1)}, f32[1024,64]{0,1:T(8,128)S(1)}, u32[]{:S(2)}, u32[]{:S(2)}) %collective-permute-start.1) | collective-permute-done | bytes 262176 | tf_op jit(solution)/shard_map/ppermute | solution.py:26
  18.1 0.3 fusion.36
  18.4 0.3 fusion.34
  18.7 0.4 fusion.29
  19.1 6.3 %collective-permute-start.2 = (bf16[256,256]{0,1:T(8,128)(2,1)S(1)}, bf16[256,256]{0,1:T(8,128)(2,1)S(1)}, u32[]{:S(2)}, u32[]{:S(2)}) collective-permute-start(bf16[256,256]{0,1:T(8,128)(2,1)S(1)} %get-tuple-element.7), channel_id=1, source_target_pairs={{0,8},{8,16},{16,24},{24,32},{32,40},{40,48},{48,56},{56,64},{64,7... | collective-permute-start | bytes 393224 | tf_op jit(solution)/shard_map/ppermute | solution.py:23
  25.5 1.9 %collective-permute-start.3 = (bf16[256,256]{0,1:T(8,128)(2,1)S(1)}, bf16[256,256]{0,1:T(8,128)(2,1)S(1)}, u32[]{:S(2)}, u32[]{:S(2)}) collective-permute-start(bf16[256,256]{0,1:T(8,128)(2,1)S(1)} %get-tuple-element.8), channel_id=1, source_target_pairs={{8,0},{16,8},{24,16},{32,24},{40,32},{48,40},{56,48},{64,56},{72,6... | collective-permute-start | bytes 393224 | tf_op jit(solution)/shard_map/ppermute | solution.py:26
  27.4 3.4 %fusion.1 = f32[4096,256]{0,1:T(8,128)S(1)} fusion(s32[4096]{0:T(1024)S(1)} %get-tuple-element.18, bf16[1024,128]{0,1:T(8,128)(2,1)S(1)} %get-tuple-element.10, bf16[1024,128]{0,1:T(8,128)(2,1)S(1)} %get-tuple-element.9), kind=kOutput, calls=%fused_computation.3 | convolution fusion | flops 2152726528 | bytes 4734976 | tf_op jit(solution)/shard_map/dot_general | solution.py:52
  30.8 0.0 collective-permute-done.2
  30.8 1.9 %collective-permute-done.3 = bf16[256,256]{0,1:T(8,128)(2,1)S(1)} collective-permute-done((bf16[256,256]{0,1:T(8,128)(2,1)S(1)}, bf16[256,256]{0,1:T(8,128)(2,1)S(1)}, u32[]{:S(2)}, u32[]{:S(2)}) %collective-permute-start.3) | collective-permute-done | bytes 131104 | tf_op jit(solution)/shard_map/ppermute | solution.py:26
  32.7 4.9 %fusion = f32[4096,256]{0,1:T(8,128)S(1)} fusion(s32[4096]{0:T(1024)S(1)} %get-tuple-element.17, bf16[256,256]{0,1:T(8,128)(2,1)S(1)} %collective-permute-done.3, bf16[1024,128]{0,1:T(8,128)(2,1)S(1)} %get-tuple-element.10, bf16[1024,128]{0,1:T(8,128)(2,1)S(1)} %get-tuple-element.9, bf16[256,256]{0,1:T(8,128)(2,1)S(1)} %collective-permute-done.2), kind=kOutput, calls=%fused_computation.1 | convolution fusion | flops 3230662656 | bytes 4997120 | tf_op jit(solution)/shard_map/dot_general | solution.py:52
  37.6 0.0 copy-start.2
  37.6 0.9 %add_convert_fusion = (bf16[4096,128]{0,1:T(8,128)(2,1)S(1)}, bf16[4096,128]{0,1:T(8,128)(2,1)S(1)}) fusion(f32[4096,256]{0,1:T(8,128)S(1)} %fusion, f32[4096,256]{0,1:T(8,128)S(1)} %fusion.1), kind=kLoop, calls=%fused_computation.13 | loop fusion | flops 4194304 | bytes 10485760 | tf_op jit(solution)/shard_map/convert.4
  38.5 0.0 copy-done.2
  38.5 2.2 %fusion.15 = f32[32,8,256]{2,1,0:T(8,128)} fusion(bf16[4096,128]{0,1:T(8,128)(2,1)S(1)} %get-tuple-element.6, bf16[4096,128]{0,1:T(8,128)(2,1)S(1)} %get-tuple-element.5, s32[4096]{0:T(1024)S(1)} %copy-done.2), kind=kOutput, calls=%fused_computation.24 | convolution fusion | flops 543162368 | bytes 2375680 | tf_op jit(solution)/shard_map/dot_general | solution.py:95
  40.6 11.1 %all-to-all-start = ((f32[32,8,256]{2,1,0:T(8,128)}), f32[32,8,256]{2,1,0:T(8,128)S(1)}, u32[]{:S(2)}, u32[]{:S(2)}) async-start(f32[32,8,256]{2,1,0:T(8,128)} %fusion.15), calls=%async_computation | async-start | bytes 524288 | tf_op jit(solution)/shard_map/all_to_all | solution.py:98
  51.7 2.5 %multiply_convert_fusion.1 = (bf16[128,1024]{0,1:T(8,128)(2,1)S(1)}, bf16[128,1024]{0,1:T(8,128)(2,1)S(1)}) fusion(s32[1024]{0:T(1024)S(1)} %iota_add_fusion, s32[128]{0:T(128)S(1)} %iota_add_fusion.1), kind=kLoop, calls=%fused_computation.56 | loop fusion | flops 2490368 | bytes 528896 | tf_op jit(solution)/shard_map/convert.2
  54.3 0.1 pad_maximum_fusion.1
  54.3 10.1 %all-to-all-done = f32[32,8,256]{2,1,0:T(8,128)S(1)} async-done(((f32[32,8,256]{2,1,0:T(8,128)}), f32[32,8,256]{2,1,0:T(8,128)S(1)}, u32[]{:S(2)}, u32[]{:S(2)}) %all-to-all-start) | async-done | bytes 262176 | tf_op jit(solution)/shard_map/all_to_all | solution.py:98
  64.5 0.5 fusion.47
  65.0 8.8 %all_to_all.19 = f32[8,8,128]{2,0,1:T(8,128)S(1)} all-to-all(f32[8,8,128]{2,0,1:T(8,128)S(1)} %fusion.47), channel_id=1, replica_groups=mesh['seg'=32,'band'=8] {'band'}, dimensions={1} | all-to-all | bytes 65536 | tf_op jit(solution)/shard_map/all_to_all | solution.py:104
  73.8 0.6 reduce_sum.19
  (7 shorter events, 0.1 us)
Async XLA Ops:
  0.0 7.2 %copy-start.1 = (s32[4096]{0:T(1024)S(1)}, s32[4096]{0:T(1024)}, u32[]{:S(2)}) copy-start(s32[4096]{0:T(1024)} %param.5) | copy-start | bytes 49156
  0.0 7.3 %copy-start = (s32[4096]{0:T(1024)S(1)}, s32[4096]{0:T(1024)}, u32[]{:S(2)}) copy-start(s32[4096]{0:T(1024)} %param.6) | copy-start | bytes 49156
  1.5 9.3 %collective-permute-start = (f32[1024,64]{0,1:T(8,128)S(1)}, f32[1024,64]{0,1:T(8,128)S(1)}, u32[]{:S(2)}, u32[]{:S(2)}) collective-permute-start(f32[1024,64]{0,1:T(8,128)S(1)} %get-tuple-element.11), channel_id=1, source_target_pairs={{0,1},{1,2},{2,3},{3,4},{4,5},{5,6},{6,7},{8,9},{9,10},{10,11},{11... | collective-permute-start | bytes 786440 | tf_op jit(solution)/shard_map/ppermute | solution.py:23
  5.9 12.1 %collective-permute-start.1 = (f32[1024,64]{0,1:T(8,128)S(1)}, f32[1024,64]{0,1:T(8,128)S(1)}, u32[]{:S(2)}, u32[]{:S(2)}) collective-permute-start(f32[1024,64]{0,1:T(8,128)S(1)} %get-tuple-element.12), channel_id=1, source_target_pairs={{1,0},{2,1},{3,2},{4,3},{5,4},{6,5},{7,6},{9,8},{10,9},{11,10},{12... | collective-permute-start | bytes 786440 | tf_op jit(solution)/shard_map/ppermute | solution.py:26
  19.1 11.6 %collective-permute-start.2 = (bf16[256,256]{0,1:T(8,128)(2,1)S(1)}, bf16[256,256]{0,1:T(8,128)(2,1)S(1)}, u32[]{:S(2)}, u32[]{:S(2)}) collective-permute-start(bf16[256,256]{0,1:T(8,128)(2,1)S(1)} %get-tuple-element.7), channel_id=1, source_target_pairs={{0,8},{8,16},{16,24},{24,32},{32,40},{40,48},{48,56},{56,64},{64,7... | collective-permute-start | bytes 393224 | tf_op jit(solution)/shard_map/ppermute | solution.py:23
  25.5 7.2 %collective-permute-start.3 = (bf16[256,256]{0,1:T(8,128)(2,1)S(1)}, bf16[256,256]{0,1:T(8,128)(2,1)S(1)}, u32[]{:S(2)}, u32[]{:S(2)}) collective-permute-start(bf16[256,256]{0,1:T(8,128)(2,1)S(1)} %get-tuple-element.8), channel_id=1, source_target_pairs={{8,0},{16,8},{24,16},{32,24},{40,32},{48,40},{56,48},{64,56},{72,6... | collective-permute-start | bytes 393224 | tf_op jit(solution)/shard_map/ppermute | solution.py:26
  37.6 0.9 %copy-start.2 = (s32[4096]{0:T(1024)S(1)}, s32[4096]{0:T(1024)}, u32[]{:S(2)}) copy-start(s32[4096]{0:T(1024)} %param.7) | copy-start | bytes 49156
  40.6 23.9 %all-to-all-start = ((f32[32,8,256]{2,1,0:T(8,128)}), f32[32,8,256]{2,1,0:T(8,128)S(1)}, u32[]{:S(2)}, u32[]{:S(2)}) async-start(f32[32,8,256]{2,1,0:T(8,128)} %fusion.15), calls=%async_computation | async-start | bytes 524288 | tf_op jit(solution)/shard_map/all_to_all | solution.py:98

commit v3 on v2

--- a/solution.py
+++ b/solution.py
@@ -95,8 +95,12 @@
     local_stack = lax.dot_general(
         members, cross_both, (((0,), (0,)), ((), ())), preferred_element_type=jnp.float32
     )
-    gathered = lax.all_to_all(local_stack, "seg", split_axis=0, concat_axis=0, tiled=True)
-    stack = jnp.sum(gathered.reshape(segments, OB_DEV, 2 * local_bins), axis=0)
+    gathered = lax.all_to_all(
+        local_stack.astype(jnp.bfloat16), "seg", split_axis=0, concat_axis=0, tiled=True
+    )
+    stack = jnp.sum(
+        gathered.reshape(segments, OB_DEV, 2 * local_bins).astype(jnp.float32), axis=0
+    )
     table = lag_table(band_position * local_bins, local_bins, FREQ, LAGS)
     partial_lags = jnp.dot(
         stack, table.astype(jnp.float32), precision=lax.Precision.HIGHEST

time: 74.8 us -> 72.8 us (0.973)
  waiting for transfers between devices: 22.8 us -> 20.7 us
    all_to_all x1, waiting for transfers between devices: 10.1 us -> 8.02 us  [per_device(): lax.all_to_all(local_stack.astype(jnp.bfloat16), 'seg', split_axis=0, con...]
where the time goes in v3:
time: 72.8 us; the launch traced here: 72.5 us
  starting transfers between devices  25 us (34%)
  waiting for transfers between devices  20.7 us (28%)
  matrix products  11.9 us (16%)
  blocking collectives  9.08 us (12%)
  other arithmetic  4.19 us (6%)
  local copies, waits for them, and re-layouts  1.43 us (2%)
    all_to_all x1, starting transfers between devices, per_device(): lax.all_to_all(local_stack.astype(jnp.bfloat16), 'seg', split_axis=0, con...  11.1 us
    ppermute x2, starting transfers between devices, extended(): lax.ppermute(lax.slice_in_dim(block, block.shape[dim] - width, None, axis...  10.7 us
    all_to_all x1, blocking collectives, per_device(): lax.all_to_all(partial_lags, 'band', split_axis=1, concat_axis=0, tiled=T...  9.08 us
    ppermute x2, waiting for transfers between devices, extended(): lax.ppermute(lax.slice_in_dim(block, 0, width, axis=dim), axis, backward)  9.08 us
    dot_general x2, matrix products, select_rows(): return jnp.dot(chosen, table, preferred_element_type=jnp.float32)  8.28 us
    all_to_all x1, waiting for transfers between devices, per_device(): lax.all_to_all(local_stack.astype(jnp.bfloat16), 'seg', split_axis=0, con...  8.02 us
    ppermute x2, waiting for transfers between devices, extended(): lax.ppermute(lax.slice_in_dim(block, block.shape[dim] - width, None, axis...  3.58 us
    another operation x2, other arithmetic  3.37 us
  transfers between devices with their start and end apart: 5, of which 4 were waited for; matrix products, arithmetic and copies ran while one was open for 8% of the time, Pallas kernels for 0%

profile of v3, /device:TPU:1, one launch (start us, length us, event | category | flops | bytes accessed | tf_op | source)
XLA Modules:
  0.0 72.5 jit_solution(17727539851796073026)
XLA Ops:
  0.0 0.0 copy-start.1
  0.0 0.0 copy-start
  0.0 1.1 %fusion.61 = (bf16[1,1024,128]{2,1,0:T(8,128)(2,1)S(1)}, bf16[1,1024,128]{2,1,0:T(8,128)(2,1)S(1)}) fusion(bf16[2,1024,128]{2,1,0:T(8,128)(2,1)} %param.4), kind=kLoop, calls=%fused_computation.81 | loop fusion | bytes 1048576 | tf_op jit(solution)/shard_map/slice | solution.py:72
  1.1 0.1 copy.7
  1.2 0.1 copy.8
  1.4 0.1 fusion.33
  1.5 4.4 %collective-permute-start = (f32[1024,64]{0,1:T(8,128)S(1)}, f32[1024,64]{0,1:T(8,128)S(1)}, u32[]{:S(2)}, u32[]{:S(2)}) collective-permute-start(f32[1024,64]{0,1:T(8,128)S(1)} %get-tuple-element.11), channel_id=1, source_target_pairs={{0,1},{1,2},{2,3},{3,4},{4,5},{5,6},{6,7},{8,9},{9,10},{10,11},{11... | collective-permute-start | bytes 786440 | tf_op jit(solution)/shard_map/ppermute | solution.py:23
  5.9 1.3 %collective-permute-start.1 = (f32[1024,64]{0,1:T(8,128)S(1)}, f32[1024,64]{0,1:T(8,128)S(1)}, u32[]{:S(2)}, u32[]{:S(2)}) collective-permute-start(f32[1024,64]{0,1:T(8,128)S(1)} %get-tuple-element.12), channel_id=1, source_target_pairs={{1,0},{2,1},{3,2},{4,3},{5,4},{6,5},{7,6},{9,8},{10,9},{11,10},{12... | collective-permute-start | bytes 786440 | tf_op jit(solution)/shard_map/ppermute | solution.py:26
  7.3 0.0 copy-done.1
  7.3 0.0 copy-done
  7.3 3.6 %collective-permute-done = f32[1024,64]{0,1:T(8,128)S(1)} collective-permute-done((f32[1024,64]{0,1:T(8,128)S(1)}, f32[1024,64]{0,1:T(8,128)S(1)}, u32[]{:S(2)}, u32[]{:S(2)}) %collective-permute-start) | collective-permute-done | bytes 262176 | tf_op jit(solution)/shard_map/ppermute | solution.py:23
  10.9 7.2 %collective-permute-done.1 = f32[1024,64]{0,1:T(8,128)S(1)} collective-permute-done((f32[1024,64]{0,1:T(8,128)S(1)}, f32[1024,64]{0,1:T(8,128)S(1)}, u32[]{:S(2)}, u32[]{:S(2)}) %collective-permute-start.1) | collective-permute-done | bytes 262176 | tf_op jit(solution)/shard_map/ppermute | solution.py:26
  18.1 0.3 fusion.41
  18.4 0.3 fusion.39
  18.7 0.4 fusion.34
  19.1 6.3 %collective-permute-start.2 = (bf16[256,256]{0,1:T(8,128)(2,1)S(1)}, bf16[256,256]{0,1:T(8,128)(2,1)S(1)}, u32[]{:S(2)}, u32[]{:S(2)}) collective-permute-start(bf16[256,256]{0,1:T(8,128)(2,1)S(1)} %get-tuple-element.7), channel_id=1, source_target_pairs={{0,8},{8,16},{16,24},{24,32},{32,40},{40,48},{48,56},{56,64},{64,7... | collective-permute-start | bytes 393224 | tf_op jit(solution)/shard_map/ppermute | solution.py:23
  25.5 1.9 %collective-permute-start.3 = (bf16[256,256]{0,1:T(8,128)(2,1)S(1)}, bf16[256,256]{0,1:T(8,128)(2,1)S(1)}, u32[]{:S(2)}, u32[]{:S(2)}) collective-permute-start(bf16[256,256]{0,1:T(8,128)(2,1)S(1)} %get-tuple-element.8), channel_id=1, source_target_pairs={{8,0},{16,8},{24,16},{32,24},{40,32},{48,40},{56,48},{64,56},{72,6... | collective-permute-start | bytes 393224 | tf_op jit(solution)/shard_map/ppermute | solution.py:26
  27.4 3.4 %fusion.1 = f32[4096,256]{0,1:T(8,128)S(1)} fusion(s32[4096]{0:T(1024)S(1)} %get-tuple-element.18, bf16[1024,128]{0,1:T(8,128)(2,1)S(1)} %get-tuple-element.10, bf16[1024,128]{0,1:T(8,128)(2,1)S(1)} %get-tuple-element.9), kind=kOutput, calls=%fused_computation.3 | convolution fusion | flops 2152726528 | bytes 4734976 | tf_op jit(solution)/shard_map/dot_general | solution.py:52
  30.8 0.0 collective-permute-done.2
  30.8 1.9 %collective-permute-done.3 = bf16[256,256]{0,1:T(8,128)(2,1)S(1)} collective-permute-done((bf16[256,256]{0,1:T(8,128)(2,1)S(1)}, bf16[256,256]{0,1:T(8,128)(2,1)S(1)}, u32[]{:S(2)}, u32[]{:S(2)}) %collective-permute-start.3) | collective-permute-done | bytes 131104 | tf_op jit(solution)/shard_map/ppermute | solution.py:26
  32.7 4.9 %fusion = f32[4096,256]{0,1:T(8,128)S(1)} fusion(s32[4096]{0:T(1024)S(1)} %get-tuple-element.17, bf16[256,256]{0,1:T(8,128)(2,1)S(1)} %collective-permute-done.3, bf16[1024,128]{0,1:T(8,128)(2,1)S(1)} %get-tuple-element.10, bf16[1024,128]{0,1:T(8,128)(2,1)S(1)} %get-tuple-element.9, bf16[256,256]{0,1:T(8,128)(2,1)S(1)} %collective-permute-done.2), kind=kOutput, calls=%fused_computation.1 | convolution fusion | flops 3230662656 | bytes 4997120 | tf_op jit(solution)/shard_map/dot_general | solution.py:52
  37.6 0.0 copy-start.2
  37.6 0.8 %add_convert_fusion = (bf16[4096,128]{0,1:T(8,128)(2,1)S(1)}, bf16[4096,128]{0,1:T(8,128)(2,1)S(1)}) fusion(f32[4096,256]{0,1:T(8,128)S(1)} %fusion, f32[4096,256]{0,1:T(8,128)S(1)} %fusion.1), kind=kLoop, calls=%fused_computation.13 | loop fusion | flops 4194304 | bytes 10485760 | tf_op jit(solution)/shard_map/convert.4
  38.5 0.0 copy-done.2
  38.5 2.1 %fusion.20 = bf16[32,8,256]{2,1,0:T(8,128)(2,1)} fusion(bf16[4096,128]{0,1:T(8,128)(2,1)S(1)} %get-tuple-element.6, bf16[4096,128]{0,1:T(8,128)(2,1)S(1)} %get-tuple-element.5, s32[4096]{0:T(1024)S(1)} %copy-done.2), kind=kOutput, calls=%fused_computation.25 | convolution fusion | flops 543227904 | bytes 2244608 | tf_op jit(solution)/shard_map/dot_general | solution.py:95
  40.5 11.1 %all-to-all-start = ((bf16[32,8,256]{2,1,0:T(8,128)(2,1)}), bf16[32,8,256]{2,1,0:T(8,128)(2,1)S(1)}, u32[]{:S(2)}, u32[]{:S(2)}) async-start(bf16[32,8,256]{2,1,0:T(8,128)(2,1)} %fusion.20), calls=%async_computation | async-start | bytes 262144 | tf_op jit(solution)/shard_map/all_to_all | solution.py:98
  51.6 2.5 %multiply_convert_fusion.1 = (bf16[128,1024]{0,1:T(8,128)(2,1)S(1)}, bf16[128,1024]{0,1:T(8,128)(2,1)S(1)}) fusion(s32[1024]{0:T(1024)S(1)} %iota_add_fusion, s32[128]{0:T(128)S(1)} %iota_add_fusion.1), kind=kLoop, calls=%fused_computation.57 | loop fusion | flops 2490368 | bytes 528896 | tf_op jit(solution)/shard_map/convert.2
  54.2 0.1 pad_maximum_fusion.1
  54.2 8.0 %all-to-all-done = bf16[32,8,256]{2,1,0:T(8,128)(2,1)S(1)} async-done(((bf16[32,8,256]{2,1,0:T(8,128)(2,1)}), bf16[32,8,256]{2,1,0:T(8,128)(2,1)S(1)}, u32[]{:S(2)}, u32[]{:S(2)}) %all-to-all-start) | async-done | bytes 131104 | tf_op jit(solution)/shard_map/all_to_all | solution.py:98
  62.3 0.5 fusion.52
  62.8 9.1 %all_to_all.19 = f32[8,8,128]{2,0,1:T(8,128)S(1)} all-to-all(f32[8,8,128]{2,0,1:T(8,128)S(1)} %fusion.52), channel_id=1, replica_groups=mesh['seg'=32,'band'=8] {'band'}, dimensions={1} | all-to-all | bytes 65536 | tf_op jit(solution)/shard_map/all_to_all | solution.py:108
  71.9 0.6 reduce_sum.19
  (7 shorter events, 0.1 us)
Async XLA Ops:
  0.0 7.3 %copy-start.1 = (s32[4096]{0:T(1024)S(1)}, s32[4096]{0:T(1024)}, u32[]{:S(2)}) copy-start(s32[4096]{0:T(1024)} %param.5) | copy-start | bytes 49156
  0.0 7.3 %copy-start = (s32[4096]{0:T(1024)S(1)}, s32[4096]{0:T(1024)}, u32[]{:S(2)}) copy-start(s32[4096]{0:T(1024)} %param.6) | copy-start | bytes 49156
  1.5 9.3 %collective-permute-start = (f32[1024,64]{0,1:T(8,128)S(1)}, f32[1024,64]{0,1:T(8,128)S(1)}, u32[]{:S(2)}, u32[]{:S(2)}) collective-permute-start(f32[1024,64]{0,1:T(8,128)S(1)} %get-tuple-element.11), channel_id=1, source_target_pairs={{0,1},{1,2},{2,3},{3,4},{4,5},{5,6},{6,7},{8,9},{9,10},{10,11},{11... | collective-permute-start | bytes 786440 | tf_op jit(solution)/shard_map/ppermute | solution.py:23
  5.9 12.1 %collective-permute-start.1 = (f32[1024,64]{0,1:T(8,128)S(1)}, f32[1024,64]{0,1:T(8,128)S(1)}, u32[]{:S(2)}, u32[]{:S(2)}) collective-permute-start(f32[1024,64]{0,1:T(8,128)S(1)} %get-tuple-element.12), channel_id=1, source_target_pairs={{1,0},{2,1},{3,2},{4,3},{5,4},{6,5},{7,6},{9,8},{10,9},{11,10},{12... | collective-permute-start | bytes 786440 | tf_op jit(solution)/shard_map/ppermute | solution.py:26
  19.1 11.6 %collective-permute-start.2 = (bf16[256,256]{0,1:T(8,128)(2,1)S(1)}, bf16[256,256]{0,1:T(8,128)(2,1)S(1)}, u32[]{:S(2)}, u32[]{:S(2)}) collective-permute-start(bf16[256,256]{0,1:T(8,128)(2,1)S(1)} %get-tuple-element.7), channel_id=1, source_target_pairs={{0,8},{8,16},{16,24},{24,32},{32,40},{40,48},{48,56},{56,64},{64,7... | collective-permute-start | bytes 393224 | tf_op jit(solution)/shard_map/ppermute | solution.py:23
  25.5 7.2 %collective-permute-start.3 = (bf16[256,256]{0,1:T(8,128)(2,1)S(1)}, bf16[256,256]{0,1:T(8,128)(2,1)S(1)}, u32[]{:S(2)}, u32[]{:S(2)}) collective-permute-start(bf16[256,256]{0,1:T(8,128)(2,1)S(1)} %get-tuple-element.8), channel_id=1, source_target_pairs={{8,0},{16,8},{24,16},{32,24},{40,32},{48,40},{56,48},{64,56},{72,6... | collective-permute-start | bytes 393224 | tf_op jit(solution)/shard_map/ppermute | solution.py:26
  37.6 0.9 %copy-start.2 = (s32[4096]{0:T(1024)S(1)}, s32[4096]{0:T(1024)}, u32[]{:S(2)}) copy-start(s32[4096]{0:T(1024)} %param.7) | copy-start | bytes 49156
  40.5 21.7 %all-to-all-start = ((bf16[32,8,256]{2,1,0:T(8,128)(2,1)}), bf16[32,8,256]{2,1,0:T(8,128)(2,1)S(1)}, u32[]{:S(2)}, u32[]{:S(2)}) async-start(bf16[32,8,256]{2,1,0:T(8,128)(2,1)} %fusion.20), calls=%async_computation | async-start | bytes 262144 | tf_op jit(solution)/shard_map/all_to_all | solution.py:98

commit v4 on v2

--- a/solution.py
+++ b/solution.py
@@ -26,6 +26,15 @@
         high = lax.ppermute(lax.slice_in_dim(block, 0, width, axis=dim), axis, backward)
         block = jnp.concatenate([low, block, high], axis=dim)
     return block
+
+
+def halos(block, axis, width):
+    count = lax.axis_size(axis)
+    forward = [(i, i + 1) for i in range(count - 1)]
+    backward = [(target, source) for source, target in forward]
+    low = lax.ppermute(block[block.shape[0] - width :], axis, forward)
+    high = lax.ppermute(block[:width], axis, backward)
+    return low, high
 
 
 def window_matrix(local_bins, half_width):
@@ -79,8 +88,11 @@
         jnp.bfloat16
     )
     first_rows = select_rows(whitened, pair_first - seg_position * channels)
-    near_rows = extended(whitened, (("seg", 0),), REACH)
-    second_rows = select_rows(near_rows, pair_second - seg_position * channels + REACH)
+    low_rows, high_rows = halos(whitened, "seg", REACH)
+    second_local = pair_second - seg_position * channels
+    second_rows = select_rows(whitened, second_local)
+    second_rows = second_rows + select_rows(low_rows, second_local + REACH)
+    second_rows = second_rows + select_rows(high_rows, second_local - channels)
     first_real = first_rows[:, :local_bins]
     first_imag = first_rows[:, local_bins:]
     second_real = second_rows[:, :local_bins]

time: 74.8 us -> 81.3 us (1.087)
  matrix products: 12 us -> 18.1 us
  waiting for transfers between devices: 22.8 us -> 21.5 us
  starting transfers between devices: 25 us -> 25.9 us
    ppermute x0 -> x2, starting transfers between devices: none -> 8.22 us  [the longest x1 6.3 us: halos(): low = lax.ppermute(block[block.shape[0] - width:], axis, forward)]
    ppermute x2 -> x1, starting transfers between devices: 10.7 us -> 4.38 us  [extended(): lax.ppermute(lax.slice_in_dim(block, block.shape[dim] - width, None, axis...]
    dot_general x2 -> x4, matrix products: 8.28 us -> 14.5 us  [select_rows(): return jnp.dot(chosen, table, preferred_element_type=jnp.float32)]
    ppermute x2 -> x1, starting transfers between devices: 3.21 us -> 1.29 us  [extended(): lax.ppermute(lax.slice_in_dim(block, 0, width, axis=dim), axis, backward)]
    ppermute x2 -> x1, waiting for transfers between devices: 9.08 us -> 7.19 us  [extended(): lax.ppermute(lax.slice_in_dim(block, 0, width, axis=dim), axis, backward)]
    all_to_all x1, starting transfers between devices: 11.1 us -> 12 us  [per_device(): lax.all_to_all(local_stack, 'seg', split_axis=0, concat_axis=0, tiled=True)]
    ppermute x2 -> x1, waiting for transfers between devices: 3.61 us -> 3.57 us  [extended(): lax.ppermute(lax.slice_in_dim(block, block.shape[dim] - width, None, axis...]
  transfers between devices with their start and end apart: 5 -> 5, of which waited for: 4 -> 3; matrix products, arithmetic and copies ran while one was open for 8% -> 12% of each run, Pallas kernels for 0% -> 0%
where the time goes in v4:
time: 81.3 us; the launch traced here: 81 us
  starting transfers between devices  25.9 us (32%)
  waiting for transfers between devices  21.5 us (26%)
  matrix products  18.1 us (22%)
  blocking collectives  9.52 us (12%)
  other arithmetic  4.2 us (5%)
  local copies, waits for them, and re-layouts  1.43 us (2%)
    dot_general x4, matrix products, select_rows(): return jnp.dot(chosen, table, preferred_element_type=jnp.float32)  14.5 us
    all_to_all x1, starting transfers between devices, per_device(): lax.all_to_all(local_stack, 'seg', split_axis=0, concat_axis=0, tiled=True)  12 us
    all_to_all x1, waiting for transfers between devices, per_device(): lax.all_to_all(local_stack, 'seg', split_axis=0, concat_axis=0, tiled=True)  10.8 us
    all_to_all x1, blocking collectives, per_device(): lax.all_to_all(partial_lags, 'band', split_axis=1, concat_axis=0, tiled=T...  9.52 us
    ppermute x1, waiting for transfers between devices, extended(): lax.ppermute(lax.slice_in_dim(block, 0, width, axis=dim), axis, backward)  7.19 us
    ppermute x1, starting transfers between devices, halos(): low = lax.ppermute(block[block.shape[0] - width:], axis, forward)  6.3 us
    ppermute x1, starting transfers between devices, extended(): lax.ppermute(lax.slice_in_dim(block, block.shape[dim] - width, None, axis...  4.38 us
    ppermute x1, waiting for transfers between devices, extended(): lax.ppermute(lax.slice_in_dim(block, block.shape[dim] - width, None, axis...  3.57 us
  transfers between devices with their start and end apart: 5, of which 3 were waited for; matrix products, arithmetic and copies ran while one was open for 12% of the time, Pallas kernels for 0%

profile of v4, /device:TPU:1, one launch (start us, length us, event | category | flops | bytes accessed | tf_op | source)
XLA Modules:
  0.0 81.0 jit_solution(17991750741492988329)
XLA Ops:
  0.0 0.0 copy-start
  0.0 0.0 copy-start.1
  0.0 1.1 %fusion.48 = (bf16[1,1024,128]{2,1,0:T(8,128)(2,1)S(1)}, bf16[1,1024,128]{2,1,0:T(8,128)(2,1)S(1)}) fusion(bf16[2,1024,128]{2,1,0:T(8,128)(2,1)} %param.4), kind=kLoop, calls=%fused_computation.78 | loop fusion | bytes 1048576 | tf_op jit(solution)/shard_map/slice | solution.py:81
  1.1 0.1 copy.7
  1.2 0.1 copy.8
  1.4 0.1 fusion.23
  1.5 4.4 %collective-permute-start = (f32[1024,64]{0,1:T(8,128)S(1)}, f32[1024,64]{0,1:T(8,128)S(1)}, u32[]{:S(2)}, u32[]{:S(2)}) collective-permute-start(f32[1024,64]{0,1:T(8,128)S(1)} %get-tuple-element.13), channel_id=1, source_target_pairs={{0,1},{1,2},{2,3},{3,4},{4,5},{5,6},{6,7},{8,9},{9,10},{10,11},{11... | collective-permute-start | bytes 786440 | tf_op jit(solution)/shard_map/ppermute | solution.py:23
  5.9 1.3 %collective-permute-start.1 = (f32[1024,64]{0,1:T(8,128)S(1)}, f32[1024,64]{0,1:T(8,128)S(1)}, u32[]{:S(2)}, u32[]{:S(2)}) collective-permute-start(f32[1024,64]{0,1:T(8,128)S(1)} %get-tuple-element.14), channel_id=1, source_target_pairs={{1,0},{2,1},{3,2},{4,3},{5,4},{6,5},{7,6},{9,8},{10,9},{11,10},{12... | collective-permute-start | bytes 786440 | tf_op jit(solution)/shard_map/ppermute | solution.py:26
  7.2 0.0 copy-done
  7.3 0.0 copy-done.1
  7.3 3.6 %collective-permute-done = f32[1024,64]{0,1:T(8,128)S(1)} collective-permute-done((f32[1024,64]{0,1:T(8,128)S(1)}, f32[1024,64]{0,1:T(8,128)S(1)}, u32[]{:S(2)}, u32[]{:S(2)}) %collective-permute-start) | collective-permute-done | bytes 262176 | tf_op jit(solution)/shard_map/ppermute | solution.py:23
  10.9 7.2 %collective-permute-done.1 = f32[1024,64]{0,1:T(8,128)S(1)} collective-permute-done((f32[1024,64]{0,1:T(8,128)S(1)}, f32[1024,64]{0,1:T(8,128)S(1)}, u32[]{:S(2)}, u32[]{:S(2)}) %collective-permute-start.1) | collective-permute-done | bytes 262176 | tf_op jit(solution)/shard_map/ppermute | solution.py:26
  18.1 0.3 fusion.31
  18.4 0.3 fusion.29
  18.7 0.4 fusion.24
  19.1 3.4 %fusion.1 = f32[4096,256]{0,1:T(8,128)S(1)} fusion(s32[4096]{0:T(1024)S(1)} %get-tuple-element.6, bf16[1024,128]{0,1:T(8,128)(2,1)S(1)} %get-tuple-element.12, bf16[1024,128]{0,1:T(8,128)(2,1)S(1)} %get-tuple-element.11), kind=kOutput, calls=%fused_computation.3 | convolution fusion | flops 2152726528 | bytes 4734976 | tf_op jit(solution)/shard_map/dot_general | solution.py:61
  22.5 6.3 %collective-permute-start.2 = (bf16[256,256]{0,1:T(8,128)(2,1)S(1)}, bf16[256,256]{0,1:T(8,128)(2,1)S(1)}, u32[]{:S(2)}, u32[]{:S(2)}) collective-permute-start(bf16[256,256]{0,1:T(8,128)(2,1)S(1)} %get-tuple-element.10), channel_id=1, source_target_pairs={{0,8},{8,16},{16,24},{24,32},{32,40},{40,48},{48,56},{56,64},{64,7... | collective-permute-start | bytes 393224 | tf_op jit(solution)/shard_map/ppermute | solution.py:35
  28.8 1.9 %collective-permute-start.3 = (bf16[256,256]{0,1:T(8,128)(2,1)S(1)}, bf16[256,256]{0,1:T(8,128)(2,1)S(1)}, u32[]{:S(2)}, u32[]{:S(2)}) collective-permute-start(bf16[256,256]{0,1:T(8,128)(2,1)S(1)} %get-tuple-element.9), channel_id=1, source_target_pairs={{8,0},{16,8},{24,16},{32,24},{40,32},{48,40},{56,48},{64,56},{72,6... | collective-permute-start | bytes 393224 | tf_op jit(solution)/shard_map/ppermute | solution.py:36
  30.7 3.4 %fusion = f32[4096,256]{0,1:T(8,128)S(1)} fusion(s32[4096]{0:T(1024)S(1)} %broadcast_subtract_fusion.1, bf16[1024,128]{0,1:T(8,128)(2,1)S(1)} %get-tuple-element.12, bf16[1024,128]{0,1:T(8,128)(2,1)S(1)} %get-tuple-element.11), kind=kOutput, calls=%fused_computation.2 | convolution fusion | flops 2152726528 | bytes 4734976 | tf_op jit(solution)/shard_map/dot_general | solution.py:61
  34.1 0.0 collective-permute-done.2
  34.1 3.9 %convolution_add_fusion.1 = f32[4096,256]{0,1:T(8,128)S(1)} fusion(f32[4096,256]{0,1:T(8,128)S(1)} %fusion.1, bf16[256,256]{0,1:T(8,128)(2,1)S(1)} %collective-permute-done.2, s32[4096]{0:T(1024)S(1)} %broadcast_add_fusion.1), kind=kOutput, calls=%fused_computation.7 | convolution fusion | flops 538968064 | bytes 8536064 | tf_op jit(solution)/shard_map/dot_general | solution.py:61
  38.0 0.0 collective-permute-done.3
  38.0 3.9 %convolution_add_fusion = f32[4096,256]{0,1:T(8,128)S(1)} fusion(f32[4096,256]{0,1:T(8,128)S(1)} %convolution_add_fusion.1, bf16[256,256]{0,1:T(8,128)(2,1)S(1)} %collective-permute-done.3, s32[4096]{0:T(1024)S(1)} %get-tuple-element.5), kind=kOutput, calls=%fused_computation.6 | convolution fusion | flops 538968064 | bytes 8536064 | tf_op jit(solution)/shard_map/dot_general | solution.py:61
  41.9 0.0 copy-start.2
  41.9 0.8 %add_convert_fusion = (bf16[4096,128]{0,1:T(8,128)(2,1)S(1)}, bf16[4096,128]{0,1:T(8,128)(2,1)S(1)}) fusion(f32[4096,256]{0,1:T(8,128)S(1)} %convolution_add_fusion, f32[4096,256]{0,1:T(8,128)S(1)} %fusion), kind=kLoop, calls=%fused_computation.17 | loop fusion | flops 4194304 | bytes 10485760 | tf_op jit(solution)/shard_map/convert.4
  42.7 0.0 copy-done.2
  42.8 2.2 %fusion.17 = f32[32,8,256]{2,1,0:T(8,128)} fusion(bf16[4096,128]{0,1:T(8,128)(2,1)S(1)} %get-tuple-element.8, bf16[4096,128]{0,1:T(8,128)(2,1)S(1)} %get-tuple-element.7, s32[4096]{0:T(1024)S(1)} %copy-done.2), kind=kOutput, calls=%fused_computation.30 | convolution fusion | flops 543162368 | bytes 2375680 | tf_op jit(solution)/shard_map/dot_general | solution.py:107
  44.9 12.0 %all-to-all-start = ((f32[32,8,256]{2,1,0:T(8,128)}), f32[32,8,256]{2,1,0:T(8,128)S(1)}, u32[]{:S(2)}, u32[]{:S(2)}) async-start(f32[32,8,256]{2,1,0:T(8,128)} %fusion.17), calls=%async_computation | async-start | bytes 524288 | tf_op jit(solution)/shard_map/all_to_all | solution.py:110
  57.0 2.5 %multiply_convert_fusion.1 = (bf16[128,1024]{0,1:T(8,128)(2,1)S(1)}, bf16[128,1024]{0,1:T(8,128)(2,1)S(1)}) fusion(s32[1024]{0:T(1024)S(1)} %iota_add_fusion, s32[128]{0:T(128)S(1)} %iota_add_fusion.1), kind=kLoop, calls=%fused_computation.53 | loop fusion | flops 2490368 | bytes 528896 | tf_op jit(solution)/shard_map/convert.2
  59.5 0.1 pad_maximum_fusion.2
  59.6 10.8 %all-to-all-done = f32[32,8,256]{2,1,0:T(8,128)S(1)} async-done(((f32[32,8,256]{2,1,0:T(8,128)}), f32[32,8,256]{2,1,0:T(8,128)S(1)}, u32[]{:S(2)}, u32[]{:S(2)}) %all-to-all-start) | async-done | bytes 262176 | tf_op jit(solution)/shard_map/all_to_all | solution.py:110
  70.4 0.5 fusion.39
  70.9 9.5 %all_to_all.19 = f32[8,8,128]{2,0,1:T(8,128)S(1)} all-to-all(f32[8,8,128]{2,0,1:T(8,128)S(1)} %fusion.39), channel_id=1, replica_groups=mesh['seg'=32,'band'=8] {'band'}, dimensions={1} | all-to-all | bytes 65536 | tf_op jit(solution)/shard_map/all_to_all | solution.py:116
  80.4 0.6 reduce_sum.19
  (9 shorter events, 0.1 us)
Async XLA Ops:
  0.0 7.2 %copy-start = (s32[4096]{0:T(1024)S(1)}, s32[4096]{0:T(1024)}, u32[]{:S(2)}) copy-start(s32[4096]{0:T(1024)} %param.6) | copy-start | bytes 49156
  0.0 7.3 %copy-start.1 = (s32[4096]{0:T(1024)S(1)}, s32[4096]{0:T(1024)}, u32[]{:S(2)}) copy-start(s32[4096]{0:T(1024)} %param.5) | copy-start | bytes 49156
  1.5 9.3 %collective-permute-start = (f32[1024,64]{0,1:T(8,128)S(1)}, f32[1024,64]{0,1:T(8,128)S(1)}, u32[]{:S(2)}, u32[]{:S(2)}) collective-permute-start(f32[1024,64]{0,1:T(8,128)S(1)} %get-tuple-element.13), channel_id=1, source_target_pairs={{0,1},{1,2},{2,3},{3,4},{4,5},{5,6},{6,7},{8,9},{9,10},{10,11},{11... | collective-permute-start | bytes 786440 | tf_op jit(solution)/shard_map/ppermute | solution.py:23
  5.9 12.1 %collective-permute-start.1 = (f32[1024,64]{0,1:T(8,128)S(1)}, f32[1024,64]{0,1:T(8,128)S(1)}, u32[]{:S(2)}, u32[]{:S(2)}) collective-permute-start(f32[1024,64]{0,1:T(8,128)S(1)} %get-tuple-element.14), channel_id=1, source_target_pairs={{1,0},{2,1},{3,2},{4,3},{5,4},{6,5},{7,6},{9,8},{10,9},{11,10},{12... | collective-permute-start | bytes 786440 | tf_op jit(solution)/shard_map/ppermute | solution.py:26
  22.5 11.6 %collective-permute-start.2 = (bf16[256,256]{0,1:T(8,128)(2,1)S(1)}, bf16[256,256]{0,1:T(8,128)(2,1)S(1)}, u32[]{:S(2)}, u32[]{:S(2)}) collective-permute-start(bf16[256,256]{0,1:T(8,128)(2,1)S(1)} %get-tuple-element.10), channel_id=1, source_target_pairs={{0,8},{8,16},{16,24},{24,32},{32,40},{40,48},{48,56},{56,64},{64,7... | collective-permute-start | bytes 393224 | tf_op jit(solution)/shard_map/ppermute | solution.py:35
  28.8 9.2 %collective-permute-start.3 = (bf16[256,256]{0,1:T(8,128)(2,1)S(1)}, bf16[256,256]{0,1:T(8,128)(2,1)S(1)}, u32[]{:S(2)}, u32[]{:S(2)}) collective-permute-start(bf16[256,256]{0,1:T(8,128)(2,1)S(1)} %get-tuple-element.9), channel_id=1, source_target_pairs={{8,0},{16,8},{24,16},{32,24},{40,32},{48,40},{56,48},{64,56},{72,6... | collective-permute-start | bytes 393224 | tf_op jit(solution)/shard_map/ppermute | solution.py:36
  41.9 0.9 %copy-start.2 = (s32[4096]{0:T(1024)S(1)}, s32[4096]{0:T(1024)}, u32[]{:S(2)}) copy-start(s32[4096]{0:T(1024)} %param.7) | copy-start | bytes 49156
  44.9 25.4 %all-to-all-start = ((f32[32,8,256]{2,1,0:T(8,128)}), f32[32,8,256]{2,1,0:T(8,128)S(1)}, u32[]{:S(2)}, u32[]{:S(2)}) async-start(f32[32,8,256]{2,1,0:T(8,128)} %fusion.17), calls=%async_computation | async-start | bytes 524288 | tf_op jit(solution)/shard_map/all_to_all | solution.py:110

commit v5 on v2

--- a/solution.py
+++ b/solution.py
@@ -62,6 +62,25 @@
     return jnp.concatenate([cosine, negsine], axis=0).astype(jnp.bfloat16)
 
 
+def shifted(block, axes, steps):
+    sizes = [lax.axis_size(axis) for axis in axes]
+    pairs = []
+    for source in range(math.prod(sizes)):
+        coords = []
+        rest = source
+        for size in reversed(sizes):
+            coords.append(rest % size)
+            rest //= size
+        coords = coords[::-1]
+        target = [c + d for c, d in zip(coords, steps)]
+        if all(0 <= t < size for t, size in zip(target, sizes)):
+            flat = 0
+            for t, size in zip(target, sizes):
+                flat = flat * size + t
+            pairs.append((source, flat))
+    return lax.ppermute(block, axes if len(axes) > 1 else axes[0], pairs)
+
+
 def per_device(spectra, pair_first, pair_second, pair_bin):
     seg_position = lax.axis_index("seg")
     band_position = lax.axis_index("band")
@@ -69,17 +88,35 @@
     bands = lax.axis_size("band")
     channels = spectra.shape[1]
     local_bins = spectra.shape[2]
-    real_part = spectra[0].astype(jnp.float32)
-    imag_part = spectra[1].astype(jnp.float32)
+    both = ("seg", "band")
+    low_spectra = shifted(spectra[:, channels - REACH :], ("seg",), (1,))
+    high_spectra = shifted(spectra[:, :REACH], ("seg",), (-1,))
+    near_spectra = jnp.concatenate([low_spectra, spectra, high_spectra], axis=1).astype(jnp.float32)
+    real_part = near_spectra[0]
+    imag_part = near_spectra[1]
+    own = spectra.astype(jnp.float32)
+    own_power = own[0] * own[0] + own[1] * own[1]
+    left = shifted(own_power[:, local_bins - HALF_WIN :], ("band",), (1,))
+    right = shifted(own_power[:, :HALF_WIN], ("band",), (-1,))
+    corner_ll = shifted(own_power[channels - REACH :, local_bins - HALF_WIN :], both, (1, 1))
+    corner_lr = shifted(own_power[channels - REACH :, :HALF_WIN], both, (1, -1))
+    corner_hl = shifted(own_power[:REACH, local_bins - HALF_WIN :], both, (-1, 1))
+    corner_hr = shifted(own_power[:REACH, :HALF_WIN], both, (-1, -1))
     power_sum = real_part * real_part + imag_part * imag_part
-    padded_power = extended(power_sum, (("band", 1),), HALF_WIN)
+    padded_power = jnp.concatenate(
+        [
+            jnp.concatenate([corner_ll, left, corner_hl], axis=0),
+            power_sum,
+            jnp.concatenate([corner_lr, right, corner_hr], axis=0),
+        ],
+        axis=1,
+    )
     window_sum = exact_dot(padded_power, window_matrix(local_bins, HALF_WIN))
     scaling = lax.rsqrt(window_sum / (2 * HALF_WIN + 1) + epsilon)
-    whitened = jnp.concatenate([real_part * scaling, imag_part * scaling], axis=1).astype(
+    near_rows = jnp.concatenate([real_part * scaling, imag_part * scaling], axis=1).astype(
         jnp.bfloat16
     )
-    first_rows = select_rows(whitened, pair_first - seg_position * channels)
-    near_rows = extended(whitened, (("seg", 0),), REACH)
+    first_rows = select_rows(near_rows[REACH : REACH + channels], pair_first - seg_position * channels)
     second_rows = select_rows(near_rows, pair_second - seg_position * channels + REACH)
     first_real = first_rows[:, :local_bins]
     first_imag = first_rows[:, local_bins:]

time: 74.8 us -> 91.3 us (1.22)
  starting transfers between devices: 25 us -> 38.5 us
  blocking collectives: 8.82 us -> 10.3 us
    ppermute x4 -> x8, starting transfers between devices: 13.9 us -> 24.7 us  [shifted(): return lax.ppermute(block, axes if len(axes) > 1 else axes[0], pairs)]
    all_to_all x1, starting transfers between devices: 11.1 us -> 13.8 us  [per_device(): lax.all_to_all(local_stack, 'seg', split_axis=0, concat_axis=0, tiled=True)]
    all_to_all x1, blocking collectives: 8.82 us -> 10.3 us  [per_device(): lax.all_to_all(partial_lags, 'band', split_axis=1, concat_axis=0, tiled=T...]
    slice x2 -> x3, local copies, waits for them, and re-layouts: 1.12 us -> 0.08 us  [the longest x1 0.04 us: per_device(): left = shifted(own_power[:, local_bins - HALF_WIN:], ('band',), (1,))]
    unnamed x8 -> x7, local copies, waits for them, and re-layouts: 0.3 us -> 1.26 us
    ppermute x4 -> x8, waiting for transfers between devices: 12.7 us -> 12.6 us  [shifted(): return lax.ppermute(block, axes if len(axes) > 1 else axes[0], pairs)]
  transfers between devices with their start and end apart: 5 -> 9, of which waited for: 4 -> 4; matrix products, arithmetic and copies ran while one was open for 8% -> 3% of each run, Pallas kernels for 0% -> 0%
where the time goes in v5:
time: 91.3 us; the launch traced here: 90.8 us
  starting transfers between devices  38.5 us (42%)
  waiting for transfers between devices  23.4 us (26%)
  matrix products  12.4 us (14%)
  blocking collectives  10.3 us (11%)
  other arithmetic  4.53 us (5%)
  local copies, waits for them, and re-layouts  1.34 us (1%)
    ppermute x8, starting transfers between devices, shifted(): return lax.ppermute(block, axes if len(axes) > 1 else axes[0], pairs)  24.7 us
    all_to_all x1, starting transfers between devices, per_device(): lax.all_to_all(local_stack, 'seg', split_axis=0, concat_axis=0, tiled=True)  13.8 us
    ppermute x8, waiting for transfers between devices, shifted(): return lax.ppermute(block, axes if len(axes) > 1 else axes[0], pairs)  12.6 us
    all_to_all x1, waiting for transfers between devices, per_device(): lax.all_to_all(local_stack, 'seg', split_axis=0, concat_axis=0, tiled=True)  10.9 us
    all_to_all x1, blocking collectives, per_device(): lax.all_to_all(partial_lags, 'band', split_axis=1, concat_axis=0, tiled=T...  10.3 us
    dot_general x2, matrix products, select_rows(): return jnp.dot(chosen, table, preferred_element_type=jnp.float32)  8.63 us
    another operation x2, other arithmetic  3.37 us
    dot_general x1, matrix products, per_device(): lax.dot_general(members, cross_both, (((0,), (0,)), ((), ())), preferred_...  2.15 us
  transfers between devices with their start and end apart: 9, of which 4 were waited for; matrix products, arithmetic and copies ran while one was open for 3% of the time, Pallas kernels for 0%

profile of v5, /device:TPU:1, one launch (start us, length us, event | category | flops | bytes accessed | tf_op | source)
XLA Modules:
  0.0 90.8 jit_solution(8696754515662363298)
XLA Ops:
  0.0 1.2 %copy.5 = bf16[2,1024,128]{1,2,0:T(8,128)(2,1)S(1)} copy(bf16[2,1024,128]{2,1,0:T(8,128)(2,1)} %param.4) | data formatting | bytes 1048576 | tf_op args[0]
  1.3 6.3 %collective-permute-start = (bf16[2,256,128]{1,2,0:T(8,128)(2,1)S(1)}, bf16[2,256,128]{1,2,0:T(8,128)(2,1)S(1)}, u32[]{:S(2)}, u32[]{:S(2)}) collective-permute-start(bf16[2,256,128]{1,2,0:T(8,128)(2,1)S(1)} %get-tuple-element.15), channel_id=1, source_target_pairs={{0,8},{8,16},{16,24},{24,32},{32,40},{40,48},{48,56},{56,64},{64,7... | collective-permute-start | bytes 393224 | tf_op jit(solution)/shard_map/ppermute | solution.py:81
  7.6 1.9 %collective-permute-start.1 = (bf16[2,256,128]{1,2,0:T(8,128)(2,1)S(1)}, bf16[2,256,128]{1,2,0:T(8,128)(2,1)S(1)}, u32[]{:S(2)}, u32[]{:S(2)}) collective-permute-start(bf16[2,256,128]{1,2,0:T(8,128)(2,1)S(1)} %get-tuple-element.16), channel_id=1, source_target_pairs={{8,0},{16,8},{24,16},{32,24},{40,32},{48,40},{56,48},{64,56},{72,6... | collective-permute-start | bytes 393224 | tf_op jit(solution)/shard_map/ppermute | solution.py:81
  9.5 0.1 convert_element_type.13
  9.6 0.0 copy-start
  9.6 0.0 copy-start.1
  9.6 0.1 fusion.32
  9.7 5.9 %collective-permute-start.2 = (f32[256,64]{0,1:T(8,128)S(1)}, f32[256,64]{0,1:T(8,128)S(1)}, u32[]{:S(2)}, u32[]{:S(2)}) collective-permute-start(f32[256,64]{0,1:T(8,128)S(1)} %get-tuple-element.9), channel_id=1, source_target_pairs={{0,9},{1,10},{2,11},{3,12},{4,13},{5,14},{6,15},{8,17},{9,18},{10,... | collective-permute-start | bytes 196616 | tf_op jit(solution)/shard_map/ppermute | solution.py:81
  15.6 1.3 %collective-permute-start.4 = (f32[256,64]{0,1:T(8,128)S(1)}, f32[256,64]{0,1:T(8,128)S(1)}, u32[]{:S(2)}, u32[]{:S(2)}) collective-permute-start(f32[256,64]{0,1:T(8,128)S(1)} %get-tuple-element.12), channel_id=1, source_target_pairs={{8,1},{9,2},{10,3},{11,4},{12,5},{13,6},{14,7},{16,9},{17,10},{18,... | collective-permute-start | bytes 196616 | tf_op jit(solution)/shard_map/ppermute | solution.py:81
  16.9 1.3 %collective-permute-start.5 = (f32[256,64]{0,1:T(8,128)S(1)}, f32[256,64]{0,1:T(8,128)S(1)}, u32[]{:S(2)}, u32[]{:S(2)}) collective-permute-start(f32[256,64]{0,1:T(8,128)S(1)} %get-tuple-element.11), channel_id=1, source_target_pairs={{1,8},{2,9},{3,10},{4,11},{5,12},{6,13},{7,14},{9,16},{10,17},{11,... | collective-permute-start | bytes 196616 | tf_op jit(solution)/shard_map/ppermute | solution.py:81
  18.3 0.0 copy-done
  18.3 0.0 copy-done.1
  18.3 0.0 collective-permute-done
  18.4 1.3 %collective-permute-start.7 = (f32[256,64]{0,1:T(8,128)S(1)}, f32[256,64]{0,1:T(8,128)S(1)}, u32[]{:S(2)}, u32[]{:S(2)}) collective-permute-start(f32[256,64]{0,1:T(8,128)S(1)} %get-tuple-element.10), channel_id=1, source_target_pairs={{9,0},{10,1},{11,2},{12,3},{13,4},{14,5},{15,6},{17,8},{18,9},{19,... | collective-permute-start | bytes 196616 | tf_op jit(solution)/shard_map/ppermute | solution.py:81
  19.7 0.0 collective-permute-done.1
  19.7 5.5 %collective-permute-start.3 = (f32[1024,64]{0,1:T(8,128)S(1)}, f32[1024,64]{0,1:T(8,128)S(1)}, u32[]{:S(2)}, u32[]{:S(2)}) collective-permute-start(f32[1024,64]{0,1:T(8,128)S(1)} %get-tuple-element.13), channel_id=1, source_target_pairs={{0,1},{1,2},{2,3},{3,4},{4,5},{5,6},{6,7},{8,9},{9,10},{10,11},{11... | collective-permute-start | bytes 786440 | tf_op jit(solution)/shard_map/ppermute | solution.py:81
  25.1 0.2 maximum_convert_fusion
  25.3 0.0 collective-permute-done.2
  25.3 1.3 %collective-permute-start.6 = (f32[1024,64]{0,1:T(8,128)S(1)}, f32[1024,64]{0,1:T(8,128)S(1)}, u32[]{:S(2)}, u32[]{:S(2)}) collective-permute-start(f32[1024,64]{0,1:T(8,128)S(1)} %get-tuple-element.14), channel_id=1, source_target_pairs={{1,0},{2,1},{3,2},{4,3},{5,4},{6,5},{7,6},{9,8},{10,9},{11,10},{12... | collective-permute-start | bytes 786440 | tf_op jit(solution)/shard_map/ppermute | solution.py:81
  26.6 0.1 multiply_add_fusion
  26.7 0.0 collective-permute-done.4
  26.7 0.0 collective-permute-done.5
  26.8 2.1 %collective-permute-done.7 = f32[256,64]{0,1:T(8,128)S(1)} collective-permute-done((f32[256,64]{0,1:T(8,128)S(1)}, f32[256,64]{0,1:T(8,128)S(1)}, u32[]{:S(2)}, u32[]{:S(2)}) %collective-permute-start.7) | collective-permute-done | bytes 65568 | tf_op jit(solution)/shard_map/ppermute | solution.py:81
  28.9 1.7 %collective-permute-done.3 = f32[1024,64]{0,1:T(8,128)S(1)} collective-permute-done((f32[1024,64]{0,1:T(8,128)S(1)}, f32[1024,64]{0,1:T(8,128)S(1)}, u32[]{:S(2)}, u32[]{:S(2)}) %collective-permute-start.3) | collective-permute-done | bytes 262176 | tf_op jit(solution)/shard_map/ppermute | solution.py:81
  30.6 8.7 %collective-permute-done.6 = f32[1024,64]{0,1:T(8,128)S(1)} collective-permute-done((f32[1024,64]{0,1:T(8,128)S(1)}, f32[1024,64]{0,1:T(8,128)S(1)}, u32[]{:S(2)}, u32[]{:S(2)}) %collective-permute-start.6) | collective-permute-done | bytes 262176 | tf_op jit(solution)/shard_map/ppermute | solution.py:81
  39.3 0.3 fusion.21
  39.6 0.3 convolution_add_fusion.1
  40.0 0.5 multiply_convert_fusion.1
  40.4 3.3 %fusion.1 = f32[4096,256]{0,1:T(8,128)S(1)} fusion(s32[4096]{0:T(1024)S(1)} %get-tuple-element.20, bf16[1536,128]{0,1:T(8,128)(2,1)S(1)} %get-tuple-element.8, bf16[1536,128]{0,1:T(8,128)(2,1)S(1)} %get-tuple-element.7), kind=kOutput, calls=%fused_computation.3 | convolution fusion | flops 2152726528 | bytes 4997120 | tf_op jit(solution)/shard_map/dot_general | solution.py:52
  43.8 5.3 %fusion = f32[4096,256]{0,1:T(8,128)S(1)} fusion(s32[4096]{0:T(1024)S(1)} %get-tuple-element.19, bf16[1536,128]{0,1:T(8,128)(2,1)S(1)} %get-tuple-element.8, bf16[1536,128]{0,1:T(8,128)(2,1)S(1)} %get-tuple-element.7), kind=kOutput, calls=%fused_computation.1 | convolution fusion | flops 3229089792 | bytes 4997120 | tf_op jit(solution)/shard_map/dot_general | solution.py:52
  49.1 0.0 copy-start.2
  49.1 0.8 add_convert_fusion
  49.9 0.0 copy-done.2
  50.0 2.1 %fusion.15 = f32[32,8,256]{2,1,0:T(8,128)} fusion(bf16[4096,128]{0,1:T(8,128)(2,1)S(1)} %get-tuple-element.6, bf16[4096,128]{0,1:T(8,128)(2,1)S(1)} %get-tuple-element.5, s32[4096]{0:T(1024)S(1)} %copy-done.2), kind=kOutput, calls=%fused_computation.26 | convolution fusion | flops 543162368 | bytes 2375680 | tf_op jit(solution)/shard_map/dot_general | solution.py:132
  52.1 13.8 %all-to-all-start = ((f32[32,8,256]{2,1,0:T(8,128)}), f32[32,8,256]{2,1,0:T(8,128)S(1)}, u32[]{:S(2)}, u32[]{:S(2)}) async-start(f32[32,8,256]{2,1,0:T(8,128)} %fusion.15), calls=%async_computation | async-start | bytes 524288 | tf_op jit(solution)/shard_map/all_to_all | solution.py:135
  65.9 2.5 %multiply_convert_fusion.3 = (bf16[128,1024]{0,1:T(8,128)(2,1)S(1)}, bf16[128,1024]{0,1:T(8,128)(2,1)S(1)}) fusion(s32[1024]{0:T(1024)S(1)} %iota_add_fusion, s32[128]{0:T(128)S(1)} %iota_add_fusion.1), kind=kLoop, calls=%fused_computation.54 | loop fusion | flops 2490368 | bytes 528896 | tf_op jit(solution)/shard_map/convert
  68.5 0.1 pad_maximum_fusion
  68.5 10.9 %all-to-all-done = f32[32,8,256]{2,1,0:T(8,128)S(1)} async-done(((f32[32,8,256]{2,1,0:T(8,128)}), f32[32,8,256]{2,1,0:T(8,128)S(1)}, u32[]{:S(2)}, u32[]{:S(2)}) %all-to-all-start) | async-done | bytes 262176 | tf_op jit(solution)/shard_map/all_to_all | solution.py:135
  79.5 0.5 fusion.40
  80.0 10.3 %all_to_all.19 = f32[8,8,128]{2,0,1:T(8,128)S(1)} all-to-all(f32[8,8,128]{2,0,1:T(8,128)S(1)} %fusion.40), channel_id=1, replica_groups=mesh['seg'=32,'band'=8] {'band'}, dimensions={1} | all-to-all | bytes 65536 | tf_op jit(solution)/shard_map/all_to_all | solution.py:141
  90.2 0.6 reduce_sum.19
  (8 shorter events, 0.1 us)
Async XLA Ops:
  1.3 17.1 %collective-permute-start = (bf16[2,256,128]{1,2,0:T(8,128)(2,1)S(1)}, bf16[2,256,128]{1,2,0:T(8,128)(2,1)S(1)}, u32[]{:S(2)}, u32[]{:S(2)}) collective-permute-start(bf16[2,256,128]{1,2,0:T(8,128)(2,1)S(1)} %get-tuple-element.15), channel_id=1, source_target_pairs={{0,8},{8,16},{16,24},{24,32},{32,40},{40,48},{48,56},{56,64},{64,7... | collective-permute-start | bytes 393224 | tf_op jit(solution)/shard_map/ppermute | solution.py:81
  7.6 12.1 %collective-permute-start.1 = (bf16[2,256,128]{1,2,0:T(8,128)(2,1)S(1)}, bf16[2,256,128]{1,2,0:T(8,128)(2,1)S(1)}, u32[]{:S(2)}, u32[]{:S(2)}) collective-permute-start(bf16[2,256,128]{1,2,0:T(8,128)(2,1)S(1)} %get-tuple-element.16), channel_id=1, source_target_pairs={{8,0},{16,8},{24,16},{32,24},{40,32},{48,40},{56,48},{64,56},{72,6... | collective-permute-start | bytes 393224 | tf_op jit(solution)/shard_map/ppermute | solution.py:81
  9.6 8.7 %copy-start = (s32[4096]{0:T(1024)S(1)}, s32[4096]{0:T(1024)}, u32[]{:S(2)}) copy-start(s32[4096]{0:T(1024)} %param.6) | copy-start | bytes 49156
  9.6 8.7 %copy-start.1 = (s32[4096]{0:T(1024)S(1)}, s32[4096]{0:T(1024)}, u32[]{:S(2)}) copy-start(s32[4096]{0:T(1024)} %param.5) | copy-start | bytes 49156
  9.7 15.6 %collective-permute-start.2 = (f32[256,64]{0,1:T(8,128)S(1)}, f32[256,64]{0,1:T(8,128)S(1)}, u32[]{:S(2)}, u32[]{:S(2)}) collective-permute-start(f32[256,64]{0,1:T(8,128)S(1)} %get-tuple-element.9), channel_id=1, source_target_pairs={{0,9},{1,10},{2,11},{3,12},{4,13},{5,14},{6,15},{8,17},{9,18},{10,... | collective-permute-start | bytes 196616 | tf_op jit(solution)/shard_map/ppermute | solution.py:81
  15.6 11.1 %collective-permute-start.4 = (f32[256,64]{0,1:T(8,128)S(1)}, f32[256,64]{0,1:T(8,128)S(1)}, u32[]{:S(2)}, u32[]{:S(2)}) collective-permute-start(f32[256,64]{0,1:T(8,128)S(1)} %get-tuple-element.12), channel_id=1, source_target_pairs={{8,1},{9,2},{10,3},{11,4},{12,5},{13,6},{14,7},{16,9},{17,10},{18,... | collective-permute-start | bytes 196616 | tf_op jit(solution)/shard_map/ppermute | solution.py:81
  16.9 9.8 %collective-permute-start.5 = (f32[256,64]{0,1:T(8,128)S(1)}, f32[256,64]{0,1:T(8,128)S(1)}, u32[]{:S(2)}, u32[]{:S(2)}) collective-permute-start(f32[256,64]{0,1:T(8,128)S(1)} %get-tuple-element.11), channel_id=1, source_target_pairs={{1,8},{2,9},{3,10},{4,11},{5,12},{6,13},{7,14},{9,16},{10,17},{11,... | collective-permute-start | bytes 196616 | tf_op jit(solution)/shard_map/ppermute | solution.py:81
  18.4 10.5 %collective-permute-start.7 = (f32[256,64]{0,1:T(8,128)S(1)}, f32[256,64]{0,1:T(8,128)S(1)}, u32[]{:S(2)}, u32[]{:S(2)}) collective-permute-start(f32[256,64]{0,1:T(8,128)S(1)} %get-tuple-element.10), channel_id=1, source_target_pairs={{9,0},{10,1},{11,2},{12,3},{13,4},{14,5},{15,6},{17,8},{18,9},{19,... | collective-permute-start | bytes 196616 | tf_op jit(solution)/shard_map/ppermute | solution.py:81
  19.7 11.0 %collective-permute-start.3 = (f32[1024,64]{0,1:T(8,128)S(1)}, f32[1024,64]{0,1:T(8,128)S(1)}, u32[]{:S(2)}, u32[]{:S(2)}) collective-permute-start(f32[1024,64]{0,1:T(8,128)S(1)} %get-tuple-element.13), channel_id=1, source_target_pairs={{0,1},{1,2},{2,3},{3,4},{4,5},{5,6},{6,7},{8,9},{9,10},{10,11},{11... | collective-permute-start | bytes 786440 | tf_op jit(solution)/shard_map/ppermute | solution.py:81
  25.3 14.0 %collective-permute-start.6 = (f32[1024,64]{0,1:T(8,128)S(1)}, f32[1024,64]{0,1:T(8,128)S(1)}, u32[]{:S(2)}, u32[]{:S(2)}) collective-permute-start(f32[1024,64]{0,1:T(8,128)S(1)} %get-tuple-element.14), channel_id=1, source_target_pairs={{1,0},{2,1},{3,2},{4,3},{5,4},{6,5},{7,6},{9,8},{10,9},{11,10},{12... | collective-permute-start | bytes 786440 | tf_op jit(solution)/shard_map/ppermute | solution.py:81
  49.1 0.9 copy-start.2
  52.1 27.3 %all-to-all-start = ((f32[32,8,256]{2,1,0:T(8,128)}), f32[32,8,256]{2,1,0:T(8,128)S(1)}, u32[]{:S(2)}, u32[]{:S(2)}) async-start(f32[32,8,256]{2,1,0:T(8,128)} %fusion.15), calls=%async_computation | async-start | bytes 524288 | tf_op jit(solution)/shard_map/all_to_all | solution.py:135

commit v6 on v2

--- a/solution.py
+++ b/solution.py
@@ -18,12 +18,16 @@
 def extended(block, sides, width):
     for axis, dim in sides:
         count = lax.axis_size(axis)
-        forward = [(i, i + 1) for i in range(count - 1)]
-        backward = [(target, source) for source, target in forward]
-        low = lax.ppermute(
-            lax.slice_in_dim(block, block.shape[dim] - width, None, axis=dim), axis, forward
-        )
-        high = lax.ppermute(lax.slice_in_dim(block, 0, width, axis=dim), axis, backward)
+        odd = lax.axis_index(axis) % 2 == 1
+        first = lax.slice_in_dim(block, 0, width, axis=dim)
+        last = lax.slice_in_dim(block, block.shape[dim] - width, None, axis=dim)
+        inner = [(i, i ^ 1) for i in range(count - count % 2)]
+        outer = [(i, i + 1) for i in range(1, count - 1, 2)]
+        outer = outer + [(target, source) for source, target in outer]
+        from_inner = lax.ppermute(jnp.where(odd, first, last), axis, inner)
+        from_outer = lax.ppermute(jnp.where(odd, last, first), axis, outer)
+        low = jnp.where(odd, from_inner, from_outer)
+        high = jnp.where(odd, from_outer, from_inner)
         block = jnp.concatenate([low, block, high], axis=dim)
     return block
 

time: 74.8 us -> 71.4 us (0.955)
  waiting for transfers between devices: 22.8 us -> 14.1 us
  blocking collectives: 8.82 us -> 16.6 us
  starting transfers between devices: 25 us -> 22.5 us
    ppermute x4, waiting for transfers between devices: 12.7 us -> 4.26 us  [the longest x2 4.26 us: extended(): from_inner = lax.ppermute(jnp.where(odd, first, last), axis, inner)]
    all_to_all x1, blocking collectives: 8.82 us -> 16.6 us  [per_device(): lax.all_to_all(partial_lags, 'band', split_axis=1, concat_axis=0, tiled=T...]
    ppermute x4, starting transfers between devices: 13.9 us -> 11.5 us  [the longest x2 8.67 us: extended(): from_outer = lax.ppermute(jnp.where(odd, last, first), axis, outer)]
  transfers between devices with their start and end apart: 5 -> 5, of which waited for: 4 -> 2; matrix products, arithmetic and copies ran while one was open for 8% -> 8% of each run, Pallas kernels for 0% -> 0%
where the time goes in v6:
time: 71.4 us; the launch traced here: 71.1 us
  starting transfers between devices  22.5 us (32%)
  blocking collectives  16.6 us (23%)
  waiting for transfers between devices  14.1 us (20%)
  matrix products  11.9 us (17%)
  other arithmetic  4.36 us (6%)
  local copies, waits for them, and re-layouts  1.38 us (2%)
    all_to_all x1, blocking collectives, per_device(): lax.all_to_all(partial_lags, 'band', split_axis=1, concat_axis=0, tiled=T...  16.6 us
    all_to_all x1, starting transfers between devices, per_device(): lax.all_to_all(local_stack, 'seg', split_axis=0, concat_axis=0, tiled=True)  11 us
    all_to_all x1, waiting for transfers between devices, per_device(): lax.all_to_all(local_stack, 'seg', split_axis=0, concat_axis=0, tiled=True)  9.8 us
    ppermute x2, starting transfers between devices, extended(): from_outer = lax.ppermute(jnp.where(odd, last, first), axis, outer)  8.67 us
    dot_general x2, matrix products, select_rows(): return jnp.dot(chosen, table, preferred_element_type=jnp.float32)  8.27 us
    ppermute x2, waiting for transfers between devices, extended(): from_inner = lax.ppermute(jnp.where(odd, first, last), axis, inner)  4.26 us
    another operation x2, other arithmetic  3.37 us
    ppermute x2, starting transfers between devices, extended(): from_inner = lax.ppermute(jnp.where(odd, first, last), axis, inner)  2.82 us
  transfers between devices with their start and end apart: 5, of which 2 were waited for; matrix products, arithmetic and copies ran while one was open for 8% of the time, Pallas kernels for 0%

profile of v6, /device:TPU:1, one launch (start us, length us, event | category | flops | bytes accessed | tf_op | source)
XLA Modules:
  0.0 71.1 jit_solution(11926238046498051047)
XLA Ops:
  0.0 0.0 copy-start
  0.0 0.0 copy-start.1
  0.0 1.1 %fusion.53 = (bf16[1,1024,128]{2,1,0:T(8,128)(2,1)S(1)}, bf16[1,1024,128]{2,1,0:T(8,128)(2,1)S(1)}) fusion(bf16[2,1024,128]{2,1,0:T(8,128)(2,1)} %param.4), kind=kLoop, calls=%fused_computation.85 | loop fusion | bytes 1048576 | tf_op jit(solution)/shard_map/slice | solution.py:76
  1.1 0.1 copy.7
  1.2 0.1 copy.8
  1.4 0.1 fusion.27
  1.5 2.5 %collective-permute-start = (f32[1024,64]{0,1:T(8,128)S(1)}, f32[1024,64]{0,1:T(8,128)S(1)}, u32[]{:S(2)}, u32[]{:S(2)}) collective-permute-start(f32[1024,64]{0,1:T(8,128)S(1)} %get-tuple-element.14), channel_id=1, source_target_pairs={{0,1},{1,0},{2,3},{3,2},{4,5},{5,4},{6,7},{7,6},{8,9},{9,8},{10,11... | collective-permute-start | bytes 786440 | tf_op jit(solution)/shard_map/ppermute | solution.py:27
  4.1 0.7 collective-permute-start.1
  4.8 0.0 copy-done
  4.8 0.0 copy-done.1
  4.8 4.3 %collective-permute-done = f32[1024,64]{0,1:T(8,128)S(1)} collective-permute-done((f32[1024,64]{0,1:T(8,128)S(1)}, f32[1024,64]{0,1:T(8,128)S(1)}, u32[]{:S(2)}, u32[]{:S(2)}) %collective-permute-start) | collective-permute-done | bytes 262176 | tf_op jit(solution)/shard_map/ppermute | solution.py:27
  9.1 0.0 collective-permute-done.1
  9.1 0.3 fusion.34
  9.4 0.3 convolution_add_fusion.1
  9.7 0.4 fusion.28
  10.2 8.0 %collective-permute-start.3 = (bf16[256,256]{0,1:T(8,128)(2,1)S(1)}, bf16[256,256]{0,1:T(8,128)(2,1)S(1)}, u32[]{:S(2)}, u32[]{:S(2)}) collective-permute-start(bf16[256,256]{0,1:T(8,128)(2,1)S(1)} %broadcast_select_fusion.2), channel_id=1, source_target_pairs={{8,16},{24,32},{40,48},{56,64},{72,80},{88,96},{104,112},{120,128}... | collective-permute-start | bytes 393224 | tf_op jit(solution)/shard_map/ppermute | solution.py:28
  18.2 0.3 collective-permute-start.2
  18.5 3.3 %fusion.1 = f32[4096,256]{0,1:T(8,128)S(1)} fusion(s32[4096]{0:T(1024)S(1)} %get-tuple-element.23, bf16[1024,128]{0,1:T(8,128)(2,1)S(1)} %get-tuple-element.11, bf16[1024,128]{0,1:T(8,128)(2,1)S(1)} %get-tuple-element.10), kind=kOutput, calls=%fused_computation.3 | convolution fusion | flops 2152726528 | bytes 4734976 | tf_op jit(solution)/shard_map/dot_general | solution.py:56
  21.8 0.0 collective-permute-done.3
  21.8 0.0 collective-permute-done.2
  21.9 4.9 %fusion = f32[4096,256]{0,1:T(8,128)S(1)} fusion(s32[4096]{0:T(1024)S(1)} %get-tuple-element.22, bf16[256,256]{0,1:T(8,128)(2,1)S(1)} %get-tuple-element.19, bf16[1024,128]{0,1:T(8,128)(2,1)S(1)} %get-tuple-element.11, bf16[1024,128]{0,1:T(8,128)(2,1)S(1)} %get-tuple-element.10, bf16[256,256]{0,1:T(8,128)(2,1)S(1)} %get-tuple-element.18), kind=kOutput, calls=%fused_computation.1 | convolution fusion | flops 3230662656 | bytes 4997120 | tf_op jit(solution)/shard_map/dot_general | solution.py:56
  26.8 0.0 copy-start.2
  26.8 0.9 %add_convert_fusion = (bf16[4096,128]{0,1:T(8,128)(2,1)S(1)}, bf16[4096,128]{0,1:T(8,128)(2,1)S(1)}) fusion(f32[4096,256]{0,1:T(8,128)S(1)} %fusion, f32[4096,256]{0,1:T(8,128)S(1)} %fusion.1), kind=kLoop, calls=%fused_computation.13 | loop fusion | flops 4194304 | bytes 10485760 | tf_op jit(solution)/shard_map/convert.4
  27.7 0.0 copy-done.2
  27.7 2.2 %fusion.14 = f32[32,8,256]{2,1,0:T(8,128)} fusion(bf16[4096,128]{0,1:T(8,128)(2,1)S(1)} %get-tuple-element.9, bf16[4096,128]{0,1:T(8,128)(2,1)S(1)} %get-tuple-element.8, s32[4096]{0:T(1024)S(1)} %copy-done.2), kind=kOutput, calls=%fused_computation.24 | convolution fusion | flops 543162368 | bytes 2375680 | tf_op jit(solution)/shard_map/dot_general | solution.py:99
  29.8 11.0 %all-to-all-start = ((f32[32,8,256]{2,1,0:T(8,128)}), f32[32,8,256]{2,1,0:T(8,128)S(1)}, u32[]{:S(2)}, u32[]{:S(2)}) async-start(f32[32,8,256]{2,1,0:T(8,128)} %fusion.14), calls=%async_computation | async-start | bytes 524288 | tf_op jit(solution)/shard_map/all_to_all | solution.py:102
  40.9 2.5 %multiply_convert_fusion.1 = (bf16[128,1024]{0,1:T(8,128)(2,1)S(1)}, bf16[128,1024]{0,1:T(8,128)(2,1)S(1)}) fusion(s32[1024]{0:T(1024)S(1)} %iota_add_fusion, s32[128]{0:T(128)S(1)} %iota_add_fusion.1), kind=kLoop, calls=%fused_computation.55 | loop fusion | flops 2490368 | bytes 528896 | tf_op jit(solution)/shard_map/convert.2
  43.4 0.1 pad_maximum_fusion.1
  43.5 9.8 %all-to-all-done = f32[32,8,256]{2,1,0:T(8,128)S(1)} async-done(((f32[32,8,256]{2,1,0:T(8,128)}), f32[32,8,256]{2,1,0:T(8,128)S(1)}, u32[]{:S(2)}, u32[]{:S(2)}) %all-to-all-start) | async-done | bytes 262176 | tf_op jit(solution)/shard_map/all_to_all | solution.py:102
  53.3 0.5 fusion.45
  53.8 16.6 %all_to_all.19 = f32[8,8,128]{2,0,1:T(8,128)S(1)} all-to-all(f32[8,8,128]{2,0,1:T(8,128)S(1)} %fusion.45), channel_id=1, replica_groups=mesh['seg'=32,'band'=8] {'band'}, dimensions={1} | all-to-all | bytes 65536 | tf_op jit(solution)/shard_map/all_to_all | solution.py:108
  70.5 0.6 reduce_sum.19
  (10 shorter events, 0.2 us)
Async XLA Ops:
  0.0 4.8 %copy-start = (s32[4096]{0:T(1024)S(1)}, s32[4096]{0:T(1024)}, u32[]{:S(2)}) copy-start(s32[4096]{0:T(1024)} %param.6) | copy-start | bytes 49156
  0.0 4.8 %copy-start.1 = (s32[4096]{0:T(1024)S(1)}, s32[4096]{0:T(1024)}, u32[]{:S(2)}) copy-start(s32[4096]{0:T(1024)} %param.5) | copy-start | bytes 49156
  1.5 7.5 %collective-permute-start = (f32[1024,64]{0,1:T(8,128)S(1)}, f32[1024,64]{0,1:T(8,128)S(1)}, u32[]{:S(2)}, u32[]{:S(2)}) collective-permute-start(f32[1024,64]{0,1:T(8,128)S(1)} %get-tuple-element.14), channel_id=1, source_target_pairs={{0,1},{1,0},{2,3},{3,2},{4,5},{5,4},{6,7},{7,6},{8,9},{9,8},{10,11... | collective-permute-start | bytes 786440 | tf_op jit(solution)/shard_map/ppermute | solution.py:27
  4.1 5.0 %collective-permute-start.1 = (f32[1024,64]{0,1:T(8,128)S(1)}, f32[1024,64]{0,1:T(8,128)S(1)}, u32[]{:S(2)}, u32[]{:S(2)}) collective-permute-start(f32[1024,64]{0,1:T(8,128)S(1)} %get-tuple-element.15), channel_id=1, source_target_pairs={{1,2},{3,4},{5,6},{2,1},{4,3},{6,5},{9,10},{11,12},{13,14},{10,9},... | collective-permute-start | bytes 786440 | tf_op jit(solution)/shard_map/ppermute | solution.py:28
  10.2 11.7 %collective-permute-start.3 = (bf16[256,256]{0,1:T(8,128)(2,1)S(1)}, bf16[256,256]{0,1:T(8,128)(2,1)S(1)}, u32[]{:S(2)}, u32[]{:S(2)}) collective-permute-start(bf16[256,256]{0,1:T(8,128)(2,1)S(1)} %broadcast_select_fusion.2), channel_id=1, source_target_pairs={{8,16},{24,32},{40,48},{56,64},{72,80},{88,96},{104,112},{120,128}... | collective-permute-start | bytes 393224 | tf_op jit(solution)/shard_map/ppermute | solution.py:28
  18.2 3.7 %collective-permute-start.2 = (bf16[256,256]{0,1:T(8,128)(2,1)S(1)}, bf16[256,256]{0,1:T(8,128)(2,1)S(1)}, u32[]{:S(2)}, u32[]{:S(2)}) collective-permute-start(bf16[256,256]{0,1:T(8,128)(2,1)S(1)} %get-tuple-element.5), channel_id=1, source_target_pairs={{0,8},{8,0},{16,24},{24,16},{32,40},{40,32},{48,56},{56,48},{64,72... | collective-permute-start | bytes 393224 | tf_op jit(solution)/shard_map/ppermute | solution.py:27
  26.8 0.9 %copy-start.2 = (s32[4096]{0:T(1024)S(1)}, s32[4096]{0:T(1024)}, u32[]{:S(2)}) copy-start(s32[4096]{0:T(1024)} %param.7) | copy-start | bytes 49156
  29.8 23.4 %all-to-all-start = ((f32[32,8,256]{2,1,0:T(8,128)}), f32[32,8,256]{2,1,0:T(8,128)S(1)}, u32[]{:S(2)}, u32[]{:S(2)}) async-start(f32[32,8,256]{2,1,0:T(8,128)} %fusion.14), calls=%async_computation | async-start | bytes 524288 | tf_op jit(solution)/shard_map/all_to_all | solution.py:102

commit v7 on v6

--- a/solution.py
+++ b/solution.py
@@ -75,8 +75,8 @@
     local_bins = spectra.shape[2]
     real_part = spectra[0].astype(jnp.float32)
     imag_part = spectra[1].astype(jnp.float32)
-    power_sum = real_part * real_part + imag_part * imag_part
-    padded_power = extended(power_sum, (("band", 1),), HALF_WIN)
+    padded_spectra = extended(spectra, (("band", 2),), HALF_WIN).astype(jnp.float32)
+    padded_power = padded_spectra[0] * padded_spectra[0] + padded_spectra[1] * padded_spectra[1]
     window_sum = exact_dot(padded_power, window_matrix(local_bins, HALF_WIN))
     scaling = lax.rsqrt(window_sum / (2 * HALF_WIN + 1) + epsilon)
     whitened = jnp.concatenate([real_part * scaling, imag_part * scaling], axis=1).astype(

time: 71.4 us -> 84.2 us (1.18)
  blocking collectives: 16.6 us -> 23 us
  waiting for transfers between devices: 14.1 us -> 19.3 us
  other arithmetic: 4.36 us -> 6.39 us
  local copies, waits for them, and re-layouts: 1.38 us -> 0.34 us
    all_to_all x1, blocking collectives: 16.6 us -> 23 us  [per_device(): lax.all_to_all(partial_lags, 'band', split_axis=1, concat_axis=0, tiled=T...]
    ppermute x2, waiting for transfers between devices: 4.26 us -> 9.49 us  [extended(): from_inner = lax.ppermute(jnp.where(odd, first, last), axis, inner)]
    select_n x2, other arithmetic: 0.09 us -> 1.61 us  [extended(): from_inner = lax.ppermute(jnp.where(odd, first, last), axis, inner)]
    slice x1, local copies, waits for them, and re-layouts: 1.08 us -> 0.04 us  [per_device(): real_part = spectra[0].astype(jnp.float32)]
  transfers between devices with their start and end apart: 5 -> 5, of which waited for: 2 -> 2; matrix products, arithmetic and copies ran while one was open for 8% -> 7% of each run, Pallas kernels for 0% -> 0%
where the time goes in v7:
time: 84.2 us; the launch traced here: 83.9 us
  blocking collectives  23 us (27%)
  starting transfers between devices  22.5 us (27%)
  waiting for transfers between devices  19.3 us (23%)
  matrix products  12.1 us (14%)
  other arithmetic  6.39 us (8%)
    all_to_all x1, blocking collectives, per_device(): lax.all_to_all(partial_lags, 'band', split_axis=1, concat_axis=0, tiled=T...  23 us
    all_to_all x1, starting transfers between devices, per_device(): lax.all_to_all(local_stack, 'seg', split_axis=0, concat_axis=0, tiled=True)  11 us
    all_to_all x1, waiting for transfers between devices, per_device(): lax.all_to_all(local_stack, 'seg', split_axis=0, concat_axis=0, tiled=True)  9.8 us
    ppermute x2, waiting for transfers between devices, extended(): from_inner = lax.ppermute(jnp.where(odd, first, last), axis, inner)  9.49 us
    ppermute x2, starting transfers between devices, extended(): from_outer = lax.ppermute(jnp.where(odd, last, first), axis, outer)  8.69 us
    dot_general x2, matrix products, select_rows(): return jnp.dot(chosen, table, preferred_element_type=jnp.float32)  8.27 us
    another operation x2, other arithmetic  3.37 us
    ppermute x2, starting transfers between devices, extended(): from_inner = lax.ppermute(jnp.where(odd, first, last), axis, inner)  2.82 us
  transfers between devices with their start and end apart: 5, of which 2 were waited for; matrix products, arithmetic and copies ran while one was open for 7% of the time, Pallas kernels for 0%

profile of v7, /device:TPU:1, one launch (start us, length us, event | category | flops | bytes accessed | tf_op | source)
XLA Modules:
  0.0 83.9 jit_solution(5634627152384593607)
XLA Ops:
  0.0 0.0 copy-start
  0.0 0.0 copy-start.1
  0.0 0.0 copy-start.2
  0.0 1.6 %broadcast_select_fusion.3 = (bf16[2,1024,64]{2,1,0:T(8,128)(2,1)S(1)}, bf16[2,1024,64]{2,1,0:T(8,128)(2,1)S(1)}) fusion(pred[]{:T(512)S(6)} %eq.56, bf16[2,1024,128]{2,1,0:T(8,128)(2,1)} %param.4), kind=kLoop, calls=%fused_computation.60 | loop fusion | flops 262144 | bytes 1048577 | tf_op jit(solution)/shard_map/jit(_where)/select_n | solution.py:27
  1.6 2.5 %collective-permute-start = (bf16[2,1024,64]{2,1,0:T(8,128)(2,1)S(1)}, bf16[2,1024,64]{2,1,0:T(8,128)(2,1)S(1)}, u32[]{:S(2)}, u32[]{:S(2)}) collective-permute-start(bf16[2,1024,64]{2,1,0:T(8,128)(2,1)S(1)} %get-tuple-element.16), channel_id=1, source_target_pairs={{0,1},{1,0},{2,3},{3,2},{4,5},{5,4},{6,7},{7,6},{8,9},{9,8},{10,11... | collective-permute-start | bytes 786440 | tf_op jit(solution)/shard_map/ppermute | solution.py:27
  4.1 0.7 collective-permute-start.1
  4.8 0.0 copy-done
  4.9 0.1 copy.7
  5.0 0.1 copy.8
  5.2 0.0 copy-done.1
  5.2 0.0 copy-done.2
  5.2 9.5 %collective-permute-done = bf16[2,1024,64]{2,1,0:T(8,128)(2,1)S(1)} collective-permute-done((bf16[2,1024,64]{2,1,0:T(8,128)(2,1)S(1)}, bf16[2,1024,64]{2,1,0:T(8,128)(2,1)S(1)}, u32[]{:S(2)}, u32[]{:S(2)}) %collective-permute-start) | collective-permute-done | bytes 262176 | tf_op jit(solution)/shard_map/ppermute | solution.py:27
  14.7 0.0 collective-permute-done.1
  14.7 0.1 broadcast_select_fusion.1
  14.8 0.6 maximum_convert_fusion
  15.4 0.3 fusion.33
  15.7 0.4 convolution_add_fusion.1
  16.1 0.5 fusion.38
  16.7 8.0 %collective-permute-start.3 = (bf16[256,256]{0,1:T(8,128)(2,1)S(1)}, bf16[256,256]{0,1:T(8,128)(2,1)S(1)}, u32[]{:S(2)}, u32[]{:S(2)}) collective-permute-start(bf16[256,256]{0,1:T(8,128)(2,1)S(1)} %broadcast_select_fusion.6), channel_id=1, source_target_pairs={{8,16},{24,32},{40,48},{56,64},{72,80},{88,96},{104,112},{120,128}... | collective-permute-start | bytes 393224 | tf_op jit(solution)/shard_map/ppermute | solution.py:28
  24.7 0.3 collective-permute-start.2
  25.0 3.4 %fusion.1 = f32[4096,256]{0,1:T(8,128)S(1)} fusion(s32[4096]{0:T(1024)S(1)} %get-tuple-element.23, bf16[1024,128]{0,1:T(8,128)(2,1)S(1)} %get-tuple-element.13, bf16[1024,128]{0,1:T(8,128)(2,1)S(1)} %get-tuple-element.12), kind=kOutput, calls=%fused_computation.3 | convolution fusion | flops 2152726528 | bytes 4734976 | tf_op jit(solution)/shard_map/dot_general | solution.py:56
  28.4 0.0 collective-permute-done.3
  28.4 0.0 collective-permute-done.2
  28.4 4.9 %fusion = f32[4096,256]{0,1:T(8,128)S(1)} fusion(s32[4096]{0:T(1024)S(1)} %get-tuple-element.22, bf16[256,256]{0,1:T(8,128)(2,1)S(1)} %get-tuple-element.19, bf16[1024,128]{0,1:T(8,128)(2,1)S(1)} %get-tuple-element.13, bf16[1024,128]{0,1:T(8,128)(2,1)S(1)} %get-tuple-element.12, bf16[256,256]{0,1:T(8,128)(2,1)S(1)} %get-tuple-element.18), kind=kOutput, calls=%fused_computation.1 | convolution fusion | flops 3230662656 | bytes 4997120 | tf_op jit(solution)/shard_map/dot_general | solution.py:56
  33.3 0.0 copy-start.3
  33.4 0.9 %add_convert_fusion = (bf16[4096,128]{0,1:T(8,128)(2,1)S(1)}, bf16[4096,128]{0,1:T(8,128)(2,1)S(1)}) fusion(f32[4096,256]{0,1:T(8,128)S(1)} %fusion, f32[4096,256]{0,1:T(8,128)S(1)} %fusion.1), kind=kLoop, calls=%fused_computation.13 | loop fusion | flops 4194304 | bytes 10485760 | tf_op jit(solution)/shard_map/convert.4
  34.2 0.0 copy-done.3
  34.2 2.1 %fusion.14 = f32[32,8,256]{2,1,0:T(8,128)} fusion(bf16[4096,128]{0,1:T(8,128)(2,1)S(1)} %get-tuple-element.9, bf16[4096,128]{0,1:T(8,128)(2,1)S(1)} %get-tuple-element.8, s32[4096]{0:T(1024)S(1)} %copy-done.3), kind=kOutput, calls=%fused_computation.24 | convolution fusion | flops 543162368 | bytes 2375680 | tf_op jit(solution)/shard_map/dot_general | solution.py:99
  36.4 11.0 %all-to-all-start = ((f32[32,8,256]{2,1,0:T(8,128)}), f32[32,8,256]{2,1,0:T(8,128)S(1)}, u32[]{:S(2)}, u32[]{:S(2)}) async-start(f32[32,8,256]{2,1,0:T(8,128)} %fusion.14), calls=%async_computation | async-start | bytes 524288 | tf_op jit(solution)/shard_map/all_to_all | solution.py:102
  47.4 2.5 %multiply_convert_fusion.1 = (bf16[128,1024]{0,1:T(8,128)(2,1)S(1)}, bf16[128,1024]{0,1:T(8,128)(2,1)S(1)}) fusion(s32[1024]{0:T(1024)S(1)} %iota_add_fusion, s32[128]{0:T(128)S(1)} %iota_add_fusion.1), kind=kLoop, calls=%fused_computation.56 | loop fusion | flops 2490368 | bytes 528896 | tf_op jit(solution)/shard_map/convert.2
  49.9 0.1 pad_maximum_fusion
  50.0 9.8 %all-to-all-done = f32[32,8,256]{2,1,0:T(8,128)S(1)} async-done(((f32[32,8,256]{2,1,0:T(8,128)}), f32[32,8,256]{2,1,0:T(8,128)S(1)}, u32[]{:S(2)}, u32[]{:S(2)}) %all-to-all-start) | async-done | bytes 262176 | tf_op jit(solution)/shard_map/all_to_all | solution.py:102
  59.9 0.5 fusion.46
  60.4 23.0 %all_to_all.19 = f32[8,8,128]{2,0,1:T(8,128)S(1)} all-to-all(f32[8,8,128]{2,0,1:T(8,128)S(1)} %fusion.46), channel_id=1, replica_groups=mesh['seg'=32,'band'=8] {'band'}, dimensions={1} | all-to-all | bytes 65536 | tf_op jit(solution)/shard_map/all_to_all | solution.py:108
  83.3 0.6 reduce_sum.19
  (9 shorter events, 0.2 us)
Async XLA Ops:
  0.0 4.8 %copy-start = (bf16[2,1024,128]{2,1,0:T(8,128)(2,1)S(1)}, bf16[2,1024,128]{2,1,0:T(8,128)(2,1)}, u32[]{:S(2)}) copy-start(bf16[2,1024,128]{2,1,0:T(8,128)(2,1)} %param.4) | copy-start | bytes 1572868
  0.0 5.2 %copy-start.1 = (s32[4096]{0:T(1024)S(1)}, s32[4096]{0:T(1024)}, u32[]{:S(2)}) copy-start(s32[4096]{0:T(1024)} %param.6) | copy-start | bytes 49156
  0.0 5.2 %copy-start.2 = (s32[4096]{0:T(1024)S(1)}, s32[4096]{0:T(1024)}, u32[]{:S(2)}) copy-start(s32[4096]{0:T(1024)} %param.5) | copy-start | bytes 49156
  1.6 13.2 %collective-permute-start = (bf16[2,1024,64]{2,1,0:T(8,128)(2,1)S(1)}, bf16[2,1024,64]{2,1,0:T(8,128)(2,1)S(1)}, u32[]{:S(2)}, u32[]{:S(2)}) collective-permute-start(bf16[2,1024,64]{2,1,0:T(8,128)(2,1)S(1)} %get-tuple-element.16), channel_id=1, source_target_pairs={{0,1},{1,0},{2,3},{3,2},{4,5},{5,4},{6,7},{7,6},{8,9},{9,8},{10,11... | collective-permute-start | bytes 786440 | tf_op jit(solution)/shard_map/ppermute | solution.py:27
  4.1 10.6 %collective-permute-start.1 = (bf16[2,1024,64]{2,1,0:T(8,128)(2,1)S(1)}, bf16[2,1024,64]{2,1,0:T(8,128)(2,1)S(1)}, u32[]{:S(2)}, u32[]{:S(2)}) collective-permute-start(bf16[2,1024,64]{2,1,0:T(8,128)(2,1)S(1)} %get-tuple-element.17), channel_id=1, source_target_pairs={{1,2},{3,4},{5,6},{2,1},{4,3},{6,5},{9,10},{11,12},{13,14},{10,9},... | collective-permute-start | bytes 786440 | tf_op jit(solution)/shard_map/ppermute | solution.py:28
  16.7 11.7 %collective-permute-start.3 = (bf16[256,256]{0,1:T(8,128)(2,1)S(1)}, bf16[256,256]{0,1:T(8,128)(2,1)S(1)}, u32[]{:S(2)}, u32[]{:S(2)}) collective-permute-start(bf16[256,256]{0,1:T(8,128)(2,1)S(1)} %broadcast_select_fusion.6), channel_id=1, source_target_pairs={{8,16},{24,32},{40,48},{56,64},{72,80},{88,96},{104,112},{120,128}... | collective-permute-start | bytes 393224 | tf_op jit(solution)/shard_map/ppermute | solution.py:28
  24.7 3.7 %collective-permute-start.2 = (bf16[256,256]{0,1:T(8,128)(2,1)S(1)}, bf16[256,256]{0,1:T(8,128)(2,1)S(1)}, u32[]{:S(2)}, u32[]{:S(2)}) collective-permute-start(bf16[256,256]{0,1:T(8,128)(2,1)S(1)} %get-tuple-element.5), channel_id=1, source_target_pairs={{0,8},{8,0},{16,24},{24,16},{32,40},{40,32},{48,56},{56,48},{64,72... | collective-permute-start | bytes 393224 | tf_op jit(solution)/shard_map/ppermute | solution.py:27
  33.3 0.9 %copy-start.3 = (s32[4096]{0:T(1024)S(1)}, s32[4096]{0:T(1024)}, u32[]{:S(2)}) copy-start(s32[4096]{0:T(1024)} %param.7) | copy-start | bytes 49156
  36.4 23.4 %all-to-all-start = ((f32[32,8,256]{2,1,0:T(8,128)}), f32[32,8,256]{2,1,0:T(8,128)S(1)}, u32[]{:S(2)}, u32[]{:S(2)}) async-start(f32[32,8,256]{2,1,0:T(8,128)} %fusion.14), calls=%async_computation | async-start | bytes 524288 | tf_op jit(solution)/shard_map/all_to_all | solution.py:102

commit v8 on v6

--- a/solution.py
+++ b/solution.py
@@ -99,8 +99,12 @@
     local_stack = lax.dot_general(
         members, cross_both, (((0,), (0,)), ((), ())), preferred_element_type=jnp.float32
     )
-    gathered = lax.all_to_all(local_stack, "seg", split_axis=0, concat_axis=0, tiled=True)
-    stack = jnp.sum(gathered.reshape(segments, OB_DEV, 2 * local_bins), axis=0)
+    gathered = lax.all_to_all(
+        local_stack.astype(jnp.bfloat16), "seg", split_axis=0, concat_axis=0, tiled=True
+    )
+    stack = jnp.sum(
+        gathered.reshape(segments, OB_DEV, 2 * local_bins).astype(jnp.float32), axis=0
+    )
     table = lag_table(band_position * local_bins, local_bins, FREQ, LAGS)
     partial_lags = jnp.dot(
         stack, table.astype(jnp.float32), precision=lax.Precision.HIGHEST

time: 71.4 us -> 69.1 us (0.968)
  waiting for transfers between devices: 14.1 us -> 12.3 us
    all_to_all x1, waiting for transfers between devices: 9.8 us -> 8.02 us  [per_device(): lax.all_to_all(local_stack.astype(jnp.bfloat16), 'seg', split_axis=0, con...]
  transfers between devices with their start and end apart: 5 -> 5, of which waited for: 2 -> 2; matrix products, arithmetic and copies ran while one was open for 8% -> 9% of each run, Pallas kernels for 0% -> 0%
where the time goes in v8:
time: 69.1 us; the launch traced here: 68.9 us
  starting transfers between devices  22.5 us (33%)
  blocking collectives  16.3 us (24%)
  waiting for transfers between devices  12.3 us (18%)
  matrix products  11.8 us (17%)
  other arithmetic  4.35 us (6%)
  local copies, waits for them, and re-layouts  1.38 us (2%)
    all_to_all x1, blocking collectives, per_device(): lax.all_to_all(partial_lags, 'band', split_axis=1, concat_axis=0, tiled=T...  16.3 us
    all_to_all x1, starting transfers between devices, per_device(): lax.all_to_all(local_stack.astype(jnp.bfloat16), 'seg', split_axis=0, con...  11 us
    ppermute x2, starting transfers between devices, extended(): from_outer = lax.ppermute(jnp.where(odd, last, first), axis, outer)  8.67 us
    dot_general x2, matrix products, select_rows(): return jnp.dot(chosen, table, preferred_element_type=jnp.float32)  8.27 us
    all_to_all x1, waiting for transfers between devices, per_device(): lax.all_to_all(local_stack.astype(jnp.bfloat16), 'seg', split_axis=0, con...  8.02 us
    ppermute x2, waiting for transfers between devices, extended(): from_inner = lax.ppermute(jnp.where(odd, first, last), axis, inner)  4.24 us
    another operation x2, other arithmetic  3.37 us
    ppermute x2, starting transfers between devices, extended(): from_inner = lax.ppermute(jnp.where(odd, first, last), axis, inner)  2.82 us
  transfers between devices with their start and end apart: 5, of which 2 were waited for; matrix products, arithmetic and copies ran while one was open for 9% of the time, Pallas kernels for 0%

profile of v8, /device:TPU:1, one launch (start us, length us, event | category | flops | bytes accessed | tf_op | source)
XLA Modules:
  0.0 68.9 jit_solution(14936344096291909260)
XLA Ops:
  0.0 0.0 copy-start
  0.0 0.0 copy-start.1
  0.0 1.1 %fusion.58 = (bf16[1,1024,128]{2,1,0:T(8,128)(2,1)S(1)}, bf16[1,1024,128]{2,1,0:T(8,128)(2,1)S(1)}) fusion(bf16[2,1024,128]{2,1,0:T(8,128)(2,1)} %param.4), kind=kLoop, calls=%fused_computation.87 | loop fusion | bytes 1048576 | tf_op jit(solution)/shard_map/slice | solution.py:76
  1.1 0.1 copy.7
  1.2 0.1 copy.8
  1.4 0.1 fusion.32
  1.5 2.5 %collective-permute-start = (f32[1024,64]{0,1:T(8,128)S(1)}, f32[1024,64]{0,1:T(8,128)S(1)}, u32[]{:S(2)}, u32[]{:S(2)}) collective-permute-start(f32[1024,64]{0,1:T(8,128)S(1)} %get-tuple-element.14), channel_id=1, source_target_pairs={{0,1},{1,0},{2,3},{3,2},{4,5},{5,4},{6,7},{7,6},{8,9},{9,8},{10,11... | collective-permute-start | bytes 786440 | tf_op jit(solution)/shard_map/ppermute | solution.py:27
  4.1 0.7 collective-permute-start.1
  4.8 0.0 copy-done
  4.8 0.0 copy-done.1
  4.8 4.2 %collective-permute-done = f32[1024,64]{0,1:T(8,128)S(1)} collective-permute-done((f32[1024,64]{0,1:T(8,128)S(1)}, f32[1024,64]{0,1:T(8,128)S(1)}, u32[]{:S(2)}, u32[]{:S(2)}) %collective-permute-start) | collective-permute-done | bytes 262176 | tf_op jit(solution)/shard_map/ppermute | solution.py:27
  9.1 0.0 collective-permute-done.1
  9.1 0.3 fusion.39
  9.4 0.3 convolution_add_fusion.1
  9.7 0.4 fusion.33
  10.2 8.0 %collective-permute-start.3 = (bf16[256,256]{0,1:T(8,128)(2,1)S(1)}, bf16[256,256]{0,1:T(8,128)(2,1)S(1)}, u32[]{:S(2)}, u32[]{:S(2)}) collective-permute-start(bf16[256,256]{0,1:T(8,128)(2,1)S(1)} %broadcast_select_fusion.2), channel_id=1, source_target_pairs={{8,16},{24,32},{40,48},{56,64},{72,80},{88,96},{104,112},{120,128}... | collective-permute-start | bytes 393224 | tf_op jit(solution)/shard_map/ppermute | solution.py:28
  18.2 0.3 collective-permute-start.2
  18.5 3.3 %fusion.1 = f32[4096,256]{0,1:T(8,128)S(1)} fusion(s32[4096]{0:T(1024)S(1)} %get-tuple-element.23, bf16[1024,128]{0,1:T(8,128)(2,1)S(1)} %get-tuple-element.11, bf16[1024,128]{0,1:T(8,128)(2,1)S(1)} %get-tuple-element.10), kind=kOutput, calls=%fused_computation.3 | convolution fusion | flops 2152726528 | bytes 4734976 | tf_op jit(solution)/shard_map/dot_general | solution.py:56
  21.8 0.0 collective-permute-done.3
  21.8 0.0 collective-permute-done.2
  21.9 4.9 %fusion = f32[4096,256]{0,1:T(8,128)S(1)} fusion(s32[4096]{0:T(1024)S(1)} %get-tuple-element.22, bf16[256,256]{0,1:T(8,128)(2,1)S(1)} %get-tuple-element.19, bf16[1024,128]{0,1:T(8,128)(2,1)S(1)} %get-tuple-element.11, bf16[1024,128]{0,1:T(8,128)(2,1)S(1)} %get-tuple-element.10, bf16[256,256]{0,1:T(8,128)(2,1)S(1)} %get-tuple-element.18), kind=kOutput, calls=%fused_computation.1 | convolution fusion | flops 3230662656 | bytes 4997120 | tf_op jit(solution)/shard_map/dot_general | solution.py:56
  26.8 0.0 copy-start.2
  26.8 0.8 %add_convert_fusion = (bf16[4096,128]{0,1:T(8,128)(2,1)S(1)}, bf16[4096,128]{0,1:T(8,128)(2,1)S(1)}) fusion(f32[4096,256]{0,1:T(8,128)S(1)} %fusion, f32[4096,256]{0,1:T(8,128)S(1)} %fusion.1), kind=kLoop, calls=%fused_computation.13 | loop fusion | flops 4194304 | bytes 10485760 | tf_op jit(solution)/shard_map/convert.4
  27.7 0.0 copy-done.2
  27.7 2.1 %fusion.19 = bf16[32,8,256]{2,1,0:T(8,128)(2,1)} fusion(bf16[4096,128]{0,1:T(8,128)(2,1)S(1)} %get-tuple-element.9, bf16[4096,128]{0,1:T(8,128)(2,1)S(1)} %get-tuple-element.8, s32[4096]{0:T(1024)S(1)} %copy-done.2), kind=kOutput, calls=%fused_computation.25 | convolution fusion | flops 543227904 | bytes 2244608 | tf_op jit(solution)/shard_map/dot_general | solution.py:99
  29.8 11.0 %all-to-all-start = ((bf16[32,8,256]{2,1,0:T(8,128)(2,1)}), bf16[32,8,256]{2,1,0:T(8,128)(2,1)S(1)}, u32[]{:S(2)}, u32[]{:S(2)}) async-start(bf16[32,8,256]{2,1,0:T(8,128)(2,1)} %fusion.19), calls=%async_computation | async-start | bytes 262144 | tf_op jit(solution)/shard_map/all_to_all | solution.py:102
  40.8 2.5 %multiply_convert_fusion.1 = (bf16[128,1024]{0,1:T(8,128)(2,1)S(1)}, bf16[128,1024]{0,1:T(8,128)(2,1)S(1)}) fusion(s32[1024]{0:T(1024)S(1)} %iota_add_fusion, s32[128]{0:T(128)S(1)} %iota_add_fusion.1), kind=kLoop, calls=%fused_computation.56 | loop fusion | flops 2490368 | bytes 528896 | tf_op jit(solution)/shard_map/convert.2
  43.3 0.1 pad_maximum_fusion.1
  43.4 8.0 %all-to-all-done = bf16[32,8,256]{2,1,0:T(8,128)(2,1)S(1)} async-done(((bf16[32,8,256]{2,1,0:T(8,128)(2,1)}), bf16[32,8,256]{2,1,0:T(8,128)(2,1)S(1)}, u32[]{:S(2)}, u32[]{:S(2)}) %all-to-all-start) | async-done | bytes 131104 | tf_op jit(solution)/shard_map/all_to_all | solution.py:102
  51.5 0.5 fusion.50
  52.0 16.3 %all_to_all.19 = f32[8,8,128]{2,0,1:T(8,128)S(1)} all-to-all(f32[8,8,128]{2,0,1:T(8,128)S(1)} %fusion.50), channel_id=1, replica_groups=mesh['seg'=32,'band'=8] {'band'}, dimensions={1} | all-to-all | bytes 65536 | tf_op jit(solution)/shard_map/all_to_all | solution.py:112
  68.3 0.6 reduce_sum.19
  (10 shorter events, 0.2 us)
Async XLA Ops:
  0.0 4.8 %copy-start = (s32[4096]{0:T(1024)S(1)}, s32[4096]{0:T(1024)}, u32[]{:S(2)}) copy-start(s32[4096]{0:T(1024)} %param.6) | copy-start | bytes 49156
  0.0 4.8 %copy-start.1 = (s32[4096]{0:T(1024)S(1)}, s32[4096]{0:T(1024)}, u32[]{:S(2)}) copy-start(s32[4096]{0:T(1024)} %param.5) | copy-start | bytes 49156
  1.5 7.5 %collective-permute-start = (f32[1024,64]{0,1:T(8,128)S(1)}, f32[1024,64]{0,1:T(8,128)S(1)}, u32[]{:S(2)}, u32[]{:S(2)}) collective-permute-start(f32[1024,64]{0,1:T(8,128)S(1)} %get-tuple-element.14), channel_id=1, source_target_pairs={{0,1},{1,0},{2,3},{3,2},{4,5},{5,4},{6,7},{7,6},{8,9},{9,8},{10,11... | collective-permute-start | bytes 786440 | tf_op jit(solution)/shard_map/ppermute | solution.py:27
  4.1 5.0 %collective-permute-start.1 = (f32[1024,64]{0,1:T(8,128)S(1)}, f32[1024,64]{0,1:T(8,128)S(1)}, u32[]{:S(2)}, u32[]{:S(2)}) collective-permute-start(f32[1024,64]{0,1:T(8,128)S(1)} %get-tuple-element.15), channel_id=1, source_target_pairs={{1,2},{3,4},{5,6},{2,1},{4,3},{6,5},{9,10},{11,12},{13,14},{10,9},... | collective-permute-start | bytes 786440 | tf_op jit(solution)/shard_map/ppermute | solution.py:28
  10.2 11.7 %collective-permute-start.3 = (bf16[256,256]{0,1:T(8,128)(2,1)S(1)}, bf16[256,256]{0,1:T(8,128)(2,1)S(1)}, u32[]{:S(2)}, u32[]{:S(2)}) collective-permute-start(bf16[256,256]{0,1:T(8,128)(2,1)S(1)} %broadcast_select_fusion.2), channel_id=1, source_target_pairs={{8,16},{24,32},{40,48},{56,64},{72,80},{88,96},{104,112},{120,128}... | collective-permute-start | bytes 393224 | tf_op jit(solution)/shard_map/ppermute | solution.py:28
  18.2 3.7 %collective-permute-start.2 = (bf16[256,256]{0,1:T(8,128)(2,1)S(1)}, bf16[256,256]{0,1:T(8,128)(2,1)S(1)}, u32[]{:S(2)}, u32[]{:S(2)}) collective-permute-start(bf16[256,256]{0,1:T(8,128)(2,1)S(1)} %get-tuple-element.5), channel_id=1, source_target_pairs={{0,8},{8,0},{16,24},{24,16},{32,40},{40,32},{48,56},{56,48},{64,72... | collective-permute-start | bytes 393224 | tf_op jit(solution)/shard_map/ppermute | solution.py:27
  26.8 0.9 %copy-start.2 = (s32[4096]{0:T(1024)S(1)}, s32[4096]{0:T(1024)}, u32[]{:S(2)}) copy-start(s32[4096]{0:T(1024)} %param.7) | copy-start | bytes 49156
  29.8 21.7 %all-to-all-start = ((bf16[32,8,256]{2,1,0:T(8,128)(2,1)}), bf16[32,8,256]{2,1,0:T(8,128)(2,1)S(1)}, u32[]{:S(2)}, u32[]{:S(2)}) async-start(bf16[32,8,256]{2,1,0:T(8,128)(2,1)} %fusion.19), calls=%async_computation | async-start | bytes 262144 | tf_op jit(solution)/shard_map/all_to_all | solution.py:102

commit v9 on v8

--- a/solution.py
+++ b/solution.py
@@ -15,12 +15,13 @@
 epsilon = 1e-06
 
 
-def extended(block, sides, width):
+def extended(block, sides, width, edges=None):
     for axis, dim in sides:
         count = lax.axis_size(axis)
         odd = lax.axis_index(axis) % 2 == 1
-        first = lax.slice_in_dim(block, 0, width, axis=dim)
-        last = lax.slice_in_dim(block, block.shape[dim] - width, None, axis=dim)
+        source = block if edges is None else edges
+        first = lax.slice_in_dim(source, 0, width, axis=dim)
+        last = lax.slice_in_dim(source, source.shape[dim] - width, None, axis=dim)
         inner = [(i, i ^ 1) for i in range(count - count % 2)]
         outer = [(i, i + 1) for i in range(1, count - 1, 2)]
         outer = outer + [(target, source) for source, target in outer]
@@ -76,7 +77,11 @@
     real_part = spectra[0].astype(jnp.float32)
     imag_part = spectra[1].astype(jnp.float32)
     power_sum = real_part * real_part + imag_part * imag_part
-    padded_power = extended(power_sum, (("band", 1),), HALF_WIN)
+    edges = jnp.concatenate(
+        [spectra[:, :, :HALF_WIN], spectra[:, :, local_bins - HALF_WIN :]], axis=2
+    ).astype(jnp.float32)
+    edge_power = edges[0] * edges[0] + edges[1] * edges[1]
+    padded_power = extended(power_sum, (("band", 1),), HALF_WIN, edge_power)
     window_sum = exact_dot(padded_power, window_matrix(local_bins, HALF_WIN))
     scaling = lax.rsqrt(window_sum / (2 * HALF_WIN + 1) + epsilon)
     whitened = jnp.concatenate([real_part * scaling, imag_part * scaling], axis=1).astype(

time: 69.1 us -> 69.1 us (level)
    slice x1 -> x0, local copies, waits for them, and re-layouts: 1.08 us -> none  [per_device(): real_part = spectra[0].astype(jnp.float32)]
    unnamed x8 -> x7, local copies, waits for them, and re-layouts: 0.3 us -> 1.26 us
where the time goes in v9:
time: 69.1 us; the launch traced here: 68.8 us
  starting transfers between devices  22.5 us (33%)
  blocking collectives  16.3 us (24%)
  waiting for transfers between devices  12.2 us (18%)
  matrix products  11.8 us (17%)
  other arithmetic  4.53 us (7%)
  local copies, waits for them, and re-layouts  1.26 us (2%)
    all_to_all x1, blocking collectives, per_device(): lax.all_to_all(partial_lags, 'band', split_axis=1, concat_axis=0, tiled=T...  16.3 us
    all_to_all x1, starting transfers between devices, per_device(): lax.all_to_all(local_stack.astype(jnp.bfloat16), 'seg', split_axis=0, con...  11 us
    ppermute x2, starting transfers between devices, extended(): from_outer = lax.ppermute(jnp.where(odd, last, first), axis, outer)  8.68 us
    dot_general x2, matrix products, select_rows(): return jnp.dot(chosen, table, preferred_element_type=jnp.float32)  8.28 us
    all_to_all x1, waiting for transfers between devices, per_device(): lax.all_to_all(local_stack.astype(jnp.bfloat16), 'seg', split_axis=0, con...  8.02 us
    ppermute x2, waiting for transfers between devices, extended(): from_inner = lax.ppermute(jnp.where(odd, first, last), axis, inner)  4.14 us
    another operation x2, other arithmetic  3.37 us
    ppermute x2, starting transfers between devices, extended(): from_inner = lax.ppermute(jnp.where(odd, first, last), axis, inner)  2.82 us
  transfers between devices with their start and end apart: 5, of which 2 were waited for; matrix products, arithmetic and copies ran while one was open for 9% of the time, Pallas kernels for 0%

profile of v9, /device:TPU:1, one launch (start us, length us, event | category | flops | bytes accessed | tf_op | source)
XLA Modules:
  0.0 68.8 jit_solution(18234940261161859406)
XLA Ops:
  0.0 1.2 %copy.5 = bf16[2,1024,128]{1,2,0:T(8,128)(2,1)S(1)} copy(bf16[2,1024,128]{2,1,0:T(8,128)(2,1)} %param.4) | data formatting | bytes 1048576 | tf_op args[0]
  1.3 0.0 copy-start
  1.3 0.0 copy-start.1
  1.3 0.1 convert_element_type.43
  1.4 0.1 fusion.41
  1.5 2.5 %collective-permute-start = (f32[1024,64]{0,1:T(8,128)S(1)}, f32[1024,64]{0,1:T(8,128)S(1)}, u32[]{:S(2)}, u32[]{:S(2)}) collective-permute-start(f32[1024,64]{0,1:T(8,128)S(1)} %get-tuple-element.14), channel_id=1, source_target_pairs={{0,1},{1,0},{2,3},{3,2},{4,5},{5,4},{6,7},{7,6},{8,9},{9,8},{10,11... | collective-permute-start | bytes 786440 | tf_op jit(solution)/shard_map/ppermute | solution.py:28
  4.1 0.7 collective-permute-start.1
  4.8 0.0 copy-done
  4.8 0.0 copy-done.1
  4.8 0.1 fusion.32
  4.9 4.1 %collective-permute-done = f32[1024,64]{0,1:T(8,128)S(1)} collective-permute-done((f32[1024,64]{0,1:T(8,128)S(1)}, f32[1024,64]{0,1:T(8,128)S(1)}, u32[]{:S(2)}, u32[]{:S(2)}) %collective-permute-start) | collective-permute-done | bytes 262176 | tf_op jit(solution)/shard_map/ppermute | solution.py:28
  9.1 0.0 collective-permute-done.1
  9.1 0.3 fusion.39
  9.4 0.3 convolution_add_fusion.1
  9.7 0.4 fusion.33
  10.2 8.0 %collective-permute-start.3 = (bf16[256,256]{0,1:T(8,128)(2,1)S(1)}, bf16[256,256]{0,1:T(8,128)(2,1)S(1)}, u32[]{:S(2)}, u32[]{:S(2)}) collective-permute-start(bf16[256,256]{0,1:T(8,128)(2,1)S(1)} %broadcast_select_fusion.2), channel_id=1, source_target_pairs={{8,16},{24,32},{40,48},{56,64},{72,80},{88,96},{104,112},{120,128}... | collective-permute-start | bytes 393224 | tf_op jit(solution)/shard_map/ppermute | solution.py:29
  18.2 0.3 collective-permute-start.2
  18.5 3.4 %fusion.1 = f32[4096,256]{0,1:T(8,128)S(1)} fusion(s32[4096]{0:T(1024)S(1)} %get-tuple-element.21, bf16[1024,128]{0,1:T(8,128)(2,1)S(1)} %get-tuple-element.11, bf16[1024,128]{0,1:T(8,128)(2,1)S(1)} %get-tuple-element.10), kind=kOutput, calls=%fused_computation.3 | convolution fusion | flops 2152726528 | bytes 4734976 | tf_op jit(solution)/shard_map/dot_general | solution.py:57
  21.8 0.0 collective-permute-done.3
  21.8 0.0 collective-permute-done.2
  21.9 4.9 %fusion = f32[4096,256]{0,1:T(8,128)S(1)} fusion(s32[4096]{0:T(1024)S(1)} %get-tuple-element.20, bf16[256,256]{0,1:T(8,128)(2,1)S(1)} %get-tuple-element.17, bf16[1024,128]{0,1:T(8,128)(2,1)S(1)} %get-tuple-element.11, bf16[1024,128]{0,1:T(8,128)(2,1)S(1)} %get-tuple-element.10, bf16[256,256]{0,1:T(8,128)(2,1)S(1)} %get-tuple-element.16), kind=kOutput, calls=%fused_computation.1 | convolution fusion | flops 3230662656 | bytes 4997120 | tf_op jit(solution)/shard_map/dot_general | solution.py:57
  26.8 0.0 copy-start.2
  26.8 0.9 %add_convert_fusion = (bf16[4096,128]{0,1:T(8,128)(2,1)S(1)}, bf16[4096,128]{0,1:T(8,128)(2,1)S(1)}) fusion(f32[4096,256]{0,1:T(8,128)S(1)} %fusion, f32[4096,256]{0,1:T(8,128)S(1)} %fusion.1), kind=kLoop, calls=%fused_computation.13 | loop fusion | flops 4194304 | bytes 10485760 | tf_op jit(solution)/shard_map/convert.4
  27.7 0.0 copy-done.2
  27.7 2.1 %fusion.19 = bf16[32,8,256]{2,1,0:T(8,128)(2,1)} fusion(bf16[4096,128]{0,1:T(8,128)(2,1)S(1)} %get-tuple-element.9, bf16[4096,128]{0,1:T(8,128)(2,1)S(1)} %get-tuple-element.8, s32[4096]{0:T(1024)S(1)} %copy-done.2), kind=kOutput, calls=%fused_computation.25 | convolution fusion | flops 543227904 | bytes 2244608 | tf_op jit(solution)/shard_map/dot_general | solution.py:104
  29.7 11.0 %all-to-all-start = ((bf16[32,8,256]{2,1,0:T(8,128)(2,1)}), bf16[32,8,256]{2,1,0:T(8,128)(2,1)S(1)}, u32[]{:S(2)}, u32[]{:S(2)}) async-start(bf16[32,8,256]{2,1,0:T(8,128)(2,1)} %fusion.19), calls=%async_computation | async-start | bytes 262144 | tf_op jit(solution)/shard_map/all_to_all | solution.py:107
  40.8 2.5 %multiply_convert_fusion.1 = (bf16[128,1024]{0,1:T(8,128)(2,1)S(1)}, bf16[128,1024]{0,1:T(8,128)(2,1)S(1)}) fusion(s32[1024]{0:T(1024)S(1)} %iota_add_fusion, s32[128]{0:T(128)S(1)} %iota_add_fusion.1), kind=kLoop, calls=%fused_computation.60 | loop fusion | flops 2490368 | bytes 528896 | tf_op jit(solution)/shard_map/convert.2
  43.3 0.1 pad_maximum_fusion.1
  43.4 8.0 %all-to-all-done = bf16[32,8,256]{2,1,0:T(8,128)(2,1)S(1)} async-done(((bf16[32,8,256]{2,1,0:T(8,128)(2,1)}), bf16[32,8,256]{2,1,0:T(8,128)(2,1)S(1)}, u32[]{:S(2)}, u32[]{:S(2)}) %all-to-all-start) | async-done | bytes 131104 | tf_op jit(solution)/shard_map/all_to_all | solution.py:107
  51.4 0.5 fusion.52
  51.9 16.3 %all_to_all.19 = f32[8,8,128]{2,0,1:T(8,128)S(1)} all-to-all(f32[8,8,128]{2,0,1:T(8,128)S(1)} %fusion.52), channel_id=1, replica_groups=mesh['seg'=32,'band'=8] {'band'}, dimensions={1} | all-to-all | bytes 65536 | tf_op jit(solution)/shard_map/all_to_all | solution.py:117
  68.2 0.6 reduce_sum.19
  (10 shorter events, 0.2 us)
Async XLA Ops:
  1.3 3.5 %copy-start = (s32[4096]{0:T(1024)S(1)}, s32[4096]{0:T(1024)}, u32[]{:S(2)}) copy-start(s32[4096]{0:T(1024)} %param.6) | copy-start | bytes 49156
  1.3 3.5 %copy-start.1 = (s32[4096]{0:T(1024)S(1)}, s32[4096]{0:T(1024)}, u32[]{:S(2)}) copy-start(s32[4096]{0:T(1024)} %param.5) | copy-start | bytes 49156
  1.5 7.5 %collective-permute-start = (f32[1024,64]{0,1:T(8,128)S(1)}, f32[1024,64]{0,1:T(8,128)S(1)}, u32[]{:S(2)}, u32[]{:S(2)}) collective-permute-start(f32[1024,64]{0,1:T(8,128)S(1)} %get-tuple-element.14), channel_id=1, source_target_pairs={{0,1},{1,0},{2,3},{3,2},{4,5},{5,4},{6,7},{7,6},{8,9},{9,8},{10,11... | collective-permute-start | bytes 786440 | tf_op jit(solution)/shard_map/ppermute | solution.py:28
  4.1 5.0 %collective-permute-start.1 = (f32[1024,64]{0,1:T(8,128)S(1)}, f32[1024,64]{0,1:T(8,128)S(1)}, u32[]{:S(2)}, u32[]{:S(2)}) collective-permute-start(f32[1024,64]{0,1:T(8,128)S(1)} %get-tuple-element.15), channel_id=1, source_target_pairs={{1,2},{3,4},{5,6},{2,1},{4,3},{6,5},{9,10},{11,12},{13,14},{10,9},... | collective-permute-start | bytes 786440 | tf_op jit(solution)/shard_map/ppermute | solution.py:29
  10.2 11.7 %collective-permute-start.3 = (bf16[256,256]{0,1:T(8,128)(2,1)S(1)}, bf16[256,256]{0,1:T(8,128)(2,1)S(1)}, u32[]{:S(2)}, u32[]{:S(2)}) collective-permute-start(bf16[256,256]{0,1:T(8,128)(2,1)S(1)} %broadcast_select_fusion.2), channel_id=1, source_target_pairs={{8,16},{24,32},{40,48},{56,64},{72,80},{88,96},{104,112},{120,128}... | collective-permute-start | bytes 393224 | tf_op jit(solution)/shard_map/ppermute | solution.py:29
  18.2 3.7 %collective-permute-start.2 = (bf16[256,256]{0,1:T(8,128)(2,1)S(1)}, bf16[256,256]{0,1:T(8,128)(2,1)S(1)}, u32[]{:S(2)}, u32[]{:S(2)}) collective-permute-start(bf16[256,256]{0,1:T(8,128)(2,1)S(1)} %get-tuple-element.5), channel_id=1, source_target_pairs={{0,8},{8,0},{16,24},{24,16},{32,40},{40,32},{48,56},{56,48},{64,72... | collective-permute-start | bytes 393224 | tf_op jit(solution)/shard_map/ppermute | solution.py:28
  26.8 0.9 %copy-start.2 = (s32[4096]{0:T(1024)S(1)}, s32[4096]{0:T(1024)}, u32[]{:S(2)}) copy-start(s32[4096]{0:T(1024)} %param.7) | copy-start | bytes 49156
  29.7 21.6 %all-to-all-start = ((bf16[32,8,256]{2,1,0:T(8,128)(2,1)}), bf16[32,8,256]{2,1,0:T(8,128)(2,1)S(1)}, u32[]{:S(2)}, u32[]{:S(2)}) async-start(bf16[32,8,256]{2,1,0:T(8,128)(2,1)} %fusion.19), calls=%async_computation | async-start | bytes 262144 | tf_op jit(solution)/shard_map/all_to_all | solution.py:107

commit v10 on v8

--- a/solution.py
+++ b/solution.py
@@ -15,7 +15,7 @@
 epsilon = 1e-06
 
 
-def extended(block, sides, width):
+def extended(block, sides, width, wire=None):
     for axis, dim in sides:
         count = lax.axis_size(axis)
         odd = lax.axis_index(axis) % 2 == 1
@@ -24,8 +24,11 @@
         inner = [(i, i ^ 1) for i in range(count - count % 2)]
         outer = [(i, i + 1) for i in range(1, count - 1, 2)]
         outer = outer + [(target, source) for source, target in outer]
-        from_inner = lax.ppermute(jnp.where(odd, first, last), axis, inner)
-        from_outer = lax.ppermute(jnp.where(odd, last, first), axis, outer)
+        wire_type = block.dtype if wire is None else wire
+        from_inner = lax.ppermute(jnp.where(odd, first, last).astype(wire_type), axis, inner)
+        from_outer = lax.ppermute(jnp.where(odd, last, first).astype(wire_type), axis, outer)
+        from_inner = from_inner.astype(block.dtype)
+        from_outer = from_outer.astype(block.dtype)
         low = jnp.where(odd, from_inner, from_outer)
         high = jnp.where(odd, from_outer, from_inner)
         block = jnp.concatenate([low, block, high], axis=dim)
@@ -76,7 +79,7 @@
     real_part = spectra[0].astype(jnp.float32)
     imag_part = spectra[1].astype(jnp.float32)
     power_sum = real_part * real_part + imag_part * imag_part
-    padded_power = extended(power_sum, (("band", 1),), HALF_WIN)
+    padded_power = extended(power_sum, (("band", 1),), HALF_WIN, jnp.bfloat16)
     window_sum = exact_dot(padded_power, window_matrix(local_bins, HALF_WIN))
     scaling = lax.rsqrt(window_sum / (2 * HALF_WIN + 1) + epsilon)
     whitened = jnp.concatenate([real_part * scaling, imag_part * scaling], axis=1).astype(

time: 69.1 us -> 63.6 us (0.920)
  waiting for transfers between devices: 12.3 us -> 9.64 us
  blocking collectives: 16.3 us -> 14.7 us
  starting transfers between devices: 22.5 us -> 21.2 us
    ppermute x4, waiting for transfers between devices: 4.24 us -> 1.62 us  [the longest x2 1.61 us: extended(): lax.ppermute(jnp.where(odd, first, last).astype(wire_type), axis, inner)]
    all_to_all x1, blocking collectives: 16.3 us -> 14.7 us  [per_device(): lax.all_to_all(partial_lags, 'band', split_axis=1, concat_axis=0, tiled=T...]
    ppermute x4, starting transfers between devices: 11.5 us -> 10.3 us  [the longest x2 7.53 us: extended(): lax.ppermute(jnp.where(odd, last, first).astype(wire_type), axis, outer)]
where the time goes in v10:
time: 63.6 us; the launch traced here: 63.3 us
  starting transfers between devices  21.2 us (33%)
  blocking collectives  14.7 us (23%)
  matrix products  11.8 us (19%)
  waiting for transfers between devices  9.64 us (15%)
  other arithmetic  4.34 us (7%)
  local copies, waits for them, and re-layouts  1.38 us (2%)
    all_to_all x1, blocking collectives, per_device(): lax.all_to_all(partial_lags, 'band', split_axis=1, concat_axis=0, tiled=T...  14.7 us
    all_to_all x1, starting transfers between devices, per_device(): lax.all_to_all(local_stack.astype(jnp.bfloat16), 'seg', split_axis=0, con...  10.9 us
    dot_general x2, matrix products, select_rows(): return jnp.dot(chosen, table, preferred_element_type=jnp.float32)  8.27 us
    all_to_all x1, waiting for transfers between devices, per_device(): lax.all_to_all(local_stack.astype(jnp.bfloat16), 'seg', split_axis=0, con...  8.03 us
    ppermute x2, starting transfers between devices, extended(): lax.ppermute(jnp.where(odd, last, first).astype(wire_type), axis, outer)  7.53 us
    another operation x2, other arithmetic  3.37 us
    ppermute x2, starting transfers between devices, extended(): lax.ppermute(jnp.where(odd, first, last).astype(wire_type), axis, inner)  2.82 us
    dot_general x1, matrix products, per_device(): lax.dot_general(members, cross_both, (((0,), (0,)), ((), ())), preferred_...  2.07 us
  transfers between devices with their start and end apart: 5, of which 2 were waited for; matrix products, arithmetic and copies ran while one was open for 9% of the time, Pallas kernels for 0%

profile of v10, /device:TPU:1, one launch (start us, length us, event | category | flops | bytes accessed | tf_op | source)
XLA Modules:
  0.0 63.3 jit_solution(1840170097927932040)
XLA Ops:
  0.0 0.0 copy-start.1
  0.0 0.0 copy-start
  0.0 1.1 %fusion.58 = (bf16[1,1024,128]{2,1,0:T(8,128)(2,1)S(1)}, bf16[1,1024,128]{2,1,0:T(8,128)(2,1)S(1)}) fusion(bf16[2,1024,128]{2,1,0:T(8,128)(2,1)} %param.4), kind=kLoop, calls=%fused_computation.87 | loop fusion | bytes 1048576 | tf_op jit(solution)/shard_map/slice | solution.py:79
  1.1 0.1 copy.7
  1.2 0.1 copy.8
  1.4 0.1 fusion.32
  1.5 2.5 %collective-permute-start = (bf16[1024,64]{0,1:T(8,128)(2,1)S(1)}, bf16[1024,64]{0,1:T(8,128)(2,1)S(1)}, u32[]{:S(2)}, u32[]{:S(2)}) collective-permute-start(bf16[1024,64]{0,1:T(8,128)(2,1)S(1)} %get-tuple-element.12), channel_id=1, source_target_pairs={{0,1},{1,0},{2,3},{3,2},{4,5},{5,4},{6,7},{7,6},{8,9},{9,8},{10,11... | collective-permute-start | bytes 393224 | tf_op jit(solution)/shard_map/ppermute | solution.py:28
  4.1 0.7 %collective-permute-start.1 = (bf16[1024,64]{0,1:T(8,128)(2,1)S(1)}, bf16[1024,64]{0,1:T(8,128)(2,1)S(1)}, u32[]{:S(2)}, u32[]{:S(2)}) collective-permute-start(bf16[1024,64]{0,1:T(8,128)(2,1)S(1)} %get-tuple-element.13), channel_id=1, source_target_pairs={{1,2},{3,4},{5,6},{2,1},{4,3},{6,5},{9,10},{11,12},{13,14},{10,9},... | collective-permute-start | bytes 393224 | tf_op jit(solution)/shard_map/ppermute | solution.py:29
  4.8 0.0 copy-done.1
  4.8 0.0 copy-done
  4.8 1.6 %collective-permute-done = bf16[1024,64]{0,1:T(8,128)(2,1)S(1)} collective-permute-done((bf16[1024,64]{0,1:T(8,128)(2,1)S(1)}, bf16[1024,64]{0,1:T(8,128)(2,1)S(1)}, u32[]{:S(2)}, u32[]{:S(2)}) %collective-permute-start) | collective-permute-done | bytes 131104 | tf_op jit(solution)/shard_map/ppermute | solution.py:28
  6.4 0.0 collective-permute-done.1
  6.5 0.3 fusion.39
  6.8 0.3 convolution_add_fusion.1
  7.1 0.4 fusion.33
  7.6 6.9 %collective-permute-start.3 = (bf16[256,256]{0,1:T(8,128)(2,1)S(1)}, bf16[256,256]{0,1:T(8,128)(2,1)S(1)}, u32[]{:S(2)}, u32[]{:S(2)}) collective-permute-start(bf16[256,256]{0,1:T(8,128)(2,1)S(1)} %broadcast_select_fusion.2), channel_id=1, source_target_pairs={{8,16},{24,32},{40,48},{56,64},{72,80},{88,96},{104,112},{120,128}... | collective-permute-start | bytes 393224 | tf_op jit(solution)/shard_map/ppermute | solution.py:29
  14.4 0.3 collective-permute-start.2
  14.7 3.3 %fusion.1 = f32[4096,256]{0,1:T(8,128)S(1)} fusion(s32[4096]{0:T(1024)S(1)} %get-tuple-element.23, bf16[1024,128]{0,1:T(8,128)(2,1)S(1)} %get-tuple-element.11, bf16[1024,128]{0,1:T(8,128)(2,1)S(1)} %get-tuple-element.10), kind=kOutput, calls=%fused_computation.3 | convolution fusion | flops 2152726528 | bytes 4734976 | tf_op jit(solution)/shard_map/dot_general | solution.py:59
  18.1 0.0 collective-permute-done.3
  18.1 0.0 collective-permute-done.2
  18.1 4.9 %fusion = f32[4096,256]{0,1:T(8,128)S(1)} fusion(s32[4096]{0:T(1024)S(1)} %get-tuple-element.22, bf16[256,256]{0,1:T(8,128)(2,1)S(1)} %get-tuple-element.17, bf16[1024,128]{0,1:T(8,128)(2,1)S(1)} %get-tuple-element.11, bf16[1024,128]{0,1:T(8,128)(2,1)S(1)} %get-tuple-element.10, bf16[256,256]{0,1:T(8,128)(2,1)S(1)} %get-tuple-element.16), kind=kOutput, calls=%fused_computation.1 | convolution fusion | flops 3230662656 | bytes 4997120 | tf_op jit(solution)/shard_map/dot_general | solution.py:59
  23.0 0.0 copy-start.2
  23.1 0.9 %add_convert_fusion = (bf16[4096,128]{0,1:T(8,128)(2,1)S(1)}, bf16[4096,128]{0,1:T(8,128)(2,1)S(1)}) fusion(f32[4096,256]{0,1:T(8,128)S(1)} %fusion, f32[4096,256]{0,1:T(8,128)S(1)} %fusion.1), kind=kLoop, calls=%fused_computation.13 | loop fusion | flops 4194304 | bytes 10485760 | tf_op jit(solution)/shard_map/convert.4
  23.9 0.0 copy-done.2
  23.9 2.1 %fusion.19 = bf16[32,8,256]{2,1,0:T(8,128)(2,1)} fusion(bf16[4096,128]{0,1:T(8,128)(2,1)S(1)} %get-tuple-element.9, bf16[4096,128]{0,1:T(8,128)(2,1)S(1)} %get-tuple-element.8, s32[4096]{0:T(1024)S(1)} %copy-done.2), kind=kOutput, calls=%fused_computation.25 | convolution fusion | flops 543227904 | bytes 2244608 | tf_op jit(solution)/shard_map/dot_general | solution.py:102
  26.0 10.9 %all-to-all-start = ((bf16[32,8,256]{2,1,0:T(8,128)(2,1)}), bf16[32,8,256]{2,1,0:T(8,128)(2,1)S(1)}, u32[]{:S(2)}, u32[]{:S(2)}) async-start(bf16[32,8,256]{2,1,0:T(8,128)(2,1)} %fusion.19), calls=%async_computation | async-start | bytes 262144 | tf_op jit(solution)/shard_map/all_to_all | solution.py:105
  36.9 2.5 %multiply_convert_fusion.1 = (bf16[128,1024]{0,1:T(8,128)(2,1)S(1)}, bf16[128,1024]{0,1:T(8,128)(2,1)S(1)}) fusion(s32[1024]{0:T(1024)S(1)} %iota_add_fusion, s32[128]{0:T(128)S(1)} %iota_add_fusion.1), kind=kLoop, calls=%fused_computation.56 | loop fusion | flops 2490368 | bytes 528896 | tf_op jit(solution)/shard_map/convert.2
  39.4 0.1 pad_maximum_fusion.1
  39.5 8.0 %all-to-all-done = bf16[32,8,256]{2,1,0:T(8,128)(2,1)S(1)} async-done(((bf16[32,8,256]{2,1,0:T(8,128)(2,1)}), bf16[32,8,256]{2,1,0:T(8,128)(2,1)S(1)}, u32[]{:S(2)}, u32[]{:S(2)}) %all-to-all-start) | async-done | bytes 131104 | tf_op jit(solution)/shard_map/all_to_all | solution.py:105
  47.5 0.5 fusion.50
  48.0 14.7 %all_to_all.19 = f32[8,8,128]{2,0,1:T(8,128)S(1)} all-to-all(f32[8,8,128]{2,0,1:T(8,128)S(1)} %fusion.50), channel_id=1, replica_groups=mesh['seg'=32,'band'=8] {'band'}, dimensions={1} | all-to-all | bytes 65536 | tf_op jit(solution)/shard_map/all_to_all | solution.py:115
  62.7 0.6 reduce_sum.19
  (10 shorter events, 0.2 us)
Async XLA Ops:
  0.0 4.8 %copy-start.1 = (s32[4096]{0:T(1024)S(1)}, s32[4096]{0:T(1024)}, u32[]{:S(2)}) copy-start(s32[4096]{0:T(1024)} %param.5) | copy-start | bytes 49156
  0.0 4.8 %copy-start = (s32[4096]{0:T(1024)S(1)}, s32[4096]{0:T(1024)}, u32[]{:S(2)}) copy-start(s32[4096]{0:T(1024)} %param.6) | copy-start | bytes 49156
  1.5 4.9 %collective-permute-start = (bf16[1024,64]{0,1:T(8,128)(2,1)S(1)}, bf16[1024,64]{0,1:T(8,128)(2,1)S(1)}, u32[]{:S(2)}, u32[]{:S(2)}) collective-permute-start(bf16[1024,64]{0,1:T(8,128)(2,1)S(1)} %get-tuple-element.12), channel_id=1, source_target_pairs={{0,1},{1,0},{2,3},{3,2},{4,5},{5,4},{6,7},{7,6},{8,9},{9,8},{10,11... | collective-permute-start | bytes 393224 | tf_op jit(solution)/shard_map/ppermute | solution.py:28
  4.1 2.4 %collective-permute-start.1 = (bf16[1024,64]{0,1:T(8,128)(2,1)S(1)}, bf16[1024,64]{0,1:T(8,128)(2,1)S(1)}, u32[]{:S(2)}, u32[]{:S(2)}) collective-permute-start(bf16[1024,64]{0,1:T(8,128)(2,1)S(1)} %get-tuple-element.13), channel_id=1, source_target_pairs={{1,2},{3,4},{5,6},{2,1},{4,3},{6,5},{9,10},{11,12},{13,14},{10,9},... | collective-permute-start | bytes 393224 | tf_op jit(solution)/shard_map/ppermute | solution.py:29
  7.6 10.5 %collective-permute-start.3 = (bf16[256,256]{0,1:T(8,128)(2,1)S(1)}, bf16[256,256]{0,1:T(8,128)(2,1)S(1)}, u32[]{:S(2)}, u32[]{:S(2)}) collective-permute-start(bf16[256,256]{0,1:T(8,128)(2,1)S(1)} %broadcast_select_fusion.2), channel_id=1, source_target_pairs={{8,16},{24,32},{40,48},{56,64},{72,80},{88,96},{104,112},{120,128}... | collective-permute-start | bytes 393224 | tf_op jit(solution)/shard_map/ppermute | solution.py:29
  14.4 3.6 %collective-permute-start.2 = (bf16[256,256]{0,1:T(8,128)(2,1)S(1)}, bf16[256,256]{0,1:T(8,128)(2,1)S(1)}, u32[]{:S(2)}, u32[]{:S(2)}) collective-permute-start(bf16[256,256]{0,1:T(8,128)(2,1)S(1)} %get-tuple-element.5), channel_id=1, source_target_pairs={{0,8},{8,0},{16,24},{24,16},{32,40},{40,32},{48,56},{56,48},{64,72... | collective-permute-start | bytes 393224 | tf_op jit(solution)/shard_map/ppermute | solution.py:28
  23.0 0.9 %copy-start.2 = (s32[4096]{0:T(1024)S(1)}, s32[4096]{0:T(1024)}, u32[]{:S(2)}) copy-start(s32[4096]{0:T(1024)} %param.7) | copy-start | bytes 49156
  26.0 21.5 %all-to-all-start = ((bf16[32,8,256]{2,1,0:T(8,128)(2,1)}), bf16[32,8,256]{2,1,0:T(8,128)(2,1)S(1)}, u32[]{:S(2)}, u32[]{:S(2)}) async-start(bf16[32,8,256]{2,1,0:T(8,128)(2,1)} %fusion.19), calls=%async_computation | async-start | bytes 262144 | tf_op jit(solution)/shard_map/all_to_all | solution.py:105

commit v11 on v10

--- a/solution.py
+++ b/solution.py
@@ -80,6 +80,8 @@
     imag_part = spectra[1].astype(jnp.float32)
     power_sum = real_part * real_part + imag_part * imag_part
     padded_power = extended(power_sum, (("band", 1),), HALF_WIN, jnp.bfloat16)
+    table = lag_table(band_position * local_bins, local_bins, FREQ, LAGS)
+    padded_power, table = lax.optimization_barrier((padded_power, table))
     window_sum = exact_dot(padded_power, window_matrix(local_bins, HALF_WIN))
     scaling = lax.rsqrt(window_sum / (2 * HALF_WIN + 1) + epsilon)
     whitened = jnp.concatenate([real_part * scaling, imag_part * scaling], axis=1).astype(
@@ -108,7 +110,6 @@
     stack = jnp.sum(
         gathered.reshape(segments, OB_DEV, 2 * local_bins).astype(jnp.float32), axis=0
     )
-    table = lag_table(band_position * local_bins, local_bins, FREQ, LAGS)
     partial_lags = jnp.dot(
         stack, table.astype(jnp.float32), precision=lax.Precision.HIGHEST
     )

time: 63.6 us -> 62.7 us (0.986)
  blocking collectives: 14.7 us -> 35.9 us
  starting transfers between devices: 21.2 us -> 9.34 us
  waiting for transfers between devices: 9.64 us -> 0.01 us
  matrix products: 11.8 us -> 11.1 us
    all_to_all x0 -> x1, blocking collectives: none -> 21.3 us  [per_device(): lax.all_to_all(local_stack.astype(jnp.bfloat16), 'seg', split_axis=0, con...]
    all_to_all x1 -> x0, starting transfers between devices: 10.9 us -> none  [per_device(): lax.all_to_all(local_stack.astype(jnp.bfloat16), 'seg', split_axis=0, con...]
    all_to_all x1 -> x0, waiting for transfers between devices: 8.03 us -> none  [per_device(): lax.all_to_all(local_stack.astype(jnp.bfloat16), 'seg', split_axis=0, con...]
    ppermute x2, waiting for transfers between devices: 1.61 us -> 0.01 us  [extended(): lax.ppermute(jnp.where(odd, first, last).astype(wire_type), axis, inner)]
    ppermute x2, starting transfers between devices: 7.53 us -> 6.53 us  [extended(): lax.ppermute(jnp.where(odd, last, first).astype(wire_type), axis, outer)]
    dot_general x1, matrix products: 2.07 us -> 1.42 us  [per_device(): lax.dot_general(members, cross_both, (((0,), (0,)), ((), ())), preferred_...]
  transfers between devices with their start and end apart: 5 -> 4, of which waited for: 2 -> 0; matrix products, arithmetic and copies ran while one was open for 9% -> 10% of each run, Pallas kernels for 0% -> 0%
where the time goes in v11:
time: 62.7 us; the launch traced here: 62.5 us
  blocking collectives  35.9 us (57%)
  matrix products  11.1 us (18%)
  starting transfers between devices  9.34 us (15%)
  other arithmetic  4.44 us (7%)
  local copies, waits for them, and re-layouts  1.38 us (2%)
    all_to_all x1, blocking collectives, per_device(): lax.all_to_all(local_stack.astype(jnp.bfloat16), 'seg', split_axis=0, con...  21.3 us
    all_to_all x1, blocking collectives, per_device(): lax.all_to_all(partial_lags, 'band', split_axis=1, concat_axis=0, tiled=T...  14.7 us
    dot_general x2, matrix products, select_rows(): return jnp.dot(chosen, table, preferred_element_type=jnp.float32)  8.28 us
    ppermute x2, starting transfers between devices, extended(): lax.ppermute(jnp.where(odd, last, first).astype(wire_type), axis, outer)  6.53 us
    another operation x2, other arithmetic  3.37 us
    ppermute x2, starting transfers between devices, extended(): lax.ppermute(jnp.where(odd, first, last).astype(wire_type), axis, inner)  2.82 us
    dot_general x1, matrix products, per_device(): lax.dot_general(members, cross_both, (((0,), (0,)), ((), ())), preferred_...  1.42 us
  transfers between devices with their start and end apart: 4, of which 0 were waited for; matrix products, arithmetic and copies ran while one was open for 10% of the time, Pallas kernels for 0%

profile of v11, /device:TPU:1, one launch (start us, length us, event | category | flops | bytes accessed | tf_op | source)
XLA Modules:
  0.0 62.5 jit_solution(18089841799273422544)
XLA Ops:
  0.0 0.0 copy-start
  0.0 0.0 copy-start.1
  0.0 1.1 %fusion.55 = (bf16[1,1024,128]{2,1,0:T(8,128)(2,1)S(1)}, bf16[1,1024,128]{2,1,0:T(8,128)(2,1)S(1)}) fusion(bf16[2,1024,128]{2,1,0:T(8,128)(2,1)} %param.4), kind=kLoop, calls=%fused_computation.84 | loop fusion | bytes 1048576 | tf_op jit(solution)/shard_map/slice | solution.py:79
  1.1 0.1 copy.7
  1.2 0.1 copy.8
  1.4 0.1 fusion.32
  1.5 2.5 %collective-permute-start = (bf16[1024,64]{0,1:T(8,128)(2,1)S(1)}, bf16[1024,64]{0,1:T(8,128)(2,1)S(1)}, u32[]{:S(2)}, u32[]{:S(2)}) collective-permute-start(bf16[1024,64]{0,1:T(8,128)(2,1)S(1)} %get-tuple-element.16), channel_id=1, source_target_pairs={{0,1},{1,0},{2,3},{3,2},{4,5},{5,4},{6,7},{7,6},{8,9},{9,8},{10,11... | collective-permute-start | bytes 393224 | tf_op jit(solution)/shard_map/ppermute | solution.py:28
  4.1 0.7 %collective-permute-start.1 = (bf16[1024,64]{0,1:T(8,128)(2,1)S(1)}, bf16[1024,64]{0,1:T(8,128)(2,1)S(1)}, u32[]{:S(2)}, u32[]{:S(2)}) collective-permute-start(bf16[1024,64]{0,1:T(8,128)(2,1)S(1)} %get-tuple-element.17), channel_id=1, source_target_pairs={{1,2},{3,4},{5,6},{2,1},{4,3},{6,5},{9,10},{11,12},{13,14},{10,9},... | collective-permute-start | bytes 393224 | tf_op jit(solution)/shard_map/ppermute | solution.py:29
  4.8 2.5 %multiply_convert_fusion.1 = (bf16[128,1024]{0,1:T(8,128)(2,1)S(1)}, bf16[128,1024]{0,1:T(8,128)(2,1)S(1)}) fusion(s32[1024]{0:T(1024)S(1)} %iota_add_fusion, s32[128]{0:T(128)S(1)} %iota_add_fusion.2), kind=kLoop, calls=%fused_computation.56 | loop fusion | flops 2490368 | bytes 528896 | tf_op jit(solution)/shard_map/convert.6
  7.3 0.0 copy-done
  7.3 0.0 copy-done.1
  7.4 0.1 pad_maximum_fusion.1
  7.4 0.0 collective-permute-done
  7.4 0.0 collective-permute-done.1
  7.5 0.1 pad_maximum_fusion
  7.6 0.3 fusion.39
  7.9 0.3 convolution_add_fusion.1
  8.2 0.4 fusion.33
  8.6 5.9 %collective-permute-start.3 = (bf16[256,256]{0,1:T(8,128)(2,1)S(1)}, bf16[256,256]{0,1:T(8,128)(2,1)S(1)}, u32[]{:S(2)}, u32[]{:S(2)}) collective-permute-start(bf16[256,256]{0,1:T(8,128)(2,1)S(1)} %broadcast_select_fusion.2), channel_id=1, source_target_pairs={{8,16},{24,32},{40,48},{56,64},{72,80},{88,96},{104,112},{120,128}... | collective-permute-start | bytes 393224 | tf_op jit(solution)/shard_map/ppermute | solution.py:29
  14.5 0.3 collective-permute-start.2
  14.8 3.4 %fusion.1 = f32[4096,256]{0,1:T(8,128)S(1)} fusion(s32[4096]{0:T(1024)S(1)} %get-tuple-element.27, bf16[1024,128]{0,1:T(8,128)(2,1)S(1)} %get-tuple-element.15, bf16[1024,128]{0,1:T(8,128)(2,1)S(1)} %get-tuple-element.14), kind=kOutput, calls=%fused_computation.3 | convolution fusion | flops 2152726528 | bytes 4734976 | tf_op jit(solution)/shard_map/dot_general | solution.py:59
  18.2 0.0 collective-permute-done.3
  18.2 0.0 collective-permute-done.2
  18.2 4.9 %fusion = f32[4096,256]{0,1:T(8,128)S(1)} fusion(s32[4096]{0:T(1024)S(1)} %get-tuple-element.26, bf16[256,256]{0,1:T(8,128)(2,1)S(1)} %get-tuple-element.21, bf16[1024,128]{0,1:T(8,128)(2,1)S(1)} %get-tuple-element.15, bf16[1024,128]{0,1:T(8,128)(2,1)S(1)} %get-tuple-element.14, bf16[256,256]{0,1:T(8,128)(2,1)S(1)} %get-tuple-element.20), kind=kOutput, calls=%fused_computation.1 | convolution fusion | flops 3230662656 | bytes 4997120 | tf_op jit(solution)/shard_map/dot_general | solution.py:59
  23.1 0.0 copy-start.2
  23.2 0.9 %add_convert_fusion = (bf16[4096,128]{0,1:T(8,128)(2,1)S(1)}, bf16[4096,128]{0,1:T(8,128)(2,1)S(1)}) fusion(f32[4096,256]{0,1:T(8,128)S(1)} %fusion, f32[4096,256]{0,1:T(8,128)S(1)} %fusion.1), kind=kLoop, calls=%fused_computation.13 | loop fusion | flops 4194304 | bytes 10485760 | tf_op jit(solution)/shard_map/convert.2
  24.0 0.0 copy-done.2
  24.0 1.4 %fusion.19 = bf16[32,8,256]{2,1,0:T(8,128)(2,1)S(1)} fusion(bf16[4096,128]{0,1:T(8,128)(2,1)S(1)} %get-tuple-element.13, bf16[4096,128]{0,1:T(8,128)(2,1)S(1)} %get-tuple-element.12, s32[4096]{0:T(1024)S(1)} %copy-done.2), kind=kOutput, calls=%fused_computation.25 | convolution fusion | flops 543227904 | bytes 2244608 | tf_op jit(solution)/shard_map/dot_general | solution.py:104
  25.5 21.3 %all_to_all.19 = bf16[32,8,256]{2,1,0:T(8,128)(2,1)S(1)} all-to-all(bf16[32,8,256]{2,1,0:T(8,128)(2,1)S(1)} %fusion.19), channel_id=1, replica_groups=mesh['seg'=32,'band'=8] {'seg'}, dimensions={0} | all-to-all | bytes 262144 | tf_op jit(solution)/shard_map/all_to_all | solution.py:107
  46.7 0.5 fusion.50
  47.3 14.7 %all_to_all.20 = f32[8,8,128]{2,0,1:T(8,128)S(1)} all-to-all(f32[8,8,128]{2,0,1:T(8,128)S(1)} %fusion.50), channel_id=1, replica_groups=mesh['seg'=32,'band'=8] {'band'}, dimensions={1} | all-to-all | bytes 65536 | tf_op jit(solution)/shard_map/all_to_all | solution.py:116
  61.9 0.6 reduce_sum.19
  (10 shorter events, 0.2 us)
Async XLA Ops:
  0.0 7.3 %copy-start = (s32[4096]{0:T(1024)S(1)}, s32[4096]{0:T(1024)}, u32[]{:S(2)}) copy-start(s32[4096]{0:T(1024)} %param.6) | copy-start | bytes 49156
  0.0 7.3 %copy-start.1 = (s32[4096]{0:T(1024)S(1)}, s32[4096]{0:T(1024)}, u32[]{:S(2)}) copy-start(s32[4096]{0:T(1024)} %param.5) | copy-start | bytes 49156
  1.5 5.9 %collective-permute-start = (bf16[1024,64]{0,1:T(8,128)(2,1)S(1)}, bf16[1024,64]{0,1:T(8,128)(2,1)S(1)}, u32[]{:S(2)}, u32[]{:S(2)}) collective-permute-start(bf16[1024,64]{0,1:T(8,128)(2,1)S(1)} %get-tuple-element.16), channel_id=1, source_target_pairs={{0,1},{1,0},{2,3},{3,2},{4,5},{5,4},{6,7},{7,6},{8,9},{9,8},{10,11... | collective-permute-start | bytes 393224 | tf_op jit(solution)/shard_map/ppermute | solution.py:28
  4.1 3.4 %collective-permute-start.1 = (bf16[1024,64]{0,1:T(8,128)(2,1)S(1)}, bf16[1024,64]{0,1:T(8,128)(2,1)S(1)}, u32[]{:S(2)}, u32[]{:S(2)}) collective-permute-start(bf16[1024,64]{0,1:T(8,128)(2,1)S(1)} %get-tuple-element.17), channel_id=1, source_target_pairs={{1,2},{3,4},{5,6},{2,1},{4,3},{6,5},{9,10},{11,12},{13,14},{10,9},... | collective-permute-start | bytes 393224 | tf_op jit(solution)/shard_map/ppermute | solution.py:29
  8.6 9.5 %collective-permute-start.3 = (bf16[256,256]{0,1:T(8,128)(2,1)S(1)}, bf16[256,256]{0,1:T(8,128)(2,1)S(1)}, u32[]{:S(2)}, u32[]{:S(2)}) collective-permute-start(bf16[256,256]{0,1:T(8,128)(2,1)S(1)} %broadcast_select_fusion.2), channel_id=1, source_target_pairs={{8,16},{24,32},{40,48},{56,64},{72,80},{88,96},{104,112},{120,128}... | collective-permute-start | bytes 393224 | tf_op jit(solution)/shard_map/ppermute | solution.py:29
  14.5 3.7 %collective-permute-start.2 = (bf16[256,256]{0,1:T(8,128)(2,1)S(1)}, bf16[256,256]{0,1:T(8,128)(2,1)S(1)}, u32[]{:S(2)}, u32[]{:S(2)}) collective-permute-start(bf16[256,256]{0,1:T(8,128)(2,1)S(1)} %get-tuple-element.9), channel_id=1, source_target_pairs={{0,8},{8,0},{16,24},{24,16},{32,40},{40,32},{48,56},{56,48},{64,72... | collective-permute-start | bytes 393224 | tf_op jit(solution)/shard_map/ppermute | solution.py:28
  23.1 0.9 %copy-start.2 = (s32[4096]{0:T(1024)S(1)}, s32[4096]{0:T(1024)}, u32[]{:S(2)}) copy-start(s32[4096]{0:T(1024)} %param.7) | copy-start | bytes 49156

commit v12 on v11

--- a/solution.py
+++ b/solution.py
@@ -15,12 +15,13 @@
 epsilon = 1e-06
 
 
-def extended(block, sides, width, wire=None):
+def extended(block, sides, width, wire=None, edges=None):
     for axis, dim in sides:
         count = lax.axis_size(axis)
         odd = lax.axis_index(axis) % 2 == 1
-        first = lax.slice_in_dim(block, 0, width, axis=dim)
-        last = lax.slice_in_dim(block, block.shape[dim] - width, None, axis=dim)
+        source = block if edges is None else edges
+        first = lax.slice_in_dim(source, 0, width, axis=dim)
+        last = lax.slice_in_dim(source, source.shape[dim] - width, None, axis=dim)
         inner = [(i, i ^ 1) for i in range(count - count % 2)]
         outer = [(i, i + 1) for i in range(1, count - 1, 2)]
         outer = outer + [(target, source) for source, target in outer]
@@ -79,7 +80,11 @@
     real_part = spectra[0].astype(jnp.float32)
     imag_part = spectra[1].astype(jnp.float32)
     power_sum = real_part * real_part + imag_part * imag_part
-    padded_power = extended(power_sum, (("band", 1),), HALF_WIN, jnp.bfloat16)
+    edges = jnp.concatenate(
+        [spectra[:, :, :HALF_WIN], spectra[:, :, local_bins - HALF_WIN :]], axis=2
+    ).astype(jnp.float32)
+    edge_power = edges[0] * edges[0] + edges[1] * edges[1]
+    padded_power = extended(power_sum, (("band", 1),), HALF_WIN, jnp.bfloat16, edge_power)
     table = lag_table(band_position * local_bins, local_bins, FREQ, LAGS)
     padded_power, table = lax.optimization_barrier((padded_power, table))
     window_sum = exact_dot(padded_power, window_matrix(local_bins, HALF_WIN))

time: 62.7 us -> 62.8 us (level)
    slice x1 -> x0, local copies, waits for them, and re-layouts: 1.08 us -> none  [per_device(): real_part = spectra[0].astype(jnp.float32)]
    unnamed x8 -> x7, local copies, waits for them, and re-layouts: 0.3 us -> 1.26 us
where the time goes in v12:
time: 62.8 us; the launch traced here: 62.5 us
  blocking collectives  35.9 us (57%)
  matrix products  11.1 us (18%)
  starting transfers between devices  9.24 us (15%)
  other arithmetic  4.6 us (7%)
  local copies, waits for them, and re-layouts  1.26 us (2%)
    all_to_all x1, blocking collectives, per_device(): lax.all_to_all(local_stack.astype(jnp.bfloat16), 'seg', split_axis=0, con...  21.3 us
    all_to_all x1, blocking collectives, per_device(): lax.all_to_all(partial_lags, 'band', split_axis=1, concat_axis=0, tiled=T...  14.7 us
    dot_general x2, matrix products, select_rows(): return jnp.dot(chosen, table, preferred_element_type=jnp.float32)  8.28 us
    ppermute x2, starting transfers between devices, extended(): lax.ppermute(jnp.where(odd, last, first).astype(wire_type), axis, outer)  6.43 us
    another operation x2, other arithmetic  3.37 us
    ppermute x2, starting transfers between devices, extended(): lax.ppermute(jnp.where(odd, first, last).astype(wire_type), axis, inner)  2.82 us
    dot_general x1, matrix products, per_device(): lax.dot_general(members, cross_both, (((0,), (0,)), ((), ())), preferred_...  1.42 us
    unnamed x7, local copies, waits for them, and re-layouts  1.26 us
  transfers between devices with their start and end apart: 4, of which 0 were waited for; matrix products, arithmetic and copies ran while one was open for 10% of the time, Pallas kernels for 0%

profile of v12, /device:TPU:1, one launch (start us, length us, event | category | flops | bytes accessed | tf_op | source)
XLA Modules:
  0.0 62.5 jit_solution(18295081320419466246)
XLA Ops:
  0.0 1.2 %copy.5 = bf16[2,1024,128]{1,2,0:T(8,128)(2,1)S(1)} copy(bf16[2,1024,128]{2,1,0:T(8,128)(2,1)} %param.4) | data formatting | bytes 1048576 | tf_op args[0]
  1.3 0.1 convert_element_type.55
  1.4 0.0 copy-start
  1.4 0.0 copy-start.1
  1.4 0.1 fusion.41
  1.5 2.5 %collective-permute-start = (bf16[1024,64]{0,1:T(8,128)(2,1)S(1)}, bf16[1024,64]{0,1:T(8,128)(2,1)S(1)}, u32[]{:S(2)}, u32[]{:S(2)}) collective-permute-start(bf16[1024,64]{0,1:T(8,128)(2,1)S(1)} %get-tuple-element.20), channel_id=1, source_target_pairs={{0,1},{1,0},{2,3},{3,2},{4,5},{5,4},{6,7},{7,6},{8,9},{9,8},{10,11... | collective-permute-start | bytes 393224 | tf_op jit(solution)/shard_map/ppermute | solution.py:29
  4.0 0.7 %collective-permute-start.1 = (bf16[1024,64]{0,1:T(8,128)(2,1)S(1)}, bf16[1024,64]{0,1:T(8,128)(2,1)S(1)}, u32[]{:S(2)}, u32[]{:S(2)}) collective-permute-start(bf16[1024,64]{0,1:T(8,128)(2,1)S(1)} %get-tuple-element.21), channel_id=1, source_target_pairs={{1,2},{3,4},{5,6},{2,1},{4,3},{6,5},{9,10},{11,12},{13,14},{10,9},... | collective-permute-start | bytes 393224 | tf_op jit(solution)/shard_map/ppermute | solution.py:30
  4.7 0.1 fusion.32
  4.8 2.5 %multiply_convert_fusion.1 = (bf16[128,1024]{0,1:T(8,128)(2,1)S(1)}, bf16[128,1024]{0,1:T(8,128)(2,1)S(1)}) fusion(s32[1024]{0:T(1024)S(1)} %iota_add_fusion, s32[128]{0:T(128)S(1)} %iota_add_fusion.2), kind=kLoop, calls=%fused_computation.60 | loop fusion | flops 2490368 | bytes 528896 | tf_op jit(solution)/shard_map/convert.6
  7.4 0.0 copy-done
  7.4 0.0 copy-done.1
  7.4 0.1 pad_maximum_fusion.1
  7.5 0.0 collective-permute-done
  7.5 0.0 collective-permute-done.1
  7.6 0.1 pad_maximum_fusion
  7.7 0.3 fusion.39
  7.9 0.3 convolution_add_fusion.1
  8.2 0.4 fusion.33
  8.7 5.8 %collective-permute-start.3 = (bf16[256,256]{0,1:T(8,128)(2,1)S(1)}, bf16[256,256]{0,1:T(8,128)(2,1)S(1)}, u32[]{:S(2)}, u32[]{:S(2)}) collective-permute-start(bf16[256,256]{0,1:T(8,128)(2,1)S(1)} %broadcast_select_fusion.2), channel_id=1, source_target_pairs={{8,16},{24,32},{40,48},{56,64},{72,80},{88,96},{104,112},{120,128}... | collective-permute-start | bytes 393224 | tf_op jit(solution)/shard_map/ppermute | solution.py:30
  14.5 0.3 collective-permute-start.2
  14.8 3.4 %fusion.1 = f32[4096,256]{0,1:T(8,128)S(1)} fusion(s32[4096]{0:T(1024)S(1)} %get-tuple-element.25, bf16[1024,128]{0,1:T(8,128)(2,1)S(1)} %get-tuple-element.15, bf16[1024,128]{0,1:T(8,128)(2,1)S(1)} %get-tuple-element.14), kind=kOutput, calls=%fused_computation.3 | convolution fusion | flops 2152726528 | bytes 4734976 | tf_op jit(solution)/shard_map/dot_general | solution.py:60
  18.1 0.0 collective-permute-done.3
  18.1 0.0 collective-permute-done.2
  18.2 4.9 %fusion = f32[4096,256]{0,1:T(8,128)S(1)} fusion(s32[4096]{0:T(1024)S(1)} %get-tuple-element.24, bf16[256,256]{0,1:T(8,128)(2,1)S(1)} %get-tuple-element.17, bf16[1024,128]{0,1:T(8,128)(2,1)S(1)} %get-tuple-element.15, bf16[1024,128]{0,1:T(8,128)(2,1)S(1)} %get-tuple-element.14, bf16[256,256]{0,1:T(8,128)(2,1)S(1)} %get-tuple-element.16), kind=kOutput, calls=%fused_computation.1 | convolution fusion | flops 3230662656 | bytes 4997120 | tf_op jit(solution)/shard_map/dot_general | solution.py:60
  23.1 0.0 copy-start.2
  23.1 0.9 %add_convert_fusion = (bf16[4096,128]{0,1:T(8,128)(2,1)S(1)}, bf16[4096,128]{0,1:T(8,128)(2,1)S(1)}) fusion(f32[4096,256]{0,1:T(8,128)S(1)} %fusion, f32[4096,256]{0,1:T(8,128)S(1)} %fusion.1), kind=kLoop, calls=%fused_computation.13 | loop fusion | flops 4194304 | bytes 10485760 | tf_op jit(solution)/shard_map/convert.2
  24.0 0.0 copy-done.2
  24.0 1.4 %fusion.19 = bf16[32,8,256]{2,1,0:T(8,128)(2,1)S(1)} fusion(bf16[4096,128]{0,1:T(8,128)(2,1)S(1)} %get-tuple-element.13, bf16[4096,128]{0,1:T(8,128)(2,1)S(1)} %get-tuple-element.12, s32[4096]{0:T(1024)S(1)} %copy-done.2), kind=kOutput, calls=%fused_computation.25 | convolution fusion | flops 543227904 | bytes 2244608 | tf_op jit(solution)/shard_map/dot_general | solution.py:109
  25.4 21.3 %all_to_all.19 = bf16[32,8,256]{2,1,0:T(8,128)(2,1)S(1)} all-to-all(bf16[32,8,256]{2,1,0:T(8,128)(2,1)S(1)} %fusion.19), channel_id=1, replica_groups=mesh['seg'=32,'band'=8] {'seg'}, dimensions={0} | all-to-all | bytes 262144 | tf_op jit(solution)/shard_map/all_to_all | solution.py:112
  46.7 0.5 fusion.52
  47.2 14.7 %all_to_all.20 = f32[8,8,128]{2,0,1:T(8,128)S(1)} all-to-all(f32[8,8,128]{2,0,1:T(8,128)S(1)} %fusion.52), channel_id=1, replica_groups=mesh['seg'=32,'band'=8] {'band'}, dimensions={1} | all-to-all | bytes 65536 | tf_op jit(solution)/shard_map/all_to_all | solution.py:121
  61.9 0.6 reduce_sum.19
  (10 shorter events, 0.2 us)
Async XLA Ops:
  1.4 6.0 %copy-start = (s32[4096]{0:T(1024)S(1)}, s32[4096]{0:T(1024)}, u32[]{:S(2)}) copy-start(s32[4096]{0:T(1024)} %param.6) | copy-start | bytes 49156
  1.4 6.0 %copy-start.1 = (s32[4096]{0:T(1024)S(1)}, s32[4096]{0:T(1024)}, u32[]{:S(2)}) copy-start(s32[4096]{0:T(1024)} %param.5) | copy-start | bytes 49156
  1.5 6.0 %collective-permute-start = (bf16[1024,64]{0,1:T(8,128)(2,1)S(1)}, bf16[1024,64]{0,1:T(8,128)(2,1)S(1)}, u32[]{:S(2)}, u32[]{:S(2)}) collective-permute-start(bf16[1024,64]{0,1:T(8,128)(2,1)S(1)} %get-tuple-element.20), channel_id=1, source_target_pairs={{0,1},{1,0},{2,3},{3,2},{4,5},{5,4},{6,7},{7,6},{8,9},{9,8},{10,11... | collective-permute-start | bytes 393224 | tf_op jit(solution)/shard_map/ppermute | solution.py:29
  4.0 3.5 %collective-permute-start.1 = (bf16[1024,64]{0,1:T(8,128)(2,1)S(1)}, bf16[1024,64]{0,1:T(8,128)(2,1)S(1)}, u32[]{:S(2)}, u32[]{:S(2)}) collective-permute-start(bf16[1024,64]{0,1:T(8,128)(2,1)S(1)} %get-tuple-element.21), channel_id=1, source_target_pairs={{1,2},{3,4},{5,6},{2,1},{4,3},{6,5},{9,10},{11,12},{13,14},{10,9},... | collective-permute-start | bytes 393224 | tf_op jit(solution)/shard_map/ppermute | solution.py:30
  8.7 9.4 %collective-permute-start.3 = (bf16[256,256]{0,1:T(8,128)(2,1)S(1)}, bf16[256,256]{0,1:T(8,128)(2,1)S(1)}, u32[]{:S(2)}, u32[]{:S(2)}) collective-permute-start(bf16[256,256]{0,1:T(8,128)(2,1)S(1)} %broadcast_select_fusion.2), channel_id=1, source_target_pairs={{8,16},{24,32},{40,48},{56,64},{72,80},{88,96},{104,112},{120,128}... | collective-permute-start | bytes 393224 | tf_op jit(solution)/shard_map/ppermute | solution.py:30
  14.5 3.7 %collective-permute-start.2 = (bf16[256,256]{0,1:T(8,128)(2,1)S(1)}, bf16[256,256]{0,1:T(8,128)(2,1)S(1)}, u32[]{:S(2)}, u32[]{:S(2)}) collective-permute-start(bf16[256,256]{0,1:T(8,128)(2,1)S(1)} %get-tuple-element.9), channel_id=1, source_target_pairs={{0,8},{8,0},{16,24},{24,16},{32,40},{40,32},{48,56},{56,48},{64,72... | collective-permute-start | bytes 393224 | tf_op jit(solution)/shard_map/ppermute | solution.py:29
  23.1 0.9 %copy-start.2 = (s32[4096]{0:T(1024)S(1)}, s32[4096]{0:T(1024)}, u32[]{:S(2)}) copy-start(s32[4096]{0:T(1024)} %param.7) | copy-start | bytes 49156

commit v13 on v11

--- a/solution.py
+++ b/solution.py
@@ -104,12 +104,22 @@
     local_stack = lax.dot_general(
         members, cross_both, (((0,), (0,)), ((), ())), preferred_element_type=jnp.float32
     )
+    parity = seg_position % 2
+    by_parity = local_stack.reshape(segments // 2, 2, OB_DEV, 2 * local_bins)
+    keep = jnp.where(parity == 0, by_parity[:, 0], by_parity[:, 1])
+    give = jnp.where(parity == 0, by_parity[:, 1], by_parity[:, 0])
+    partner = lax.ppermute(give, "seg", [(i, i ^ 1) for i in range(segments)])
+    chip_stack = keep + partner
+    same_core = [list(range(0, segments, 2)), list(range(1, segments, 2))]
     gathered = lax.all_to_all(
-        local_stack.astype(jnp.bfloat16), "seg", split_axis=0, concat_axis=0, tiled=True
+        chip_stack.astype(jnp.bfloat16),
+        "seg",
+        split_axis=0,
+        concat_axis=0,
+        tiled=True,
+        axis_index_groups=same_core,
     )
-    stack = jnp.sum(
-        gathered.reshape(segments, OB_DEV, 2 * local_bins).astype(jnp.float32), axis=0
-    )
+    stack = jnp.sum(gathered.astype(jnp.float32), axis=0)
     partial_lags = jnp.dot(
         stack, table.astype(jnp.float32), precision=lax.Precision.HIGHEST
     )

time: 62.7 us -> 62.5 us (level); the launches traced: 62.5 us -> 61.6 us
  blocking collectives: 35.9 us -> 33.3 us
  waiting for transfers between devices: 0.01 us -> 1 us
    all_to_all x1, blocking collectives: 21.3 us -> 18.8 us  [per_device(): lax.all_to_all(chip_stack.astype(jnp.bfloat16), 'seg', split_axis=0, conc...]
    ppermute x0 -> x1, waiting for transfers between devices: none -> 0.99 us  [per_device(): partner = lax.ppermute(give, 'seg', [(i, i ^ 1) for i in range(segments)])]
  transfers between devices with their start and end apart: 4 -> 5, of which waited for: 0 -> 1; matrix products, arithmetic and copies ran while one was open for 10% -> 10% of each run, Pallas kernels for 0% -> 0%
where the time goes in v13:
time: 62.5 us; the launch traced here: 61.6 us
  blocking collectives  33.3 us (53%)
  matrix products  11.2 us (18%)
  starting transfers between devices  9.93 us (16%)
  other arithmetic  4.46 us (7%)
  local copies, waits for them, and re-layouts  1.38 us (2%)
  waiting for transfers between devices  1 us (2%)
    all_to_all x1, blocking collectives, per_device(): lax.all_to_all(chip_stack.astype(jnp.bfloat16), 'seg', split_axis=0, conc...  18.8 us
    all_to_all x1, blocking collectives, per_device(): lax.all_to_all(partial_lags, 'band', split_axis=1, concat_axis=0, tiled=T...  14.5 us
    dot_general x2, matrix products, select_rows(): return jnp.dot(chosen, table, preferred_element_type=jnp.float32)  8.28 us
    ppermute x2, starting transfers between devices, extended(): lax.ppermute(jnp.where(odd, last, first).astype(wire_type), axis, outer)  6.52 us
    another operation x2, other arithmetic  3.37 us
    ppermute x2, starting transfers between devices, extended(): lax.ppermute(jnp.where(odd, first, last).astype(wire_type), axis, inner)  2.82 us
    dot_general x1, matrix products, per_device(): lax.dot_general(members, cross_both, (((0,), (0,)), ((), ())), preferred_...  1.43 us
  transfers between devices with their start and end apart: 5, of which 1 were waited for; matrix products, arithmetic and copies ran while one was open for 10% of the time, Pallas kernels for 0%

profile of v13, /device:TPU:1, one launch (start us, length us, event | category | flops | bytes accessed | tf_op | source)
XLA Modules:
  0.0 61.6 jit_solution(11743353322146322359)
XLA Ops:
  0.0 0.0 copy-start
  0.0 0.0 copy-start.1
  0.0 1.1 %fusion.48 = (bf16[1,1024,128]{2,1,0:T(8,128)(2,1)S(1)}, bf16[1,1024,128]{2,1,0:T(8,128)(2,1)S(1)}) fusion(bf16[2,1024,128]{2,1,0:T(8,128)(2,1)} %param.4), kind=kLoop, calls=%fused_computation.87 | loop fusion | bytes 1048576 | tf_op jit(solution)/shard_map/slice | solution.py:79
  1.1 0.1 copy.11
  1.2 0.1 copy.12
  1.4 0.1 fusion.22
  1.5 2.5 %collective-permute-start = (bf16[1024,64]{0,1:T(8,128)(2,1)S(1)}, bf16[1024,64]{0,1:T(8,128)(2,1)S(1)}, u32[]{:S(2)}, u32[]{:S(2)}) collective-permute-start(bf16[1024,64]{0,1:T(8,128)(2,1)S(1)} %get-tuple-element.16), channel_id=1, source_target_pairs={{0,1},{1,0},{2,3},{3,2},{4,5},{5,4},{6,7},{7,6},{8,9},{9,8},{10,11... | collective-permute-start | bytes 393224 | tf_op jit(solution)/shard_map/ppermute | solution.py:28
  4.1 0.7 %collective-permute-start.1 = (bf16[1024,64]{0,1:T(8,128)(2,1)S(1)}, bf16[1024,64]{0,1:T(8,128)(2,1)S(1)}, u32[]{:S(2)}, u32[]{:S(2)}) collective-permute-start(bf16[1024,64]{0,1:T(8,128)(2,1)S(1)} %get-tuple-element.17), channel_id=1, source_target_pairs={{1,2},{3,4},{5,6},{2,1},{4,3},{6,5},{9,10},{11,12},{13,14},{10,9},... | collective-permute-start | bytes 393224 | tf_op jit(solution)/shard_map/ppermute | solution.py:29
  4.8 2.5 %multiply_convert_fusion.1 = (bf16[128,1024]{0,1:T(8,128)(2,1)S(1)}, bf16[128,1024]{0,1:T(8,128)(2,1)S(1)}) fusion(s32[1024]{0:T(1024)S(1)} %iota_add_fusion, s32[128]{0:T(128)S(1)} %iota_add_fusion.2), kind=kLoop, calls=%fused_computation.54 | loop fusion | flops 2490368 | bytes 528896 | tf_op jit(solution)/shard_map/convert.6
  7.3 0.0 copy-done
  7.3 0.0 copy-done.1
  7.4 0.1 pad_maximum_fusion.1
  7.4 0.0 collective-permute-done
  7.4 0.0 collective-permute-done.1
  7.5 0.1 pad_maximum_fusion
  7.6 0.3 fusion.29
  7.9 0.3 convolution_add_fusion.1
  8.2 0.4 fusion.23
  8.6 5.9 %collective-permute-start.3 = (bf16[256,256]{0,1:T(8,128)(2,1)S(1)}, bf16[256,256]{0,1:T(8,128)(2,1)S(1)}, u32[]{:S(2)}, u32[]{:S(2)}) collective-permute-start(bf16[256,256]{0,1:T(8,128)(2,1)S(1)} %broadcast_select_fusion.2), channel_id=1, source_target_pairs={{8,16},{24,32},{40,48},{56,64},{72,80},{88,96},{104,112},{120,128}... | collective-permute-start | bytes 393224 | tf_op jit(solution)/shard_map/ppermute | solution.py:29
  14.5 0.3 collective-permute-start.2
  14.8 3.4 %fusion.1 = f32[4096,256]{0,1:T(8,128)S(1)} fusion(s32[4096]{0:T(1024)S(1)} %get-tuple-element.27, bf16[1024,128]{0,1:T(8,128)(2,1)S(1)} %get-tuple-element.15, bf16[1024,128]{0,1:T(8,128)(2,1)S(1)} %get-tuple-element.14), kind=kOutput, calls=%fused_computation.3 | convolution fusion | flops 2152726528 | bytes 4734976 | tf_op jit(solution)/shard_map/dot_general | solution.py:59
  18.2 0.0 collective-permute-done.3
  18.2 0.0 collective-permute-done.2
  18.2 4.9 %fusion = f32[4096,256]{0,1:T(8,128)S(1)} fusion(s32[4096]{0:T(1024)S(1)} %get-tuple-element.26, bf16[256,256]{0,1:T(8,128)(2,1)S(1)} %get-tuple-element.21, bf16[1024,128]{0,1:T(8,128)(2,1)S(1)} %get-tuple-element.15, bf16[1024,128]{0,1:T(8,128)(2,1)S(1)} %get-tuple-element.14, bf16[256,256]{0,1:T(8,128)(2,1)S(1)} %get-tuple-element.20), kind=kOutput, calls=%fused_computation.1 | convolution fusion | flops 3230662656 | bytes 4997120 | tf_op jit(solution)/shard_map/dot_general | solution.py:59
  23.1 0.0 copy-start.2
  23.2 0.9 %add_convert_fusion = (bf16[4096,128]{0,1:T(8,128)(2,1)S(1)}, bf16[4096,128]{0,1:T(8,128)(2,1)S(1)}) fusion(f32[4096,256]{0,1:T(8,128)S(1)} %fusion, f32[4096,256]{0,1:T(8,128)S(1)} %fusion.1), kind=kLoop, calls=%fused_computation.13 | loop fusion | flops 4194304 | bytes 10485760 | tf_op jit(solution)/shard_map/convert.2
  24.0 0.0 copy-done.2
  24.0 1.4 %fusion.5 = f32[256,256]{1,0:T(8,128)S(1)} fusion(bf16[4096,128]{0,1:T(8,128)(2,1)S(1)} %get-tuple-element.13, bf16[4096,128]{0,1:T(8,128)(2,1)S(1)} %get-tuple-element.12, s32[4096]{0:T(1024)S(1)} %copy-done.2), kind=kOutput, calls=%fused_computation.8 | convolution fusion | flops 543162368 | bytes 2375680 | tf_op jit(solution)/shard_map/dot_general | solution.py:104
  25.5 0.6 collective-permute-start.4
  26.1 1.0 %collective-permute-done.4 = f32[16,8,256]{2,1,0:T(8,128)S(1)} collective-permute-done((f32[16,8,256]{2,1,0:T(8,128)S(1)}, f32[16,8,256]{2,1,0:T(8,128)S(1)}, u32[]{:S(2)}, u32[]{:S(2)}) %collective-permute-start.4) | collective-permute-done | bytes 131104 | tf_op jit(solution)/shard_map/ppermute | solution.py:111
  27.1 18.8 %all_to_all.15 = bf16[16,8,256]{2,1,0:T(8,128)(2,1)S(1)} all-to-all(bf16[16,8,256]{2,1,0:T(8,128)(2,1)S(1)} %fusion.35), channel_id=1, replica_groups={{0,16,32,48,64,80,96,112,128,144,160,176,192,208,224,240},{8,24,40,56,7..., dimensions={0} | all-to-all | bytes 131072 | tf_op jit(solution)/shard_map/all_to_all | solution.py:114
  45.9 0.5 fusion.43
  46.4 14.5 %all_to_all.16 = f32[8,8,128]{2,0,1:T(8,128)S(1)} all-to-all(f32[8,8,128]{2,0,1:T(8,128)S(1)} %fusion.43), channel_id=1, replica_groups=mesh['seg'=32,'band'=8] {'band'}, dimensions={1} | all-to-all | bytes 65536 | tf_op jit(solution)/shard_map/all_to_all | solution.py:126
  61.0 0.6 reduce_sum.19
  (12 shorter events, 0.2 us)
Async XLA Ops:
  0.0 7.3 %copy-start = (s32[4096]{0:T(1024)S(1)}, s32[4096]{0:T(1024)}, u32[]{:S(2)}) copy-start(s32[4096]{0:T(1024)} %param.6) | copy-start | bytes 49156
  0.0 7.3 %copy-start.1 = (s32[4096]{0:T(1024)S(1)}, s32[4096]{0:T(1024)}, u32[]{:S(2)}) copy-start(s32[4096]{0:T(1024)} %param.5) | copy-start | bytes 49156
  1.5 5.9 %collective-permute-start = (bf16[1024,64]{0,1:T(8,128)(2,1)S(1)}, bf16[1024,64]{0,1:T(8,128)(2,1)S(1)}, u32[]{:S(2)}, u32[]{:S(2)}) collective-permute-start(bf16[1024,64]{0,1:T(8,128)(2,1)S(1)} %get-tuple-element.16), channel_id=1, source_target_pairs={{0,1},{1,0},{2,3},{3,2},{4,5},{5,4},{6,7},{7,6},{8,9},{9,8},{10,11... | collective-permute-start | bytes 393224 | tf_op jit(solution)/shard_map/ppermute | solution.py:28
  4.1 3.4 %collective-permute-start.1 = (bf16[1024,64]{0,1:T(8,128)(2,1)S(1)}, bf16[1024,64]{0,1:T(8,128)(2,1)S(1)}, u32[]{:S(2)}, u32[]{:S(2)}) collective-permute-start(bf16[1024,64]{0,1:T(8,128)(2,1)S(1)} %get-tuple-element.17), channel_id=1, source_target_pairs={{1,2},{3,4},{5,6},{2,1},{4,3},{6,5},{9,10},{11,12},{13,14},{10,9},... | collective-permute-start | bytes 393224 | tf_op jit(solution)/shard_map/ppermute | solution.py:29
  8.6 9.5 %collective-permute-start.3 = (bf16[256,256]{0,1:T(8,128)(2,1)S(1)}, bf16[256,256]{0,1:T(8,128)(2,1)S(1)}, u32[]{:S(2)}, u32[]{:S(2)}) collective-permute-start(bf16[256,256]{0,1:T(8,128)(2,1)S(1)} %broadcast_select_fusion.2), channel_id=1, source_target_pairs={{8,16},{24,32},{40,48},{56,64},{72,80},{88,96},{104,112},{120,128}... | collective-permute-start | bytes 393224 | tf_op jit(solution)/shard_map/ppermute | solution.py:29
  14.5 3.7 %collective-permute-start.2 = (bf16[256,256]{0,1:T(8,128)(2,1)S(1)}, bf16[256,256]{0,1:T(8,128)(2,1)S(1)}, u32[]{:S(2)}, u32[]{:S(2)}) collective-permute-start(bf16[256,256]{0,1:T(8,128)(2,1)S(1)} %get-tuple-element.9), channel_id=1, source_target_pairs={{0,8},{8,0},{16,24},{24,16},{32,40},{40,32},{48,56},{56,48},{64,72... | collective-permute-start | bytes 393224 | tf_op jit(solution)/shard_map/ppermute | solution.py:28
  23.1 0.9 %copy-start.2 = (s32[4096]{0:T(1024)S(1)}, s32[4096]{0:T(1024)}, u32[]{:S(2)}) copy-start(s32[4096]{0:T(1024)} %param.7) | copy-start | bytes 49156
  25.5 1.6 %collective-permute-start.4 = (f32[16,8,256]{2,1,0:T(8,128)S(1)}, f32[16,8,256]{2,1,0:T(8,128)S(1)}, u32[]{:S(2)}, u32[]{:S(2)}) collective-permute-start(f32[16,8,256]{2,1,0:T(8,128)S(1)} %select_bitcast_fusion), channel_id=1, source_target_pairs={{0,8},{8,0},{16,24},{24,16},{32,40},{40,32},{48,56},{56,48},{64,72... | collective-permute-start | bytes 393224 | tf_op jit(solution)/shard_map/ppermute | solution.py:111

commit v14 on v11

--- a/solution.py
+++ b/solution.py
@@ -96,14 +96,18 @@
     second_imag = second_rows[:, local_bins:]
     cross_real = first_real * second_real + first_imag * second_imag
     cross_imag = first_imag * second_real - first_real * second_imag
-    cross_both = jnp.concatenate([cross_real, cross_imag], axis=1).astype(jnp.bfloat16)
     all_bins = segments * OB_DEV
     members = (pair_bin[:, None] == jnp.arange(all_bins, dtype=jnp.int32)[None, :]).astype(
         jnp.bfloat16
     )
-    local_stack = lax.dot_general(
-        members, cross_both, (((0,), (0,)), ((), ())), preferred_element_type=jnp.float32
+    by_bin = (((0,), (0,)), ((), ()))
+    stack_real = lax.dot_general(
+        members, cross_real.astype(jnp.bfloat16), by_bin, preferred_element_type=jnp.float32
     )
+    stack_imag = lax.dot_general(
+        members, cross_imag.astype(jnp.bfloat16), by_bin, preferred_element_type=jnp.float32
+    )
+    local_stack = jnp.concatenate([stack_real, stack_imag], axis=1)
     gathered = lax.all_to_all(
         local_stack.astype(jnp.bfloat16), "seg", split_axis=0, concat_axis=0, tiled=True
     )

time: 62.7 us -> 64.2 us (1.024)
  matrix products: 11.1 us -> 13.2 us
  other arithmetic: 4.44 us -> 3.6 us
    dot_general x1 -> x2, matrix products: 1.42 us -> 3.81 us  [the longest x1 1.92 us: per_device(): lax.dot_general(members, cross_real.astype(jnp.bfloat16), by_bin, preferr...]
    another operation x2 -> x1, other arithmetic: 3.37 us -> 2.52 us
  transfers between devices with their start and end apart: 4 -> 4, of which waited for: 0 -> 0; matrix products, arithmetic and copies ran while one was open for 10% -> 9% of each run, Pallas kernels for 0% -> 0%
where the time goes in v14:
time: 64.2 us; the launch traced here: 64 us
  blocking collectives  36.2 us (56%)
  matrix products  13.2 us (21%)
  starting transfers between devices  9.34 us (15%)
  other arithmetic  3.6 us (6%)
  local copies, waits for them, and re-layouts  1.38 us (2%)
    all_to_all x1, blocking collectives, per_device(): lax.all_to_all(local_stack.astype(jnp.bfloat16), 'seg', split_axis=0, con...  21.5 us
    all_to_all x1, blocking collectives, per_device(): lax.all_to_all(partial_lags, 'band', split_axis=1, concat_axis=0, tiled=T...  14.7 us
    dot_general x2, matrix products, select_rows(): return jnp.dot(chosen, table, preferred_element_type=jnp.float32)  7.99 us
    ppermute x2, starting transfers between devices, extended(): lax.ppermute(jnp.where(odd, last, first).astype(wire_type), axis, outer)  6.53 us
    ppermute x2, starting transfers between devices, extended(): lax.ppermute(jnp.where(odd, first, last).astype(wire_type), axis, inner)  2.82 us
    another operation x1, other arithmetic  2.52 us
    dot_general x1, matrix products, per_device(): lax.dot_general(members, cross_real.astype(jnp.bfloat16), by_bin, preferr...  1.92 us
    dot_general x1, matrix products, per_device(): lax.dot_general(members, cross_imag.astype(jnp.bfloat16), by_bin, preferr...  1.9 us
  transfers between devices with their start and end apart: 4, of which 0 were waited for; matrix products, arithmetic and copies ran while one was open for 9% of the time, Pallas kernels for 0%

profile of v14, /device:TPU:1, one launch (start us, length us, event | category | flops | bytes accessed | tf_op | source)
XLA Modules:
  0.0 64.0 jit_solution(7779410588741516821)
XLA Ops:
  0.0 0.0 copy-start
  0.0 0.0 copy-start.1
  0.0 1.1 %fusion.45 = (bf16[1,1024,128]{2,1,0:T(8,128)(2,1)S(1)}, bf16[1,1024,128]{2,1,0:T(8,128)(2,1)S(1)}) fusion(bf16[2,1024,128]{2,1,0:T(8,128)(2,1)} %param.4), kind=kLoop, calls=%fused_computation.84 | loop fusion | bytes 1048576 | tf_op jit(solution)/shard_map/slice | solution.py:79
  1.1 0.1 copy.7
  1.2 0.1 copy.8
  1.4 0.1 fusion.23
  1.5 2.5 %collective-permute-start = (bf16[1024,64]{0,1:T(8,128)(2,1)S(1)}, bf16[1024,64]{0,1:T(8,128)(2,1)S(1)}, u32[]{:S(2)}, u32[]{:S(2)}) collective-permute-start(bf16[1024,64]{0,1:T(8,128)(2,1)S(1)} %get-tuple-element.14), channel_id=1, source_target_pairs={{0,1},{1,0},{2,3},{3,2},{4,5},{5,4},{6,7},{7,6},{8,9},{9,8},{10,11... | collective-permute-start | bytes 393224 | tf_op jit(solution)/shard_map/ppermute | solution.py:28
  4.1 0.7 %collective-permute-start.1 = (bf16[1024,64]{0,1:T(8,128)(2,1)S(1)}, bf16[1024,64]{0,1:T(8,128)(2,1)S(1)}, u32[]{:S(2)}, u32[]{:S(2)}) collective-permute-start(bf16[1024,64]{0,1:T(8,128)(2,1)S(1)} %get-tuple-element.15), channel_id=1, source_target_pairs={{1,2},{3,4},{5,6},{2,1},{4,3},{6,5},{9,10},{11,12},{13,14},{10,9},... | collective-permute-start | bytes 393224 | tf_op jit(solution)/shard_map/ppermute | solution.py:29
  4.8 2.5 %multiply_convert_fusion.1 = (bf16[128,1024]{0,1:T(8,128)(2,1)S(1)}, bf16[128,1024]{0,1:T(8,128)(2,1)S(1)}) fusion(s32[1024]{0:T(1024)S(1)} %iota_add_fusion, s32[128]{0:T(128)S(1)} %iota_add_fusion.2), kind=kLoop, calls=%fused_computation.56 | loop fusion | flops 2490368 | bytes 528896 | tf_op jit(solution)/shard_map/convert.8
  7.3 0.0 copy-done
  7.3 0.0 copy-done.1
  7.4 0.1 pad_maximum_fusion.1
  7.4 0.0 collective-permute-done
  7.4 0.0 collective-permute-done.1
  7.5 0.1 pad_maximum_fusion
  7.6 0.3 fusion.30
  7.9 0.3 convolution_add_fusion.1
  8.2 0.4 fusion.24
  8.6 5.9 %collective-permute-start.3 = (bf16[256,256]{0,1:T(8,128)(2,1)S(1)}, bf16[256,256]{0,1:T(8,128)(2,1)S(1)}, u32[]{:S(2)}, u32[]{:S(2)}) collective-permute-start(bf16[256,256]{0,1:T(8,128)(2,1)S(1)} %broadcast_select_fusion.2), channel_id=1, source_target_pairs={{8,16},{24,32},{40,48},{56,64},{72,80},{88,96},{104,112},{120,128}... | collective-permute-start | bytes 393224 | tf_op jit(solution)/shard_map/ppermute | solution.py:29
  14.5 0.3 collective-permute-start.2
  14.8 3.1 %fusion.1 = f32[4096,256]{1,0:T(8,128)S(1)} fusion(s32[4096]{0:T(1024)S(1)} %get-tuple-element.25, bf16[1024,128]{0,1:T(8,128)(2,1)S(1)} %get-tuple-element.13, bf16[1024,128]{0,1:T(8,128)(2,1)S(1)} %get-tuple-element.12), kind=kOutput, calls=%fused_computation.3 | convolution fusion | flops 2152726528 | bytes 4734976 | tf_op jit(solution)/shard_map/dot_general | solution.py:59
  17.9 0.0 collective-permute-done.3
  18.0 0.0 collective-permute-done.2
  18.0 0.0 copy-start.2
  18.0 4.8 %fusion = f32[4096,256]{1,0:T(8,128)S(1)} fusion(s32[4096]{0:T(1024)S(1)} %get-tuple-element.24, bf16[256,256]{0,1:T(8,128)(2,1)S(1)} %get-tuple-element.19, bf16[1024,128]{0,1:T(8,128)(2,1)S(1)} %get-tuple-element.13, bf16[1024,128]{0,1:T(8,128)(2,1)S(1)} %get-tuple-element.12, bf16[256,256]{0,1:T(8,128)(2,1)S(1)} %get-tuple-element.18), kind=kOutput, calls=%fused_computation.1 | convolution fusion | flops 3230662656 | bytes 4997120 | tf_op jit(solution)/shard_map/dot_general | solution.py:59
  22.9 0.0 copy-done.2
  22.9 1.9 %fusion.14 = bf16[32,8,128]{2,1,0:T(8,128)(2,1)S(1)} fusion(s32[4096]{0:T(1024)S(1)} %copy-done.2, f32[4096,256]{1,0:T(8,128)S(1)} %fusion, f32[4096,256]{1,0:T(8,128)S(1)} %fusion.1), kind=kOutput, calls=%fused_computation.25 | convolution fusion | flops 271613952 | bytes 8470528 | tf_op jit(solution)/shard_map/dot_general | solution.py:104
  24.8 1.9 %fusion.13 = bf16[32,8,128]{2,1,0:T(8,128)(2,1)S(1)} fusion(s32[4096]{0:T(1024)S(1)} %copy-done.2, f32[4096,256]{1,0:T(8,128)S(1)} %fusion, f32[4096,256]{1,0:T(8,128)S(1)} %fusion.1), kind=kOutput, calls=%fused_computation.24 | convolution fusion | flops 271613952 | bytes 8470528 | tf_op jit(solution)/shard_map/dot_general | solution.py:107
  26.7 21.5 %all_to_all.16 = bf16[32,8,256]{2,1,0:T(8,128)(2,1)S(1)} all-to-all(bf16[32,8,256]{2,1,0:T(8,128)(2,1)S(1)} %pad_maximum_fusion.4), channel_id=1, replica_groups=mesh['seg'=32,'band'=8] {'seg'}, dimensions={0} | all-to-all | bytes 262144 | tf_op jit(solution)/shard_map/all_to_all | solution.py:111
  48.2 0.5 fusion.41
  48.7 14.7 %all_to_all.17 = f32[8,8,128]{2,0,1:T(8,128)S(1)} all-to-all(f32[8,8,128]{2,0,1:T(8,128)S(1)} %fusion.41), channel_id=1, replica_groups=mesh['seg'=32,'band'=8] {'band'}, dimensions={1} | all-to-all | bytes 65536 | tf_op jit(solution)/shard_map/all_to_all | solution.py:120
  63.4 0.6 reduce_sum.19
  (11 shorter events, 0.2 us)
Async XLA Ops:
  0.0 7.3 %copy-start = (s32[4096]{0:T(1024)S(1)}, s32[4096]{0:T(1024)}, u32[]{:S(2)}) copy-start(s32[4096]{0:T(1024)} %param.6) | copy-start | bytes 49156
  0.0 7.3 %copy-start.1 = (s32[4096]{0:T(1024)S(1)}, s32[4096]{0:T(1024)}, u32[]{:S(2)}) copy-start(s32[4096]{0:T(1024)} %param.5) | copy-start | bytes 49156
  1.5 5.9 %collective-permute-start = (bf16[1024,64]{0,1:T(8,128)(2,1)S(1)}, bf16[1024,64]{0,1:T(8,128)(2,1)S(1)}, u32[]{:S(2)}, u32[]{:S(2)}) collective-permute-start(bf16[1024,64]{0,1:T(8,128)(2,1)S(1)} %get-tuple-element.14), channel_id=1, source_target_pairs={{0,1},{1,0},{2,3},{3,2},{4,5},{5,4},{6,7},{7,6},{8,9},{9,8},{10,11... | collective-permute-start | bytes 393224 | tf_op jit(solution)/shard_map/ppermute | solution.py:28
  4.1 3.4 %collective-permute-start.1 = (bf16[1024,64]{0,1:T(8,128)(2,1)S(1)}, bf16[1024,64]{0,1:T(8,128)(2,1)S(1)}, u32[]{:S(2)}, u32[]{:S(2)}) collective-permute-start(bf16[1024,64]{0,1:T(8,128)(2,1)S(1)} %get-tuple-element.15), channel_id=1, source_target_pairs={{1,2},{3,4},{5,6},{2,1},{4,3},{6,5},{9,10},{11,12},{13,14},{10,9},... | collective-permute-start | bytes 393224 | tf_op jit(solution)/shard_map/ppermute | solution.py:29
  8.6 9.3 %collective-permute-start.3 = (bf16[256,256]{0,1:T(8,128)(2,1)S(1)}, bf16[256,256]{0,1:T(8,128)(2,1)S(1)}, u32[]{:S(2)}, u32[]{:S(2)}) collective-permute-start(bf16[256,256]{0,1:T(8,128)(2,1)S(1)} %broadcast_select_fusion.2), channel_id=1, source_target_pairs={{8,16},{24,32},{40,48},{56,64},{72,80},{88,96},{104,112},{120,128}... | collective-permute-start | bytes 393224 | tf_op jit(solution)/shard_map/ppermute | solution.py:29
  14.5 3.4 %collective-permute-start.2 = (bf16[256,256]{0,1:T(8,128)(2,1)S(1)}, bf16[256,256]{0,1:T(8,128)(2,1)S(1)}, u32[]{:S(2)}, u32[]{:S(2)}) collective-permute-start(bf16[256,256]{0,1:T(8,128)(2,1)S(1)} %get-tuple-element.9), channel_id=1, source_target_pairs={{0,8},{8,0},{16,24},{24,16},{32,40},{40,32},{48,56},{56,48},{64,72... | collective-permute-start | bytes 393224 | tf_op jit(solution)/shard_map/ppermute | solution.py:28
  18.0 4.9 %copy-start.2 = (s32[4096]{0:T(1024)S(1)}, s32[4096]{0:T(1024)}, u32[]{:S(2)}) copy-start(s32[4096]{0:T(1024)} %param.7) | copy-start | bytes 49156

commit v15 on v11

--- a/solution.py
+++ b/solution.py
@@ -56,7 +56,7 @@
     chosen = (index[:, None] == jnp.arange(table.shape[0], dtype=jnp.int32)[None, :]).astype(
         table.dtype
     )
-    return jnp.dot(chosen, table, preferred_element_type=jnp.float32)
+    return jnp.dot(chosen, table, preferred_element_type=jnp.float32).astype(table.dtype)
 
 
 def lag_table(first_bin, local_bins, total_bins, lag_count):
@@ -90,10 +90,10 @@
     first_rows = select_rows(whitened, pair_first - seg_position * channels)
     near_rows = extended(whitened, (("seg", 0),), REACH)
     second_rows = select_rows(near_rows, pair_second - seg_position * channels + REACH)
-    first_real = first_rows[:, :local_bins]
-    first_imag = first_rows[:, local_bins:]
-    second_real = second_rows[:, :local_bins]
-    second_imag = second_rows[:, local_bins:]
+    first_real = first_rows[:, :local_bins].astype(jnp.float32)
+    first_imag = first_rows[:, local_bins:].astype(jnp.float32)
+    second_real = second_rows[:, :local_bins].astype(jnp.float32)
+    second_imag = second_rows[:, local_bins:].astype(jnp.float32)
     cross_real = first_real * second_real + first_imag * second_imag
     cross_imag = first_imag * second_real - first_real * second_imag
     cross_both = jnp.concatenate([cross_real, cross_imag], axis=1).astype(jnp.bfloat16)

time: 62.7 us -> 63.4 us (1.011)
  matrix products: 11.1 us -> 12.3 us
    dot_general x2, matrix products: 8.28 us -> 9.47 us  [select_rows(): jnp.dot(chosen, table, preferred_element_type=jnp.float32)]
where the time goes in v15:
time: 63.4 us; the launch traced here: 63.2 us
  blocking collectives  35.6 us (56%)
  matrix products  12.3 us (19%)
  starting transfers between devices  9.16 us (14%)
  other arithmetic  4.43 us (7%)
  local copies, waits for them, and re-layouts  1.38 us (2%)
    all_to_all x1, blocking collectives, per_device(): lax.all_to_all(local_stack.astype(jnp.bfloat16), 'seg', split_axis=0, con...  20.9 us
    all_to_all x1, blocking collectives, per_device(): lax.all_to_all(partial_lags, 'band', split_axis=1, concat_axis=0, tiled=T...  14.7 us
    dot_general x2, matrix products, select_rows(): jnp.dot(chosen, table, preferred_element_type=jnp.float32)  9.47 us
    ppermute x2, starting transfers between devices, extended(): lax.ppermute(jnp.where(odd, last, first).astype(wire_type), axis, outer)  6.52 us
    another operation x2, other arithmetic  3.35 us
    ppermute x2, starting transfers between devices, extended(): lax.ppermute(jnp.where(odd, first, last).astype(wire_type), axis, inner)  2.63 us
    dot_general x1, matrix products, per_device(): lax.dot_general(members, cross_both, (((0,), (0,)), ((), ())), preferred_...  1.42 us
  transfers between devices with their start and end apart: 4, of which 0 were waited for; matrix products, arithmetic and copies ran while one was open for 10% of the time, Pallas kernels for 0%

profile of v15, /device:TPU:1, one launch (start us, length us, event | category | flops | bytes accessed | tf_op | source)
XLA Modules:
  0.0 63.2 jit_solution(16486868925059652303)
XLA Ops:
  0.0 0.0 copy-start
  0.0 0.0 copy-start.1
  0.0 1.1 %fusion.61 = (bf16[1,1024,128]{2,1,0:T(8,128)(2,1)S(1)}, bf16[1,1024,128]{2,1,0:T(8,128)(2,1)S(1)}) fusion(bf16[2,1024,128]{2,1,0:T(8,128)(2,1)} %param.4), kind=kLoop, calls=%fused_computation.92 | loop fusion | bytes 1048576 | tf_op jit(solution)/shard_map/slice | solution.py:79
  1.1 0.1 copy.7
  1.2 0.1 copy.8
  1.4 0.1 fusion.38
  1.5 2.5 %collective-permute-start = (bf16[1024,64]{0,1:T(8,128)(2,1)S(1)}, bf16[1024,64]{0,1:T(8,128)(2,1)S(1)}, u32[]{:S(2)}, u32[]{:S(2)}) collective-permute-start(bf16[1024,64]{0,1:T(8,128)(2,1)S(1)} %get-tuple-element.16), channel_id=1, source_target_pairs={{0,1},{1,0},{2,3},{3,2},{4,5},{5,4},{6,7},{7,6},{8,9},{9,8},{10,11... | collective-permute-start | bytes 393224 | tf_op jit(solution)/shard_map/ppermute | solution.py:28
  4.1 0.7 %collective-permute-start.1 = (bf16[1024,64]{0,1:T(8,128)(2,1)S(1)}, bf16[1024,64]{0,1:T(8,128)(2,1)S(1)}, u32[]{:S(2)}, u32[]{:S(2)}) collective-permute-start(bf16[1024,64]{0,1:T(8,128)(2,1)S(1)} %get-tuple-element.17), channel_id=1, source_target_pairs={{1,2},{3,4},{5,6},{2,1},{4,3},{6,5},{9,10},{11,12},{13,14},{10,9},... | collective-permute-start | bytes 393224 | tf_op jit(solution)/shard_map/ppermute | solution.py:29
  4.8 2.5 %multiply_convert_fusion.1 = (bf16[128,1024]{0,1:T(8,128)(2,1)S(1)}, bf16[128,1024]{0,1:T(8,128)(2,1)S(1)}) fusion(s32[1024]{0:T(1024)S(1)} %iota_add_fusion, s32[128]{0:T(128)S(1)} %iota_add_fusion.2), kind=kLoop, calls=%fused_computation.64 | loop fusion | flops 2490368 | bytes 528896 | tf_op jit(solution)/shard_map/convert.6
  7.3 0.0 copy-done
  7.3 0.0 copy-done.1
  7.4 0.1 pad_maximum_fusion.1
  7.4 0.0 collective-permute-done
  7.4 0.0 collective-permute-done.1
  7.5 0.1 pad_maximum_fusion
  7.6 0.3 fusion.45
  7.9 0.3 convolution_add_fusion.1
  8.2 0.4 fusion.39
  8.7 5.9 %collective-permute-start.3 = (bf16[256,256]{0,1:T(8,128)(2,1)S(1)}, bf16[256,256]{0,1:T(8,128)(2,1)S(1)}, u32[]{:S(2)}, u32[]{:S(2)}) collective-permute-start(bf16[256,256]{0,1:T(8,128)(2,1)S(1)} %broadcast_select_fusion.2), channel_id=1, source_target_pairs={{8,16},{24,32},{40,48},{56,64},{72,80},{88,96},{104,112},{120,128}... | collective-permute-start | bytes 393224 | tf_op jit(solution)/shard_map/ppermute | solution.py:29
  14.5 0.1 collective-permute-start.2
  14.6 3.9 %fusion.5 = bf16[4096,256]{0,1:T(8,128)(2,1)S(1)} fusion(s32[4096]{0:T(1024)S(1)} %get-tuple-element.27, bf16[1024,128]{0,1:T(8,128)(2,1)S(1)} %get-tuple-element.15, bf16[1024,128]{0,1:T(8,128)(2,1)S(1)} %get-tuple-element.14), kind=kOutput, calls=%fused_computation.7 | convolution fusion | flops 2153775104 | bytes 2637824 | tf_op jit(solution)/shard_map/dot_general | solution.py:59
  18.5 0.0 collective-permute-done.3
  18.5 0.0 collective-permute-done.2
  18.6 5.6 %fusion.4 = bf16[4096,256]{0,1:T(8,128)(2,1)S(1)} fusion(s32[4096]{0:T(1024)S(1)} %get-tuple-element.26, bf16[256,256]{0,1:T(8,128)(2,1)S(1)} %get-tuple-element.21, bf16[1024,128]{0,1:T(8,128)(2,1)S(1)} %get-tuple-element.15, bf16[1024,128]{0,1:T(8,128)(2,1)S(1)} %get-tuple-element.14, bf16[256,256]{0,1:T(8,128)(2,1)S(1)} %get-tuple-element.20), kind=kOutput, calls=%fused_computation.6 | convolution fusion | flops 3231711232 | bytes 2899968 | tf_op jit(solution)/shard_map/dot_general | solution.py:59
  24.2 0.0 copy-start.2
  24.2 0.8 %fusion.8 = (bf16[4096,128]{0,1:T(8,128)(2,1)S(1)}, bf16[4096,128]{0,1:T(8,128)(2,1)S(1)}) fusion(bf16[4096,256]{0,1:T(8,128)(2,1)S(1)} %fusion.4, bf16[4096,256]{0,1:T(8,128)(2,1)S(1)} %fusion.5), kind=kLoop, calls=%fused_computation.15 | loop fusion | flops 6291456 | bytes 6291456 | tf_op jit(solution)/shard_map/convert.2
  25.0 0.0 copy-done.2
  25.0 1.4 %fusion.25 = bf16[32,8,256]{2,1,0:T(8,128)(2,1)S(1)} fusion(bf16[4096,128]{0,1:T(8,128)(2,1)S(1)} %get-tuple-element.13, bf16[4096,128]{0,1:T(8,128)(2,1)S(1)} %get-tuple-element.12, s32[4096]{0:T(1024)S(1)} %copy-done.2), kind=kOutput, calls=%fused_computation.33 | convolution fusion | flops 543227904 | bytes 2244608 | tf_op jit(solution)/shard_map/dot_general | solution.py:104
  26.5 20.9 %all_to_all.19 = bf16[32,8,256]{2,1,0:T(8,128)(2,1)S(1)} all-to-all(bf16[32,8,256]{2,1,0:T(8,128)(2,1)S(1)} %fusion.25), channel_id=1, replica_groups=mesh['seg'=32,'band'=8] {'seg'}, dimensions={0} | all-to-all | bytes 262144 | tf_op jit(solution)/shard_map/all_to_all | solution.py:107
  47.4 0.5 fusion.56
  47.9 14.7 %all_to_all.20 = f32[8,8,128]{2,0,1:T(8,128)S(1)} all-to-all(f32[8,8,128]{2,0,1:T(8,128)S(1)} %fusion.56), channel_id=1, replica_groups=mesh['seg'=32,'band'=8] {'band'}, dimensions={1} | all-to-all | bytes 65536 | tf_op jit(solution)/shard_map/all_to_all | solution.py:116
  62.6 0.6 reduce_sum.19
  (10 shorter events, 0.2 us)
Async XLA Ops:
  0.0 7.3 %copy-start = (s32[4096]{0:T(1024)S(1)}, s32[4096]{0:T(1024)}, u32[]{:S(2)}) copy-start(s32[4096]{0:T(1024)} %param.6) | copy-start | bytes 49156
  0.0 7.3 %copy-start.1 = (s32[4096]{0:T(1024)S(1)}, s32[4096]{0:T(1024)}, u32[]{:S(2)}) copy-start(s32[4096]{0:T(1024)} %param.5) | copy-start | bytes 49156
  1.5 5.9 %collective-permute-start = (bf16[1024,64]{0,1:T(8,128)(2,1)S(1)}, bf16[1024,64]{0,1:T(8,128)(2,1)S(1)}, u32[]{:S(2)}, u32[]{:S(2)}) collective-permute-start(bf16[1024,64]{0,1:T(8,128)(2,1)S(1)} %get-tuple-element.16), channel_id=1, source_target_pairs={{0,1},{1,0},{2,3},{3,2},{4,5},{5,4},{6,7},{7,6},{8,9},{9,8},{10,11... | collective-permute-start | bytes 393224 | tf_op jit(solution)/shard_map/ppermute | solution.py:28
  4.1 3.4 %collective-permute-start.1 = (bf16[1024,64]{0,1:T(8,128)(2,1)S(1)}, bf16[1024,64]{0,1:T(8,128)(2,1)S(1)}, u32[]{:S(2)}, u32[]{:S(2)}) collective-permute-start(bf16[1024,64]{0,1:T(8,128)(2,1)S(1)} %get-tuple-element.17), channel_id=1, source_target_pairs={{1,2},{3,4},{5,6},{2,1},{4,3},{6,5},{9,10},{11,12},{13,14},{10,9},... | collective-permute-start | bytes 393224 | tf_op jit(solution)/shard_map/ppermute | solution.py:29
  8.7 9.8 %collective-permute-start.3 = (bf16[256,256]{0,1:T(8,128)(2,1)S(1)}, bf16[256,256]{0,1:T(8,128)(2,1)S(1)}, u32[]{:S(2)}, u32[]{:S(2)}) collective-permute-start(bf16[256,256]{0,1:T(8,128)(2,1)S(1)} %broadcast_select_fusion.2), channel_id=1, source_target_pairs={{8,16},{24,32},{40,48},{56,64},{72,80},{88,96},{104,112},{120,128}... | collective-permute-start | bytes 393224 | tf_op jit(solution)/shard_map/ppermute | solution.py:29
  14.5 4.0 %collective-permute-start.2 = (bf16[256,256]{0,1:T(8,128)(2,1)S(1)}, bf16[256,256]{0,1:T(8,128)(2,1)S(1)}, u32[]{:S(2)}, u32[]{:S(2)}) collective-permute-start(bf16[256,256]{0,1:T(8,128)(2,1)S(1)} %get-tuple-element.9), channel_id=1, source_target_pairs={{0,8},{8,0},{16,24},{24,16},{32,40},{40,32},{48,56},{56,48},{64,72... | collective-permute-start | bytes 393224 | tf_op jit(solution)/shard_map/ppermute | solution.py:28
  24.2 0.8 %copy-start.2 = (s32[4096]{0:T(1024)S(1)}, s32[4096]{0:T(1024)}, u32[]{:S(2)}) copy-start(s32[4096]{0:T(1024)} %param.7) | copy-start | bytes 49156

commit v16 on v11

--- a/solution.py
+++ b/solution.py
@@ -113,8 +113,10 @@
     partial_lags = jnp.dot(
         stack, table.astype(jnp.float32), precision=lax.Precision.HIGHEST
     )
-    pieces = lax.all_to_all(partial_lags, "band", split_axis=1, concat_axis=0, tiled=True)
-    return jnp.sum(pieces.reshape(bands, OB_DEV, LAGS // bands), axis=0)
+    pieces = lax.all_to_all(
+        partial_lags.astype(jnp.bfloat16), "band", split_axis=1, concat_axis=0, tiled=True
+    )
+    return jnp.sum(pieces.reshape(bands, OB_DEV, LAGS // bands).astype(jnp.float32), axis=0)
 
 
 def solution(mesh):

time: 62.7 us -> 62.5 us (level)
  transfers between devices with their start and end apart: 4 -> 4, of which waited for: 0 -> 0; matrix products, arithmetic and copies ran while one was open for 10% -> 9% of each run, Pallas kernels for 0% -> 0%
where the time goes in v16:
time: 62.5 us; the launch traced here: 62.3 us
  blocking collectives  35.9 us (57%)
  matrix products  11 us (18%)
  starting transfers between devices  9.43 us (15%)
  other arithmetic  4.35 us (7%)
  local copies, waits for them, and re-layouts  1.38 us (2%)
    all_to_all x1, blocking collectives, per_device(): lax.all_to_all(local_stack.astype(jnp.bfloat16), 'seg', split_axis=0, con...  21.3 us
    all_to_all x1, blocking collectives, per_device(): lax.all_to_all(partial_lags.astype(jnp.bfloat16), 'band', split_axis=1, c...  14.6 us
    dot_general x2, matrix products, select_rows(): return jnp.dot(chosen, table, preferred_element_type=jnp.float32)  8.28 us
    ppermute x2, starting transfers between devices, extended(): lax.ppermute(jnp.where(odd, last, first).astype(wire_type), axis, outer)  6.61 us
    another operation x2, other arithmetic  3.31 us
    ppermute x2, starting transfers between devices, extended(): lax.ppermute(jnp.where(odd, first, last).astype(wire_type), axis, inner)  2.82 us
    dot_general x1, matrix products, per_device(): lax.dot_general(members, cross_both, (((0,), (0,)), ((), ())), preferred_...  1.42 us
  transfers between devices with their start and end apart: 4, of which 0 were waited for; matrix products, arithmetic and copies ran while one was open for 9% of the time, Pallas kernels for 0%

profile of v16, /device:TPU:1, one launch (start us, length us, event | category | flops | bytes accessed | tf_op | source)
XLA Modules:
  0.0 62.3 jit_solution(14387107160570663462)
XLA Ops:
  0.0 0.0 copy-start
  0.0 0.0 copy-start.1
  0.0 1.1 %fusion.54 = (bf16[1,1024,128]{2,1,0:T(8,128)(2,1)S(1)}, bf16[1,1024,128]{2,1,0:T(8,128)(2,1)S(1)}) fusion(bf16[2,1024,128]{2,1,0:T(8,128)(2,1)} %param.4), kind=kLoop, calls=%fused_computation.85 | loop fusion | bytes 1048576 | tf_op jit(solution)/shard_map/slice | solution.py:79
  1.1 0.1 copy.7
  1.2 0.1 copy.8
  1.4 0.1 fusion.33
  1.5 2.5 %collective-permute-start = (bf16[1024,64]{0,1:T(8,128)(2,1)S(1)}, bf16[1024,64]{0,1:T(8,128)(2,1)S(1)}, u32[]{:S(2)}, u32[]{:S(2)}) collective-permute-start(bf16[1024,64]{0,1:T(8,128)(2,1)S(1)} %get-tuple-element.16), channel_id=1, source_target_pairs={{0,1},{1,0},{2,3},{3,2},{4,5},{5,4},{6,7},{7,6},{8,9},{9,8},{10,11... | collective-permute-start | bytes 393224 | tf_op jit(solution)/shard_map/ppermute | solution.py:28
  4.1 0.7 %collective-permute-start.1 = (bf16[1024,64]{0,1:T(8,128)(2,1)S(1)}, bf16[1024,64]{0,1:T(8,128)(2,1)S(1)}, u32[]{:S(2)}, u32[]{:S(2)}) collective-permute-start(bf16[1024,64]{0,1:T(8,128)(2,1)S(1)} %get-tuple-element.17), channel_id=1, source_target_pairs={{1,2},{3,4},{5,6},{2,1},{4,3},{6,5},{9,10},{11,12},{13,14},{10,9},... | collective-permute-start | bytes 393224 | tf_op jit(solution)/shard_map/ppermute | solution.py:29
  4.8 2.5 %multiply_convert_fusion.1 = (bf16[128,1024]{1,0:T(8,128)(2,1)S(1)}, bf16[128,1024]{1,0:T(8,128)(2,1)S(1)}) fusion(s32[1024]{0:T(1024)S(1)} %iota_add_fusion, s32[128]{0:T(128)S(1)} %iota_add_fusion.2), kind=kLoop, calls=%fused_computation.58 | loop fusion | flops 2490368 | bytes 528896 | tf_op jit(solution)/shard_map/convert.6
  7.2 0.0 copy-done
  7.2 0.0 copy-done.1
  7.3 0.0 collective-permute-done
  7.3 0.0 collective-permute-done.1
  7.4 0.1 pad_maximum_fusion
  7.5 0.3 fusion.40
  7.8 0.3 convolution_add_fusion.1
  8.1 0.4 fusion.34
  8.6 6.0 %collective-permute-start.3 = (bf16[256,256]{0,1:T(8,128)(2,1)S(1)}, bf16[256,256]{0,1:T(8,128)(2,1)S(1)}, u32[]{:S(2)}, u32[]{:S(2)}) collective-permute-start(bf16[256,256]{0,1:T(8,128)(2,1)S(1)} %broadcast_select_fusion.2), channel_id=1, source_target_pairs={{8,16},{24,32},{40,48},{56,64},{72,80},{88,96},{104,112},{120,128}... | collective-permute-start | bytes 393224 | tf_op jit(solution)/shard_map/ppermute | solution.py:29
  14.5 0.3 collective-permute-start.2
  14.8 3.4 %fusion.1 = f32[4096,256]{0,1:T(8,128)S(1)} fusion(s32[4096]{0:T(1024)S(1)} %get-tuple-element.27, bf16[1024,128]{0,1:T(8,128)(2,1)S(1)} %get-tuple-element.15, bf16[1024,128]{0,1:T(8,128)(2,1)S(1)} %get-tuple-element.14), kind=kOutput, calls=%fused_computation.3 | convolution fusion | flops 2152726528 | bytes 4734976 | tf_op jit(solution)/shard_map/dot_general | solution.py:59
  18.2 0.0 collective-permute-done.3
  18.2 0.0 collective-permute-done.2
  18.2 4.9 %fusion = f32[4096,256]{0,1:T(8,128)S(1)} fusion(s32[4096]{0:T(1024)S(1)} %get-tuple-element.26, bf16[256,256]{0,1:T(8,128)(2,1)S(1)} %get-tuple-element.21, bf16[1024,128]{0,1:T(8,128)(2,1)S(1)} %get-tuple-element.15, bf16[1024,128]{0,1:T(8,128)(2,1)S(1)} %get-tuple-element.14, bf16[256,256]{0,1:T(8,128)(2,1)S(1)} %get-tuple-element.20), kind=kOutput, calls=%fused_computation.1 | convolution fusion | flops 3230662656 | bytes 4997120 | tf_op jit(solution)/shard_map/dot_general | solution.py:59
  23.1 0.0 copy-start.2
  23.2 0.9 %add_convert_fusion = (bf16[4096,128]{0,1:T(8,128)(2,1)S(1)}, bf16[4096,128]{0,1:T(8,128)(2,1)S(1)}) fusion(f32[4096,256]{0,1:T(8,128)S(1)} %fusion, f32[4096,256]{0,1:T(8,128)S(1)} %fusion.1), kind=kLoop, calls=%fused_computation.13 | loop fusion | flops 4194304 | bytes 10485760 | tf_op jit(solution)/shard_map/convert.2
  24.0 0.0 copy-done.2
  24.0 1.4 %fusion.19 = bf16[32,8,256]{2,1,0:T(8,128)(2,1)S(1)} fusion(bf16[4096,128]{0,1:T(8,128)(2,1)S(1)} %get-tuple-element.13, bf16[4096,128]{0,1:T(8,128)(2,1)S(1)} %get-tuple-element.12, s32[4096]{0:T(1024)S(1)} %copy-done.2), kind=kOutput, calls=%fused_computation.25 | convolution fusion | flops 543227904 | bytes 2244608 | tf_op jit(solution)/shard_map/dot_general | solution.py:104
  25.5 21.3 %all_to_all.22 = bf16[32,8,256]{2,1,0:T(8,128)(2,1)S(1)} all-to-all(bf16[32,8,256]{2,1,0:T(8,128)(2,1)S(1)} %fusion.19), channel_id=1, replica_groups=mesh['seg'=32,'band'=8] {'seg'}, dimensions={0} | all-to-all | bytes 262144 | tf_op jit(solution)/shard_map/all_to_all | solution.py:107
  46.7 0.3 fusion.24
  47.1 14.6 %all_to_all.23 = bf16[8,8,128]{2,0,1:T(8,128)(2,1)S(1)} all-to-all(bf16[8,8,128]{2,0,1:T(8,128)(2,1)S(1)} %fusion.24), channel_id=1, replica_groups=mesh['seg'=32,'band'=8] {'band'}, dimensions={1} | all-to-all | bytes 32768 | tf_op jit(solution)/shard_map/all_to_all | solution.py:116
  61.7 0.6 convert_reduce_fusion.1
  (11 shorter events, 0.3 us)
Async XLA Ops:
  0.0 7.2 %copy-start = (s32[4096]{0:T(1024)S(1)}, s32[4096]{0:T(1024)}, u32[]{:S(2)}) copy-start(s32[4096]{0:T(1024)} %param.6) | copy-start | bytes 49156
  0.0 7.2 %copy-start.1 = (s32[4096]{0:T(1024)S(1)}, s32[4096]{0:T(1024)}, u32[]{:S(2)}) copy-start(s32[4096]{0:T(1024)} %param.5) | copy-start | bytes 49156
  1.5 5.8 %collective-permute-start = (bf16[1024,64]{0,1:T(8,128)(2,1)S(1)}, bf16[1024,64]{0,1:T(8,128)(2,1)S(1)}, u32[]{:S(2)}, u32[]{:S(2)}) collective-permute-start(bf16[1024,64]{0,1:T(8,128)(2,1)S(1)} %get-tuple-element.16), channel_id=1, source_target_pairs={{0,1},{1,0},{2,3},{3,2},{4,5},{5,4},{6,7},{7,6},{8,9},{9,8},{10,11... | collective-permute-start | bytes 393224 | tf_op jit(solution)/shard_map/ppermute | solution.py:28
  4.1 3.3 %collective-permute-start.1 = (bf16[1024,64]{0,1:T(8,128)(2,1)S(1)}, bf16[1024,64]{0,1:T(8,128)(2,1)S(1)}, u32[]{:S(2)}, u32[]{:S(2)}) collective-permute-start(bf16[1024,64]{0,1:T(8,128)(2,1)S(1)} %get-tuple-element.17), channel_id=1, source_target_pairs={{1,2},{3,4},{5,6},{2,1},{4,3},{6,5},{9,10},{11,12},{13,14},{10,9},... | collective-permute-start | bytes 393224 | tf_op jit(solution)/shard_map/ppermute | solution.py:29
  8.6 9.6 %collective-permute-start.3 = (bf16[256,256]{0,1:T(8,128)(2,1)S(1)}, bf16[256,256]{0,1:T(8,128)(2,1)S(1)}, u32[]{:S(2)}, u32[]{:S(2)}) collective-permute-start(bf16[256,256]{0,1:T(8,128)(2,1)S(1)} %broadcast_select_fusion.2), channel_id=1, source_target_pairs={{8,16},{24,32},{40,48},{56,64},{72,80},{88,96},{104,112},{120,128}... | collective-permute-start | bytes 393224 | tf_op jit(solution)/shard_map/ppermute | solution.py:29
  14.5 3.7 %collective-permute-start.2 = (bf16[256,256]{0,1:T(8,128)(2,1)S(1)}, bf16[256,256]{0,1:T(8,128)(2,1)S(1)}, u32[]{:S(2)}, u32[]{:S(2)}) collective-permute-start(bf16[256,256]{0,1:T(8,128)(2,1)S(1)} %get-tuple-element.9), channel_id=1, source_target_pairs={{0,8},{8,0},{16,24},{24,16},{32,40},{40,32},{48,56},{56,48},{64,72... | collective-permute-start | bytes 393224 | tf_op jit(solution)/shard_map/ppermute | solution.py:28
  23.1 0.9 %copy-start.2 = (s32[4096]{0:T(1024)S(1)}, s32[4096]{0:T(1024)}, u32[]{:S(2)}) copy-start(s32[4096]{0:T(1024)} %param.7) | copy-start | bytes 49156

commit v17 on v11

--- a/solution.py
+++ b/solution.py
@@ -45,11 +45,8 @@
 def exact_dot(values, selector):
     high = lax.reduce_precision(values, exponent_bits=8, mantissa_bits=7)
     rest = values - high
-    mid = lax.reduce_precision(rest, exponent_bits=8, mantissa_bits=7)
-    low = rest - mid
     total = jnp.dot(high.astype(jnp.bfloat16), selector, preferred_element_type=jnp.float32)
-    total = total + jnp.dot(mid.astype(jnp.bfloat16), selector, preferred_element_type=jnp.float32)
-    return total + jnp.dot(low.astype(jnp.bfloat16), selector, preferred_element_type=jnp.float32)
+    return total + jnp.dot(rest.astype(jnp.bfloat16), selector, preferred_element_type=jnp.float32)
 
 
 def select_rows(table, index):

time: 62.7 us -> 62.4 us (level)
  no operation moved by 1% of the time
where the time goes in v17:
time: 62.4 us; the launch traced here: 62.2 us
  blocking collectives  35.9 us (58%)
  matrix products  10.8 us (17%)
  starting transfers between devices  9.34 us (15%)
  other arithmetic  4.44 us (7%)
  local copies, waits for them, and re-layouts  1.38 us (2%)
    all_to_all x1, blocking collectives, per_device(): lax.all_to_all(local_stack.astype(jnp.bfloat16), 'seg', split_axis=0, con...  21.2 us
    all_to_all x1, blocking collectives, per_device(): lax.all_to_all(partial_lags, 'band', split_axis=1, concat_axis=0, tiled=T...  14.7 us
    dot_general x2, matrix products, select_rows(): return jnp.dot(chosen, table, preferred_element_type=jnp.float32)  8.3 us
    ppermute x2, starting transfers between devices, extended(): lax.ppermute(jnp.where(odd, last, first).astype(wire_type), axis, outer)  6.53 us
    another operation x2, other arithmetic  3.37 us
    ppermute x2, starting transfers between devices, extended(): lax.ppermute(jnp.where(odd, first, last).astype(wire_type), axis, inner)  2.82 us
    dot_general x1, matrix products, per_device(): lax.dot_general(members, cross_both, (((0,), (0,)), ((), ())), preferred_...  1.42 us
  transfers between devices with their start and end apart: 4, of which 0 were waited for; matrix products, arithmetic and copies ran while one was open for 10% of the time, Pallas kernels for 0%

profile of v17, /device:TPU:1, one launch (start us, length us, event | category | flops | bytes accessed | tf_op | source)
XLA Modules:
  0.0 62.2 jit_solution(6241991930881724331)
XLA Ops:
  0.0 0.0 copy-start
  0.0 0.0 copy-start.1
  0.0 1.1 %fusion.53 = (bf16[1,1024,128]{2,1,0:T(8,128)(2,1)S(1)}, bf16[1,1024,128]{2,1,0:T(8,128)(2,1)S(1)}) fusion(bf16[2,1024,128]{2,1,0:T(8,128)(2,1)} %param.4), kind=kLoop, calls=%fused_computation.80 | loop fusion | bytes 1048576 | tf_op jit(solution)/shard_map/slice | solution.py:76
  1.1 0.1 copy.7
  1.2 0.1 copy.8
  1.4 0.1 fusion.32
  1.5 2.5 %collective-permute-start = (bf16[1024,64]{0,1:T(8,128)(2,1)S(1)}, bf16[1024,64]{0,1:T(8,128)(2,1)S(1)}, u32[]{:S(2)}, u32[]{:S(2)}) collective-permute-start(bf16[1024,64]{0,1:T(8,128)(2,1)S(1)} %get-tuple-element.16), channel_id=1, source_target_pairs={{0,1},{1,0},{2,3},{3,2},{4,5},{5,4},{6,7},{7,6},{8,9},{9,8},{10,11... | collective-permute-start | bytes 393224 | tf_op jit(solution)/shard_map/ppermute | solution.py:28
  4.1 0.7 %collective-permute-start.1 = (bf16[1024,64]{0,1:T(8,128)(2,1)S(1)}, bf16[1024,64]{0,1:T(8,128)(2,1)S(1)}, u32[]{:S(2)}, u32[]{:S(2)}) collective-permute-start(bf16[1024,64]{0,1:T(8,128)(2,1)S(1)} %get-tuple-element.17), channel_id=1, source_target_pairs={{1,2},{3,4},{5,6},{2,1},{4,3},{6,5},{9,10},{11,12},{13,14},{10,9},... | collective-permute-start | bytes 393224 | tf_op jit(solution)/shard_map/ppermute | solution.py:29
  4.8 2.5 %multiply_convert_fusion.1 = (bf16[128,1024]{0,1:T(8,128)(2,1)S(1)}, bf16[128,1024]{0,1:T(8,128)(2,1)S(1)}) fusion(s32[1024]{0:T(1024)S(1)} %iota_add_fusion, s32[128]{0:T(128)S(1)} %iota_add_fusion.2), kind=kLoop, calls=%fused_computation.53 | loop fusion | flops 2490368 | bytes 528896 | tf_op jit(solution)/shard_map/convert.6
  7.3 0.0 copy-done
  7.3 0.0 copy-done.1
  7.4 0.1 pad_maximum_fusion.1
  7.4 0.0 collective-permute-done
  7.4 0.0 collective-permute-done.1
  7.5 0.1 pad_maximum_fusion
  7.6 0.3 fusion.39
  7.9 0.4 fusion.33
  8.3 5.9 %collective-permute-start.3 = (bf16[256,256]{0,1:T(8,128)(2,1)S(1)}, bf16[256,256]{0,1:T(8,128)(2,1)S(1)}, u32[]{:S(2)}, u32[]{:S(2)}) collective-permute-start(bf16[256,256]{0,1:T(8,128)(2,1)S(1)} %broadcast_select_fusion.2), channel_id=1, source_target_pairs={{8,16},{24,32},{40,48},{56,64},{72,80},{88,96},{104,112},{120,128}... | collective-permute-start | bytes 393224 | tf_op jit(solution)/shard_map/ppermute | solution.py:29
  14.2 0.3 collective-permute-start.2
  14.5 3.4 %fusion.1 = f32[4096,256]{0,1:T(8,128)S(1)} fusion(s32[4096]{0:T(1024)S(1)} %get-tuple-element.27, bf16[1024,128]{0,1:T(8,128)(2,1)S(1)} %get-tuple-element.15, bf16[1024,128]{0,1:T(8,128)(2,1)S(1)} %get-tuple-element.14), kind=kOutput, calls=%fused_computation.3 | convolution fusion | flops 2152726528 | bytes 4734976 | tf_op jit(solution)/shard_map/dot_general | solution.py:56
  17.9 0.0 collective-permute-done.3
  17.9 0.0 collective-permute-done.2
  17.9 4.9 %fusion = f32[4096,256]{0,1:T(8,128)S(1)} fusion(s32[4096]{0:T(1024)S(1)} %get-tuple-element.26, bf16[256,256]{0,1:T(8,128)(2,1)S(1)} %get-tuple-element.21, bf16[1024,128]{0,1:T(8,128)(2,1)S(1)} %get-tuple-element.15, bf16[1024,128]{0,1:T(8,128)(2,1)S(1)} %get-tuple-element.14, bf16[256,256]{0,1:T(8,128)(2,1)S(1)} %get-tuple-element.20), kind=kOutput, calls=%fused_computation.1 | convolution fusion | flops 3230662656 | bytes 4997120 | tf_op jit(solution)/shard_map/dot_general | solution.py:56
  22.8 0.0 copy-start.2
  22.8 0.9 %add_convert_fusion = (bf16[4096,128]{0,1:T(8,128)(2,1)S(1)}, bf16[4096,128]{0,1:T(8,128)(2,1)S(1)}) fusion(f32[4096,256]{0,1:T(8,128)S(1)} %fusion, f32[4096,256]{0,1:T(8,128)S(1)} %fusion.1), kind=kLoop, calls=%fused_computation.13 | loop fusion | flops 4194304 | bytes 10485760 | tf_op jit(solution)/shard_map/convert.2
  23.7 0.0 copy-done.2
  23.7 1.4 %fusion.19 = bf16[32,8,256]{2,1,0:T(8,128)(2,1)S(1)} fusion(bf16[4096,128]{0,1:T(8,128)(2,1)S(1)} %get-tuple-element.13, bf16[4096,128]{0,1:T(8,128)(2,1)S(1)} %get-tuple-element.12, s32[4096]{0:T(1024)S(1)} %copy-done.2), kind=kOutput, calls=%fused_computation.22 | convolution fusion | flops 543227904 | bytes 2244608 | tf_op jit(solution)/shard_map/dot_general | solution.py:101
  25.1 21.2 %all_to_all.19 = bf16[32,8,256]{2,1,0:T(8,128)(2,1)S(1)} all-to-all(bf16[32,8,256]{2,1,0:T(8,128)(2,1)S(1)} %fusion.19), channel_id=1, replica_groups=mesh['seg'=32,'band'=8] {'seg'}, dimensions={0} | all-to-all | bytes 262144 | tf_op jit(solution)/shard_map/all_to_all | solution.py:104
  46.4 0.5 fusion.48
  46.9 14.7 %all_to_all.20 = f32[8,8,128]{2,0,1:T(8,128)S(1)} all-to-all(f32[8,8,128]{2,0,1:T(8,128)S(1)} %fusion.48), channel_id=1, replica_groups=mesh['seg'=32,'band'=8] {'band'}, dimensions={1} | all-to-all | bytes 65536 | tf_op jit(solution)/shard_map/all_to_all | solution.py:113
  61.6 0.6 reduce_sum.19
  (10 shorter events, 0.2 us)
Async XLA Ops:
  0.0 7.3 %copy-start = (s32[4096]{0:T(1024)S(1)}, s32[4096]{0:T(1024)}, u32[]{:S(2)}) copy-start(s32[4096]{0:T(1024)} %param.6) | copy-start | bytes 49156
  0.0 7.3 %copy-start.1 = (s32[4096]{0:T(1024)S(1)}, s32[4096]{0:T(1024)}, u32[]{:S(2)}) copy-start(s32[4096]{0:T(1024)} %param.5) | copy-start | bytes 49156
  1.5 5.9 %collective-permute-start = (bf16[1024,64]{0,1:T(8,128)(2,1)S(1)}, bf16[1024,64]{0,1:T(8,128)(2,1)S(1)}, u32[]{:S(2)}, u32[]{:S(2)}) collective-permute-start(bf16[1024,64]{0,1:T(8,128)(2,1)S(1)} %get-tuple-element.16), channel_id=1, source_target_pairs={{0,1},{1,0},{2,3},{3,2},{4,5},{5,4},{6,7},{7,6},{8,9},{9,8},{10,11... | collective-permute-start | bytes 393224 | tf_op jit(solution)/shard_map/ppermute | solution.py:28
  4.1 3.4 %collective-permute-start.1 = (bf16[1024,64]{0,1:T(8,128)(2,1)S(1)}, bf16[1024,64]{0,1:T(8,128)(2,1)S(1)}, u32[]{:S(2)}, u32[]{:S(2)}) collective-permute-start(bf16[1024,64]{0,1:T(8,128)(2,1)S(1)} %get-tuple-element.17), channel_id=1, source_target_pairs={{1,2},{3,4},{5,6},{2,1},{4,3},{6,5},{9,10},{11,12},{13,14},{10,9},... | collective-permute-start | bytes 393224 | tf_op jit(solution)/shard_map/ppermute | solution.py:29
  8.3 9.5 %collective-permute-start.3 = (bf16[256,256]{0,1:T(8,128)(2,1)S(1)}, bf16[256,256]{0,1:T(8,128)(2,1)S(1)}, u32[]{:S(2)}, u32[]{:S(2)}) collective-permute-start(bf16[256,256]{0,1:T(8,128)(2,1)S(1)} %broadcast_select_fusion.2), channel_id=1, source_target_pairs={{8,16},{24,32},{40,48},{56,64},{72,80},{88,96},{104,112},{120,128}... | collective-permute-start | bytes 393224 | tf_op jit(solution)/shard_map/ppermute | solution.py:29
  14.2 3.7 %collective-permute-start.2 = (bf16[256,256]{0,1:T(8,128)(2,1)S(1)}, bf16[256,256]{0,1:T(8,128)(2,1)S(1)}, u32[]{:S(2)}, u32[]{:S(2)}) collective-permute-start(bf16[256,256]{0,1:T(8,128)(2,1)S(1)} %get-tuple-element.9), channel_id=1, source_target_pairs={{0,8},{8,0},{16,24},{24,16},{32,40},{40,32},{48,56},{56,48},{64,72... | collective-permute-start | bytes 393224 | tf_op jit(solution)/shard_map/ppermute | solution.py:28
  22.8 0.9 %copy-start.2 = (s32[4096]{0:T(1024)S(1)}, s32[4096]{0:T(1024)}, u32[]{:S(2)}) copy-start(s32[4096]{0:T(1024)} %param.7) | copy-start | bytes 49156
